TPU v7x, 512 devices: a whole 4x8x8 slice. The times are simulated.
512 devices in a mesh: sub: 32 (over x_lo, z, core), grp: 16 (over x_hi, y).
Axes of the slice: x: 4 (x_hi: 2, x_lo: 2; x = x_hi * 2 + x_lo), y: 8, z: 8, core: 2. Of those that a mesh axis runs over, the one named last changes fastest.
Arguments:
- deflation: bfloat16 [32, 3, 512, 128, 128], P(None, None, 'sub', 'grp'), may hold values from -10 to 10, as said below
- stiffness: bfloat16 [4, 512, 128, 128], P(None, 'sub', 'grp'), may hold values from 0.02 to 40, as said below
- depths: int32 [512], P(('sub', 'grp')), may hold values from 1 to 128, 49152 in all
Outputs:
- coarse_rows: float32 [32, 16, 32, 96], P('sub')
Inputs may be any that keep to these rules, and one draw needn't show every extreme that they name: `deflation`: entries of order one. `stiffness`: positive coefficients. `depths`: the deepest subdomain has all 128 cells live.
All inputs are finite; a program needn't handle non-finite values. No bound on the sum of `depths` on one device may be relied on, other than what follows from the above.
Results may differ from a plain program's by a relative error of at most 0.0003.
Values may be sent and summed in bfloat16 or wider, within the bound.
No kernel may reach another device: no remote copies, remote signals or barrier semaphores. Data moves between devices by JAX's collectives and lax.ppermute only.
A program may use at most 128 MiB of HBM per device.

v0:
```python
import jax
import jax.numpy as jnp
from jax import lax
from jax.sharding import PartitionSpec as P


def from_behind(x, axis, by):
    length = lax.axis_size(axis)
    pairs = [(i, i + by) for i in range(length) if 0 <= i + by < length]
    return lax.ppermute(x, axis, pairs)


def gram_of(left_side, right_side):
    count = left_side.shape[0]
    return jnp.dot(
        left_side.reshape(count, -1),
        right_side.reshape(count, -1).T,
        preferred_element_type=jnp.float32,
    )


def weighted(weight, values):
    return (weight.astype(jnp.float32) * values.astype(jnp.float32)).astype(jnp.bfloat16)


def differences(values, dim_index):
    widened = values.astype(jnp.float32)
    length = widened.shape[dim_index]
    following = jnp.concatenate(
        [
            lax.slice_in_dim(widened, 1, length, axis=dim_index),
            jnp.zeros_like(lax.slice_in_dim(widened, 0, 1, axis=dim_index)),
        ],
        axis=dim_index,
    )
    return (widened - following).astype(jnp.bfloat16)


def local_terms(live_field, coefficients):
    accumulated = gram_of(live_field, weighted(coefficients[0], live_field))
    for entry in range(3):
        stepped = differences(live_field, entry + 2)
        accumulated = accumulated + gram_of(stepped, weighted(coefficients[entry + 1], stepped))
    return accumulated


def shards(deflation, stiffness, depths):
    cell_count = deflation.shape[2] * deflation.shape[3] * deflation.shape[4]
    normalizer = 1.0 / (24.0 * cell_count)
    live_mask = (lax.iota(jnp.int32, deflation.shape[4]) < depths[0]).astype(jnp.bfloat16)
    live_field = deflation * live_mask
    diagonal_block = local_terms(live_field, stiffness)
    top_x = live_field[:, :, -1]
    bottom_x = live_field[:, :, 0]
    weight_top_x = stiffness[1, -1]
    next_x = from_behind(bottom_x, "sub", -1)
    coupling_x = -gram_of(weighted(weight_top_x, top_x), next_x)
    face_term = gram_of(next_x, weighted(weight_top_x, next_x))
    lower_x = from_behind(face_term, "sub", 1)
    diagonal_block = diagonal_block + lower_x
    bottom_y = live_field[:, :, :, 0]
    weight_top_y = stiffness[2, :, -1]
    next_y = from_behind(bottom_y, "grp", -1)
    weight_low_y = from_behind(weight_top_y, "grp", 1)
    diagonal_block = diagonal_block + gram_of(bottom_y, weighted(weight_low_y, bottom_y))
    coupling_y = -gram_of(weighted(weight_top_y, live_field[:, :, :, -1]), next_y)
    row_block = normalizer * jnp.concatenate([diagonal_block, coupling_x, coupling_y], axis=1)
    return lax.all_gather(row_block[None, None], "grp", axis=1, tiled=True)


def solution(mesh):
    in_specs = (P(None, None, "sub", "grp", None), P(None, "sub", "grp", None), P(("sub", "grp")))
    out_specs = P("sub", None, None, None)
    return jax.shard_map(shards, mesh=mesh, in_specs=in_specs, out_specs=out_specs, check_vma=False)
```

profile of v0, /device:TPU:2, one launch (start us, length us, event | category | flops | bytes accessed | tf_op | source)
XLA Modules:
  0.0 105.4 jit_solution(15280825005196992566)
XLA Ops:
  0.0 0.8 slice.49
  0.8 3.5 %collective-permute-start.2 = (bf16[16,128]{1,0:T(8,128)(2,1)S(1)}, bf16[16,128]{1,0:T(8,128)(2,1)S(1)}, u32[]{:S(2)}, u32[]{:S(2)}) collective-permute-start(bf16[16,128]{1,0:T(8,128)(2,1)S(1)} %get-tuple-element.14), channel_id=1, source_target_pairs={{0,1},{1,2},{2,3},{3,4},{4,5},{5,6},{6,7},{7,8},{8,9},{9,10},{10,1... | collective-permute-start | bytes 12296 | tf_op jit(solution)/shard_map/ppermute | solution.py:10
  4.3 0.8 bitcast_convert_fusion
  5.8 6.2 %multiply_convert_fusion.3 = (bf16[32,3,16,8,128]{4,0,3,1,2:T(8,128)(2,1)S(1)}, bf16[32,3,16,8,128]{4,0,3,1,2:T(8,128)(2,1)S(1)}) fusion(f32[16,8,128]{2,1,0:T(8,128)S(1)} %get-tuple-element.22, bf16[128]{0:T(256)(128)(2,1)S(1)} %compare_convert_fusion, bf16[32,3,16,8,128]{4,3,2,1,0:T(8,128)(2,1)} %param.3), kind=kLoop, calls=%fused_computation.6 | loop fusion | flops 6291456 | bytes 9502976 | tf_op jit(solution)/shard_map/convert_element_type | solution.py:23
  12.0 10.1 %collective-permute-start = (bf16[32,3,8,128]{3,0,2,1:T(8,128)(2,1)S(1)}, bf16[32,3,8,128]{3,0,2,1:T(8,128)(2,1)S(1)}, u32[]{:S(2)}, u32[]{:S(2)}) collective-permute-start(bf16[32,3,8,128]{3,0,2,1:T(8,128)(2,1)S(1)} %slice_bitcast_fusion.4), channel_id=1, source_target_pairs={{16,0},{32,16},{48,32},{64,48},{80,64},{96,80},{112,96},{128,112},... | collective-permute-start | bytes 589832 | tf_op jit(solution)/shard_map/ppermute | solution.py:10
  22.1 1.5 %collective-permute-start.3 = (bf16[32,3,16,128]{3,0,1,2:T(8,128)(2,1)S(1)}, bf16[32,3,16,128]{3,0,1,2:T(8,128)(2,1)S(1)}, u32[]{:S(2)}, u32[]{:S(2)}) collective-permute-start(bf16[32,3,16,128]{3,0,1,2:T(8,128)(2,1)S(1)} %slice_bitcast_fusion.1), channel_id=1, source_target_pairs={{1,0},{2,1},{3,2},{4,3},{5,4},{6,5},{7,6},{8,7},{9,8},{10,9},{11,1... | collective-permute-start | bytes 1179656 | tf_op jit(solution)/shard_map/ppermute | solution.py:10
  23.6 3.2 %slice.53 = f32[32,3,16,7,128]{4,0,3,1,2:T(8,128)} slice(bf16[32,3,16,8,128]{4,0,3,1,2:T(8,128)(2,1)S(1)} %get-tuple-element.12), slice={[0:32], [0:3], [0:16], [1:8], [0:128]} | slice | bytes 11010048 | tf_op jit(solution)/shard_map/slice | solution.py:31
  26.8 3.4 %slice.52 = f32[32,3,15,8,128]{4,0,3,1,2:T(8,128)} slice(bf16[32,3,16,8,128]{4,0,3,1,2:T(8,128)(2,1)S(1)} %get-tuple-element.12), slice={[0:32], [0:3], [1:16], [0:8], [0:128]} | slice | bytes 11796480 | tf_op jit(solution)/shard_map/slice | solution.py:31
  30.1 1.0 slice.54
  31.2 0.9 fusion.12
  32.1 12.0 %multiply_convert_fusion = (bf16[32,3,16,8,128]{4,0,3,1,2:T(8,128)(2,1)}, bf16[32,3,16,8,128]{4,0,3,1,2:T(8,128)(2,1)}, bf16[32,3,16,8,128]{4,0,3,1,2:T(8,128)(2...) fusion(f32[16,8,128]{2,1,0:T(8,128)S(1)} %get-tuple-element.19,, ...), kind=kLoop, calls=%fused_computation | loop fusion | flops 25165824 | bytes 39862272 | tf_op jit(solution)/shard_map/convert_element_type | solution.py:23
  44.1 0.0 copy-start.2
  44.1 0.0 copy-start.3
  44.1 3.9 %fusion.46 = f32[32,32]{1,0:T(8,128)S(1)} fusion(f32[32,32]{1,0:T(8,128)S(1)} %fusion.12, bf16[32,3,16,8,128]{4,0,3,1,2:T(8,128)(2,1)} %get-tuple-element.15, bf16[32,3,16,8,128]{4,0,3,1,2:T(8,128)(2,1)} %get-tuple-element.16), kind=kOutput, calls=%fused_computation.34 | convolution fusion | flops 100664320 | bytes 6299648 | tf_op jit(solution)/shard_map/dot_general | solution.py:15
  48.1 0.0 copy-done.2
  48.1 0.7 copy-done.3
  48.8 0.0 copy-start
  48.8 0.0 copy-start.1
  48.8 1.0 fusion.41
  49.8 0.9 copy-done
  50.7 1.0 copy-done.1
  51.7 1.0 fusion.36
  52.6 0.7 bitcast_convert_fusion.4
  53.3 0.0 collective-permute-done.2
  53.3 0.0 collective-permute-done
  53.3 0.2 convolution_bitcast_fusion.3
  53.5 1.9 %collective-permute-start.1 = (f32[32,32]{1,0:T(8,128)S(1)}, f32[32,32]{1,0:T(8,128)S(1)}, u32[]{:S(2)}, u32[]{:S(2)}) collective-permute-start(f32[32,32]{1,0:T(8,128)S(1)} %convolution_bitcast_fusion.3), channel_id=1, source_target_pairs={{0,16},{16,32},{32,48},{48,64},{64,80},{80,96},{96,112},{112,128},... | collective-permute-start | bytes 12296 | tf_op jit(solution)/shard_map/ppermute | solution.py:10
  55.5 0.2 fusion.35
  55.6 5.1 %collective-permute-done.1 = f32[32,32]{1,0:T(8,128)S(1)} collective-permute-done((f32[32,32]{1,0:T(8,128)S(1)}, f32[32,32]{1,0:T(8,128)S(1)}, u32[]{:S(2)}, u32[]{:S(2)}) %collective-permute-start.1) | collective-permute-done | bytes 4128 | tf_op jit(solution)/shard_map/ppermute | solution.py:10
  60.7 0.2 add_bitcast_fusion
  60.9 0.0 collective-permute-done.3
  61.0 0.2 fusion.33
  61.2 0.1 fusion.61
  61.3 43.4 %all_gather.3 = f32[1,16,32,96]{3,2,0,1:T(8,128)S(1)} all-gather(f32[1,1,32,96]{3,2,0,1:T(8,128)S(1)} %fusion.61), channel_id=1, replica_groups=mesh['sub'=32,'grp'=16] {'grp'}, dimensions={1}, use_global_device_ids=true | all-gather | bytes 208896 | tf_op jit(solution)/shard_map/all_gather | solution.py:68
  104.7 0.7 copy.118
  (5 shorter events, 0.1 us)
Async XLA Ops:
  0.8 52.5 %collective-permute-start.2 = (bf16[16,128]{1,0:T(8,128)(2,1)S(1)}, bf16[16,128]{1,0:T(8,128)(2,1)S(1)}, u32[]{:S(2)}, u32[]{:S(2)}) collective-permute-start(bf16[16,128]{1,0:T(8,128)(2,1)S(1)} %get-tuple-element.14), channel_id=1, source_target_pairs={{0,1},{1,2},{2,3},{3,4},{4,5},{5,6},{6,7},{7,8},{8,9},{9,10},{10,1... | collective-permute-start | bytes 12296 | tf_op jit(solution)/shard_map/ppermute | solution.py:10
  12.0 41.4 %collective-permute-start = (bf16[32,3,8,128]{3,0,2,1:T(8,128)(2,1)S(1)}, bf16[32,3,8,128]{3,0,2,1:T(8,128)(2,1)S(1)}, u32[]{:S(2)}, u32[]{:S(2)}) collective-permute-start(bf16[32,3,8,128]{3,0,2,1:T(8,128)(2,1)S(1)} %slice_bitcast_fusion.4), channel_id=1, source_target_pairs={{16,0},{32,16},{48,32},{64,48},{80,64},{96,80},{112,96},{128,112},... | collective-permute-start | bytes 589832 | tf_op jit(solution)/shard_map/ppermute | solution.py:10
  22.1 38.9 %collective-permute-start.3 = (bf16[32,3,16,128]{3,0,1,2:T(8,128)(2,1)S(1)}, bf16[32,3,16,128]{3,0,1,2:T(8,128)(2,1)S(1)}, u32[]{:S(2)}, u32[]{:S(2)}) collective-permute-start(bf16[32,3,16,128]{3,0,1,2:T(8,128)(2,1)S(1)} %slice_bitcast_fusion.1), channel_id=1, source_target_pairs={{1,0},{2,1},{3,2},{4,3},{5,4},{6,5},{7,6},{8,7},{9,8},{10,9},{11,1... | collective-permute-start | bytes 1179656 | tf_op jit(solution)/shard_map/ppermute | solution.py:10
  44.1 4.0 %copy-start.2 = (bf16[32,3,16,8,128]{4,0,3,1,2:T(8,128)(2,1)S(1)}, bf16[32,3,16,8,128]{4,0,3,1,2:T(8,128)(2,1)}, u32[]{:S(2)}) copy-start(bf16[32,3,16,8,128]{4,0,3,1,2:T(8,128)(2,1)} %get-tuple-element.17) | copy-start | bytes 9437188
  44.1 4.7 %copy-start.3 = (bf16[32,3,16,8,128]{4,0,3,1,2:T(8,128)(2,1)S(1)}, bf16[32,3,16,8,128]{4,0,3,1,2:T(8,128)(2,1)}, u32[]{:S(2)}) copy-start(bf16[32,3,16,8,128]{4,0,3,1,2:T(8,128)(2,1)} %get-tuple-element.18) | copy-start | bytes 9437188
  48.8 1.9 %copy-start = (bf16[32,3,16,8,128]{4,0,3,1,2:T(8,128)(2,1)S(1)}, bf16[32,3,16,8,128]{4,0,3,1,2:T(8,128)(2,1)}, u32[]{:S(2)}) copy-start(bf16[32,3,16,8,128]{4,0,3,1,2:T(8,128)(2,1)} %get-tuple-element.5) | copy-start | bytes 9437188
  48.8 2.8 %copy-start.1 = (bf16[32,3,16,8,128]{4,0,3,1,2:T(8,128)(2,1)S(1)}, bf16[32,3,16,8,128]{4,0,3,1,2:T(8,128)(2,1)}, u32[]{:S(2)}) copy-start(bf16[32,3,16,8,128]{4,0,3,1,2:T(8,128)(2,1)} %get-tuple-element.6) | copy-start | bytes 9437188
  53.5 7.2 %collective-permute-start.1 = (f32[32,32]{1,0:T(8,128)S(1)}, f32[32,32]{1,0:T(8,128)S(1)}, u32[]{:S(2)}, u32[]{:S(2)}) collective-permute-start(f32[32,32]{1,0:T(8,128)S(1)} %convolution_bitcast_fusion.3), channel_id=1, source_target_pairs={{0,16},{16,32},{32,48},{48,64},{64,80},{80,96},{96,112},{112,128},... | collective-permute-start | bytes 12296 | tf_op jit(solution)/shard_map/ppermute | solution.py:10
where the time goes:
time: 106 us; the launch traced here: 105 us
  blocking collectives  43.4 us (41%)
  other arithmetic  19.8 us (19%)
  starting transfers between devices  17 us (16%)
  local copies, waits for them, and re-layouts  11.7 us (11%)
  matrix products  7.63 us (7%)
  waiting for transfers between devices  5.07 us (5%)
    all_gather x1, blocking collectives, shards(): return lax.all_gather(row_block[None, None], 'grp', axis=1, tiled=True)  43.4 us
    convert_element_type x2, other arithmetic, weighted(): (weight.astype(jnp.float32) * values.astype(jnp.float32)).astype(jnp.bflo...  18.2 us
    ppermute x4, starting transfers between devices, from_behind(): return lax.ppermute(x, axis, pairs)  17 us
    dot_general x8, matrix products, gram_of(): jnp.dot(left_side.reshape(count, -1), right_side.reshape(count, -1).T, pr...  7.63 us
    slice x3, local copies, waits for them, and re-layouts, differences(): lax.slice_in_dim(widened, 1, length, axis=dim_index)  7.61 us
    ppermute x4, waiting for transfers between devices, from_behind(): return lax.ppermute(x, axis, pairs)  5.07 us
    unnamed x9, local copies, waits for them, and re-layouts  3.33 us
  transfers between devices with their start and end apart: 4, of which 1 were waited for; matrix products, arithmetic and copies ran while one was open for 33% of the time, Pallas kernels for 0%

commit v1 on v0

--- a/solution.py
+++ b/solution.py
@@ -1,6 +1,8 @@
 import jax
 import jax.numpy as jnp
 from jax import lax
+from jax.experimental import pallas as pl
+from jax.experimental.pallas import tpu as pltpu
 from jax.sharding import PartitionSpec as P
 
 
@@ -23,25 +25,65 @@
     return (weight.astype(jnp.float32) * values.astype(jnp.float32)).astype(jnp.bfloat16)
 
 
-def differences(values, dim_index):
-    widened = values.astype(jnp.float32)
-    length = widened.shape[dim_index]
-    following = jnp.concatenate(
-        [
-            lax.slice_in_dim(widened, 1, length, axis=dim_index),
-            jnp.zeros_like(lax.slice_in_dim(widened, 0, 1, axis=dim_index)),
-        ],
-        axis=dim_index,
-    )
-    return (widened - following).astype(jnp.bfloat16)
+def local_kernel(live_ref, coeff_ref, out_ref):
+    comps, rows, count, width = live_ref.shape
+    lane = lax.broadcasted_iota(jnp.int32, (count, width), 1)
+    last_z = (lane & 127) == 127
+    zero_slab = jnp.zeros((count, 128), jnp.float32)
+
+    def weight(entry, row):
+        return coeff_ref[entry, pl.ds(row, 1), :]
+
+    def body(row, acc):
+        has_next = row < rows - 1
+        following_row = jnp.minimum(row + 1, rows - 1)
+        w_mass = weight(0, row)
+        w_x = weight(1, row)
+        w_y = weight(2, row)
+        w_z = weight(3, row)
+        lefts, rights = [], []
+        for comp in range(comps):
+            live_b = live_ref[comp, row]
+            live = live_b.astype(jnp.float32)
+            next_x = live_ref[comp, following_row].astype(jnp.float32)
+            next_x = jnp.where(has_next, next_x, 0.0)
+            next_y = jnp.concatenate([live[:, 128:], zero_slab], axis=1)
+            next_z = jnp.where(last_z, 0.0, pltpu.roll(live, width - 1, 1))
+            step_x = (live - next_x).astype(jnp.bfloat16)
+            step_y = (live - next_y).astype(jnp.bfloat16)
+            step_z = (live - next_z).astype(jnp.bfloat16)
+            lefts += [live_b, step_x, step_y, step_z]
+            rights += [
+                (w_mass * live).astype(jnp.bfloat16),
+                (w_x * step_x.astype(jnp.float32)).astype(jnp.bfloat16),
+                (w_y * step_y.astype(jnp.float32)).astype(jnp.bfloat16),
+                (w_z * step_z.astype(jnp.float32)).astype(jnp.bfloat16),
+            ]
+        left = jnp.concatenate(lefts, axis=1)
+        right = jnp.concatenate(rights, axis=1)
+        return acc + lax.dot_general(
+            left, right, (((1,), (1,)), ((), ())), preferred_element_type=jnp.float32
+        )
+
+    acc = lax.fori_loop(0, rows, body, jnp.zeros((count, count), jnp.float32))
+    out_ref[...] = acc
 
 
 def local_terms(live_field, coefficients):
-    accumulated = gram_of(live_field, weighted(coefficients[0], live_field))
-    for entry in range(3):
-        stepped = differences(live_field, entry + 2)
-        accumulated = accumulated + gram_of(stepped, weighted(coefficients[entry + 1], stepped))
-    return accumulated
+    count, comps, rows, cols, depth = live_field.shape
+    live_t = jnp.transpose(live_field, (1, 2, 0, 3, 4)).reshape(comps, rows, count, cols * depth)
+    coeff_t = coefficients.astype(jnp.float32).reshape(4, rows, cols * depth)
+    return pl.pallas_call(
+        local_kernel,
+        out_shape=jax.ShapeDtypeStruct((count, count), jnp.float32),
+        in_specs=[pl.BlockSpec(memory_space=pltpu.VMEM)] * 2,
+        out_specs=pl.BlockSpec(memory_space=pltpu.VMEM),
+        cost_estimate=pl.CostEstimate(
+            flops=2 * 4 * count * count * live_field.size // count,
+            bytes_accessed=live_t.size * 2 + coeff_t.size * 4,
+            transcendentals=0,
+        ),
+    )(live_t, coeff_t)
 
 
 def shards(deflation, stiffness, depths):

time: 106 us -> 101 us (0.953)
  other arithmetic: 19.8 us -> 6.29 us
  Pallas kernels: 0 us -> 9.92 us
  matrix products: 7.63 us -> 5 us
  local copies, waits for them, and re-layouts: 11.7 us -> 12.9 us
    convert_element_type x2 -> x0, other arithmetic: 18.2 us -> none  [weighted(): (weight.astype(jnp.float32) * values.astype(jnp.float32)).astype(jnp.bflo...]
    pallas_call x0 -> x1, Pallas kernels: none -> 9.92 us  [local_terms(): pl.pallas_call(local_kernel, out_shape=jax.ShapeDtypeStruct((count, count...]
    slice x3 -> x0, local copies, waits for them, and re-layouts: 7.61 us -> none  [differences(): lax.slice_in_dim(widened, 1, length, axis=dim_index)]
    reshape x0 -> x2, local copies, waits for them, and re-layouts: none -> 7.45 us  [the longest x1 5.78 us: local_terms(): jnp.transpose(live_field, (1, 2, 0, 3, 4))]
    mul x0 -> x1, other arithmetic: none -> 3.77 us  [shards(): live_field = deflation * live_mask]
    transpose x0 -> x1, local copies, waits for them, and re-layouts: none -> 3.22 us  [local_terms(): jnp.transpose(live_field, (1, 2, 0, 3, 4))]
    dot_general x8 -> x4, matrix products: 7.63 us -> 5 us  [gram_of(): jnp.dot(left_side.reshape(count, -1), right_side.reshape(count, -1).T, pr...]
    unnamed x9 -> x5, local copies, waits for them, and re-layouts: 3.33 us -> 0.71 us
  transfers between devices with their start and end apart: 4 -> 4, of which waited for: 1 -> 1; matrix products, arithmetic and copies ran while one was open for 33% -> 18% of each run, Pallas kernels for 0% -> 10%
where the time goes in v1:
time: 101 us; the launch traced here: 100 us
  blocking collectives  44.1 us (44%)
  starting transfers between devices  17.1 us (17%)
  local copies, waits for them, and re-layouts  12.9 us (13%)
  Pallas kernels  9.92 us (10%)
  other arithmetic  6.29 us (6%)
  matrix products  5 us (5%)
  waiting for transfers between devices  4.05 us (4%)
    all_gather x1, blocking collectives, shards(): return lax.all_gather(row_block[None, None], 'grp', axis=1, tiled=True)  44.1 us
    ppermute x4, starting transfers between devices, from_behind(): return lax.ppermute(x, axis, pairs)  17.1 us
    pallas_call x1, Pallas kernels, local_terms(): pl.pallas_call(local_kernel, out_shape=jax.ShapeDtypeStruct((count, count...  9.92 us
    reshape x1, local copies, waits for them, and re-layouts, local_terms(): jnp.transpose(live_field, (1, 2, 0, 3, 4))  5.78 us
    dot_general x4, matrix products, gram_of(): jnp.dot(left_side.reshape(count, -1), right_side.reshape(count, -1).T, pr...  5 us
    ppermute x4, waiting for transfers between devices, from_behind(): return lax.ppermute(x, axis, pairs)  4.05 us
    mul x1, other arithmetic, shards(): live_field = deflation * live_mask  3.77 us
    transpose x1, local copies, waits for them, and re-layouts, local_terms(): jnp.transpose(live_field, (1, 2, 0, 3, 4))  3.22 us
  transfers between devices with their start and end apart: 4, of which 1 were waited for; matrix products, arithmetic and copies ran while one was open for 18% of the time, Pallas kernels for 10%

profile of v1, /device:TPU:2, one launch (start us, length us, event | category | flops | bytes accessed | tf_op | source)
XLA Modules:
  0.0 100.1 jit_solution(17478492289048416034)
XLA Ops:
  0.7 0.0 copy-start
  0.7 3.8 %copy_multiply_fusion = bf16[32,3,16,8,128]{4,0,3,1,2:T(8,128)(2,1)S(1)} fusion(bf16[32,3,16,8,128]{4,3,2,1,0:T(8,128)(2,1)} %param.3, bf16[128]{0:T(256)(128)(2,1)S(1)} %compare_convert_fusion), kind=kLoop, calls=%fused_computation | loop fusion | flops 1572864 | bytes 6291712 | tf_op jit(solution)/shard_map/mul | solution.py:93
  4.4 0.0 copy-start.1
  4.5 0.8 slice_bitcast_fusion.4
  5.2 10.3 %collective-permute-start = (bf16[32,3,8,128]{3,0,2,1:T(8,128)(2,1)}, bf16[32,3,8,128]{3,0,2,1:T(8,128)(2,1)}, u32[]{:S(2)}, u32[]{:S(2)}) collective-permute-start(bf16[32,3,8,128]{3,0,2,1:T(8,128)(2,1)} %slice_bitcast_fusion.4), channel_id=1, source_target_pairs={{16,0},{32,16},{48,32},{64,48},{80,64},{96,80},{112,96},{128,112},... | collective-permute-start | bytes 589832 | tf_op jit(solution)/shard_map/ppermute | solution.py:12
  15.6 0.8 slice.21
  16.4 3.5 %collective-permute-start.2 = (bf16[16,128]{1,0:T(8,128)(2,1)S(1)}, bf16[16,128]{1,0:T(8,128)(2,1)S(1)}, u32[]{:S(2)}, u32[]{:S(2)}) collective-permute-start(bf16[16,128]{1,0:T(8,128)(2,1)S(1)} %get-tuple-element.6), channel_id=1, source_target_pairs={{0,1},{1,2},{2,3},{3,4},{4,5},{5,6},{6,7},{7,8},{8,9},{9,10},{10,1... | collective-permute-start | bytes 12296 | tf_op jit(solution)/shard_map/ppermute | solution.py:12
  19.9 0.0 copy-done.1
  19.9 1.3 %collective-permute-start.3 = (bf16[32,3,16,128]{3,0,1,2:T(8,128)(2,1)S(1)}, bf16[32,3,16,128]{3,0,1,2:T(8,128)(2,1)}, u32[]{:S(2)}, u32[]{:S(2)}) collective-permute-start(bf16[32,3,16,128]{3,0,1,2:T(8,128)(2,1)S(1)} %slice_bitcast_fusion.1), channel_id=1, source_target_pairs={{1,0},{2,1},{3,2},{4,3},{5,4},{6,5},{7,6},{8,7},{9,8},{10,9},{11,1... | collective-permute-start | bytes 1179656 | tf_op jit(solution)/shard_map/ppermute | solution.py:12
  21.2 0.0 copy-done
  21.2 1.7 %fusion.22 = bf16[3,16,32,8,128]{4,2,3,0,1:T(8,128)(2,1)S(1)} fusion(bf16[128]{0:T(256)(128)(2,1)S(1)} %compare_convert_fusion, bf16[32,3,16,8,128]{4,3,2,1,0:T(8,128)(2,1)S(1)} %copy-done), kind=kLoop, calls=%fused_computation.33 | loop fusion | flops 1572864 | bytes 6291712 | tf_op jit(solution)/shard_map/transpose | solution.py:74
  22.9 1.7 %reshape.92.coeff_ref = f32[4,16,1024]{2,1,0:T(8,128)} reshape(bf16[4,16,8,128]{3,2,1,0:T(8,128)(2,1)} %param.4) | data formatting | bytes 393216 | tf_op jit(solution)/shard_map/reshape | solution.py:75
  24.6 3.2 %copy.18 = bf16[3,16,32,8,128]{4,3,2,1,0:T(8,128)(2,1)} copy(bf16[3,16,32,8,128]{4,2,3,0,1:T(8,128)(2,1)S(1)} %fusion.22) | data formatting | bytes 6291456 | tf_op jit(solution)/shard_map/transpose | solution.py:74
  27.8 5.8 %reshape.86.live_ref = bf16[3,16,32,1024]{3,2,1,0:T(8,128)(2,1)} reshape(bf16[3,16,32,8,128]{4,3,2,1,0:T(8,128)(2,1)} %copy.18) | data formatting | bytes 6291456 | tf_op jit(solution)/shard_map/reshape | solution.py:74
  33.6 0.7 bitcast_convert_fusion
  34.3 9.9 %shard_map.37 = f32[32,32]{1,0:T(8,128)} custom-call(bf16[3,16,32,1024]{3,2,1,0:T(8,128)(2,1)} %reshape.86.live_ref, f32[4,16,1024]{2,1,0:T(8,128)} %reshape.92.coeff_ref), custom_call_target="tpu_custom_call" | custom-call | flops 402653184 | bytes 3407872 | tf_op jit(solution)/shard_map/pallas_call | solution.py:76
  44.2 0.0 collective-permute-done.2
  44.2 0.0 collective-permute-done
  44.2 1.2 %convolution_bitcast_fusion.3 = f32[32,32]{1,0:T(8,128)S(1)} fusion(bf16[32,3,8,128]{3,0,2,1:T(8,128)(2,1)} %collective-permute-done, f32[8,128]{1,0:T(8,128)S(1)} %bitcast_convert_fusion), kind=kOutput, calls=%fused_computation.8 | convolution fusion | flops 6586368 | bytes 204800 | tf_op jit(solution)/shard_map/dot_general | solution.py:17
  45.4 1.9 %collective-permute-start.1 = (f32[32,32]{1,0:T(8,128)S(1)}, f32[32,32]{1,0:T(8,128)S(1)}, u32[]{:S(2)}, u32[]{:S(2)}) collective-permute-start(f32[32,32]{1,0:T(8,128)S(1)} %convolution_bitcast_fusion.3), channel_id=1, source_target_pairs={{0,16},{16,32},{32,48},{48,64},{64,80},{80,96},{96,112},{112,128},... | collective-permute-start | bytes 12296 | tf_op jit(solution)/shard_map/ppermute | solution.py:12
  47.3 1.2 %fusion.3 = f32[1,1,32,32]{3,2,1,0:T(8,128)S(1)} fusion(bf16[32,3,8,128]{3,0,2,1:T(8,128)(2,1)} %collective-permute-done, bf16[32,3,16,8,128]{4,0,3,1,2:T(8,128)(2,1)} %copy-done.1, f32[8,128]{1,0:T(8,128)S(1)} %bitcast_convert_fusion), kind=kOutput, calls=%fused_computation.7 | convolution fusion | flops 6587392 | bytes 401408 | tf_op jit(solution)/shard_map/dot_general | solution.py:17
  48.5 4.0 %collective-permute-done.1 = f32[32,32]{1,0:T(8,128)S(1)} collective-permute-done((f32[32,32]{1,0:T(8,128)S(1)}, f32[32,32]{1,0:T(8,128)S(1)}, u32[]{:S(2)}, u32[]{:S(2)}) %collective-permute-start.1) | collective-permute-done | bytes 4128 | tf_op jit(solution)/shard_map/ppermute | solution.py:12
  52.6 1.2 %add_bitcast_fusion = f32[1,1,32,32]{3,2,1,0:T(8,128)S(1)} fusion(f32[32,32]{1,0:T(8,128)} %shard_map.37, f32[32,32]{1,0:T(8,128)S(1)} %collective-permute-done.1, bf16[32,3,16,128]{3,0,1,2:T(8,128)(2,1)S(1)} %slice_bitcast_fusion.1, f32[16,128]{1,0:T(8,128)S(1)} %convert_element_type.58, bf16[32,3,16,8,128]{4,0,3,1,2:T(8,128)(2,1)} %copy-done.1), kind=kOutput, calls=%fused_computation.28 | convolution fusion | flops 13174784 | bytes 819200 | tf_op jit(solution)/shard_map/dot_general | solution.py:17
  53.8 0.0 collective-permute-done.3
  53.9 1.4 %fusion.1 = f32[1,1,32,32]{3,2,1,0:T(8,128)S(1)} fusion(bf16[32,3,16,128]{3,0,1,2:T(8,128)(2,1)} %collective-permute-done.3, bf16[32,3,16,8,128]{4,0,3,1,2:T(8,128)(2,1)} %copy-done.1, f32[16,128]{1,0:T(8,128)S(1)} %get-tuple-element.5), kind=kOutput, calls=%fused_computation.3 | convolution fusion | flops 13173760 | bytes 798720 | tf_op jit(solution)/shard_map/dot_general | solution.py:17
  55.2 0.1 fusion.14
  55.3 44.1 %all_gather.3 = f32[1,16,32,96]{3,2,0,1:T(8,128)S(1)} all-gather(f32[1,1,32,96]{3,2,0,1:T(8,128)S(1)} %fusion.14), channel_id=1, replica_groups=mesh['sub'=32,'grp'=16] {'grp'}, dimensions={1}, use_global_device_ids=true | all-gather | bytes 208896 | tf_op jit(solution)/shard_map/all_gather | solution.py:110
  99.4 0.7 copy.50
  (4 shorter events, 0.0 us)
Async XLA Ops:
  0.7 20.5 %copy-start = (bf16[32,3,16,8,128]{4,3,2,1,0:T(8,128)(2,1)S(1)}, bf16[32,3,16,8,128]{4,3,2,1,0:T(8,128)(2,1)}, u32[]{:S(2)}) copy-start(bf16[32,3,16,8,128]{4,3,2,1,0:T(8,128)(2,1)} %param.3) | copy-start | bytes 9437188
  4.4 15.4 %copy-start.1 = (bf16[32,3,16,8,128]{4,0,3,1,2:T(8,128)(2,1)}, bf16[32,3,16,8,128]{4,0,3,1,2:T(8,128)(2,1)S(1)}, u32[]{:S(2)}) copy-start(bf16[32,3,16,8,128]{4,0,3,1,2:T(8,128)(2,1)S(1)} %copy_multiply_fusion) | copy-start | bytes 9437188
  5.2 39.0 %collective-permute-start = (bf16[32,3,8,128]{3,0,2,1:T(8,128)(2,1)}, bf16[32,3,8,128]{3,0,2,1:T(8,128)(2,1)}, u32[]{:S(2)}, u32[]{:S(2)}) collective-permute-start(bf16[32,3,8,128]{3,0,2,1:T(8,128)(2,1)} %slice_bitcast_fusion.4), channel_id=1, source_target_pairs={{16,0},{32,16},{48,32},{64,48},{80,64},{96,80},{112,96},{128,112},... | collective-permute-start | bytes 589832 | tf_op jit(solution)/shard_map/ppermute | solution.py:12
  16.4 27.9 %collective-permute-start.2 = (bf16[16,128]{1,0:T(8,128)(2,1)S(1)}, bf16[16,128]{1,0:T(8,128)(2,1)S(1)}, u32[]{:S(2)}, u32[]{:S(2)}) collective-permute-start(bf16[16,128]{1,0:T(8,128)(2,1)S(1)} %get-tuple-element.6), channel_id=1, source_target_pairs={{0,1},{1,2},{2,3},{3,4},{4,5},{5,6},{6,7},{7,8},{8,9},{9,10},{10,1... | collective-permute-start | bytes 12296 | tf_op jit(solution)/shard_map/ppermute | solution.py:12
  19.9 34.0 %collective-permute-start.3 = (bf16[32,3,16,128]{3,0,1,2:T(8,128)(2,1)S(1)}, bf16[32,3,16,128]{3,0,1,2:T(8,128)(2,1)}, u32[]{:S(2)}, u32[]{:S(2)}) collective-permute-start(bf16[32,3,16,128]{3,0,1,2:T(8,128)(2,1)S(1)} %slice_bitcast_fusion.1), channel_id=1, source_target_pairs={{1,0},{2,1},{3,2},{4,3},{5,4},{6,5},{7,6},{8,7},{9,8},{10,9},{11,1... | collective-permute-start | bytes 1179656 | tf_op jit(solution)/shard_map/ppermute | solution.py:12
  45.4 7.2 %collective-permute-start.1 = (f32[32,32]{1,0:T(8,128)S(1)}, f32[32,32]{1,0:T(8,128)S(1)}, u32[]{:S(2)}, u32[]{:S(2)}) collective-permute-start(f32[32,32]{1,0:T(8,128)S(1)} %convolution_bitcast_fusion.3), channel_id=1, source_target_pairs={{0,16},{16,32},{32,48},{48,64},{64,80},{80,96},{96,112},{112,128},... | collective-permute-start | bytes 12296 | tf_op jit(solution)/shard_map/ppermute | solution.py:12

commit v2 on v1

--- a/solution.py
+++ b/solution.py
@@ -107,7 +107,9 @@
     diagonal_block = diagonal_block + gram_of(bottom_y, weighted(weight_low_y, bottom_y))
     coupling_y = -gram_of(weighted(weight_top_y, live_field[:, :, :, -1]), next_y)
     row_block = normalizer * jnp.concatenate([diagonal_block, coupling_x, coupling_y], axis=1)
-    return lax.all_gather(row_block[None, None], "grp", axis=1, tiled=True)
+    groups = lax.axis_size("grp")
+    copies = jnp.broadcast_to(row_block[None, None], (1, groups) + row_block.shape)
+    return lax.all_to_all(copies, "grp", 1, 1, tiled=True)
 
 
 def solution(mesh):

time: 101 us -> 78.6 us (0.78)
  the two profiles are of different devices: /device:TPU:2 before, /device:TPU:10 now
where the time goes in v2:
time: 78.6 us; the launch traced here: 78.1 us
  blocking collectives  21 us (27%)
  starting transfers between devices  18.1 us (23%)
  local copies, waits for them, and re-layouts  13 us (17%)
  Pallas kernels  9.92 us (13%)
  other arithmetic  6.29 us (8%)
  matrix products  5 us (6%)
  waiting for transfers between devices  4.05 us (5%)
    all_to_all x1, blocking collectives, shards(): return lax.all_to_all(copies, 'grp', 1, 1, tiled=True)  21 us
    ppermute x4, starting transfers between devices, from_behind(): return lax.ppermute(x, axis, pairs)  18.1 us
    pallas_call x1, Pallas kernels, local_terms(): pl.pallas_call(local_kernel, out_shape=jax.ShapeDtypeStruct((count, count...  9.92 us
    reshape x1, local copies, waits for them, and re-layouts, local_terms(): jnp.transpose(live_field, (1, 2, 0, 3, 4))  5.78 us
    dot_general x4, matrix products, gram_of(): jnp.dot(left_side.reshape(count, -1), right_side.reshape(count, -1).T, pr...  5 us
    ppermute x4, waiting for transfers between devices, from_behind(): return lax.ppermute(x, axis, pairs)  4.05 us
    mul x1, other arithmetic, shards(): live_field = deflation * live_mask  3.77 us
    transpose x1, local copies, waits for them, and re-layouts, local_terms(): jnp.transpose(live_field, (1, 2, 0, 3, 4))  3.22 us
  transfers between devices with their start and end apart: 4, of which 1 were waited for; matrix products, arithmetic and copies ran while one was open for 22% of the time, Pallas kernels for 13%

profile of v2, /device:TPU:10, one launch (start us, length us, event | category | flops | bytes accessed | tf_op | source)
XLA Modules:
  0.0 78.1 jit_solution(6310284894187526853)
XLA Ops:
  0.7 0.0 copy-start
  0.7 3.8 %copy_multiply_fusion = bf16[32,3,16,8,128]{4,0,3,1,2:T(8,128)(2,1)S(1)} fusion(bf16[32,3,16,8,128]{4,3,2,1,0:T(8,128)(2,1)} %param.3, bf16[128]{0:T(256)(128)(2,1)S(1)} %compare_convert_fusion), kind=kLoop, calls=%fused_computation | loop fusion | flops 1572864 | bytes 6291712 | tf_op jit(solution)/shard_map/mul | solution.py:93
  4.4 0.0 copy-start.1
  4.5 0.8 slice_bitcast_fusion.4
  5.2 10.3 %collective-permute-start = (bf16[32,3,8,128]{3,0,2,1:T(8,128)(2,1)}, bf16[32,3,8,128]{3,0,2,1:T(8,128)(2,1)}, u32[]{:S(2)}, u32[]{:S(2)}) collective-permute-start(bf16[32,3,8,128]{3,0,2,1:T(8,128)(2,1)} %slice_bitcast_fusion.4), channel_id=1, source_target_pairs={{16,0},{32,16},{48,32},{64,48},{80,64},{96,80},{112,96},{128,112},... | collective-permute-start | bytes 589832 | tf_op jit(solution)/shard_map/ppermute | solution.py:12
  15.6 0.8 slice.21
  16.4 3.5 %collective-permute-start.2 = (bf16[16,128]{1,0:T(8,128)(2,1)S(1)}, bf16[16,128]{1,0:T(8,128)(2,1)S(1)}, u32[]{:S(2)}, u32[]{:S(2)}) collective-permute-start(bf16[16,128]{1,0:T(8,128)(2,1)S(1)} %get-tuple-element.6), channel_id=1, source_target_pairs={{0,1},{1,2},{2,3},{3,4},{4,5},{5,6},{6,7},{7,8},{8,9},{9,10},{10,1... | collective-permute-start | bytes 12296 | tf_op jit(solution)/shard_map/ppermute | solution.py:12
  19.9 0.0 copy-done.1
  19.9 2.4 %collective-permute-start.3 = (bf16[32,3,16,128]{3,0,1,2:T(8,128)(2,1)S(1)}, bf16[32,3,16,128]{3,0,1,2:T(8,128)(2,1)}, u32[]{:S(2)}, u32[]{:S(2)}) collective-permute-start(bf16[32,3,16,128]{3,0,1,2:T(8,128)(2,1)S(1)} %slice_bitcast_fusion.1), channel_id=1, source_target_pairs={{1,0},{2,1},{3,2},{4,3},{5,4},{6,5},{7,6},{8,7},{9,8},{10,9},{11,1... | collective-permute-start | bytes 1179656 | tf_op jit(solution)/shard_map/ppermute | solution.py:12
  22.3 0.0 copy-done
  22.3 1.7 %fusion.15 = bf16[3,16,32,8,128]{4,2,3,0,1:T(8,128)(2,1)S(1)} fusion(bf16[128]{0:T(256)(128)(2,1)S(1)} %compare_convert_fusion, bf16[32,3,16,8,128]{4,3,2,1,0:T(8,128)(2,1)S(1)} %copy-done), kind=kLoop, calls=%fused_computation.30 | loop fusion | flops 1572864 | bytes 6291712 | tf_op jit(solution)/shard_map/transpose | solution.py:74
  24.0 1.7 %reshape.74.coeff_ref = f32[4,16,1024]{2,1,0:T(8,128)} reshape(bf16[4,16,8,128]{3,2,1,0:T(8,128)(2,1)} %param.4) | data formatting | bytes 393216 | tf_op jit(solution)/shard_map/reshape | solution.py:75
  25.7 3.2 %copy.18 = bf16[3,16,32,8,128]{4,3,2,1,0:T(8,128)(2,1)} copy(bf16[3,16,32,8,128]{4,2,3,0,1:T(8,128)(2,1)S(1)} %fusion.15) | data formatting | bytes 6291456 | tf_op jit(solution)/shard_map/transpose | solution.py:74
  28.9 5.8 %reshape.68.live_ref = bf16[3,16,32,1024]{3,2,1,0:T(8,128)(2,1)} reshape(bf16[3,16,32,8,128]{4,3,2,1,0:T(8,128)(2,1)} %copy.18) | data formatting | bytes 6291456 | tf_op jit(solution)/shard_map/reshape | solution.py:74
  34.7 0.7 bitcast_convert_fusion
  35.4 9.9 %shard_map.37 = f32[32,32]{1,0:T(8,128)} custom-call(bf16[3,16,32,1024]{3,2,1,0:T(8,128)(2,1)} %reshape.68.live_ref, f32[4,16,1024]{2,1,0:T(8,128)} %reshape.74.coeff_ref), custom_call_target="tpu_custom_call" | custom-call | flops 402653184 | bytes 3407872 | tf_op jit(solution)/shard_map/pallas_call | solution.py:76
  45.3 0.0 collective-permute-done.2
  45.3 0.0 collective-permute-done
  45.3 1.2 %convolution_bitcast_fusion.3 = f32[32,32]{1,0:T(8,128)S(1)} fusion(bf16[32,3,8,128]{3,0,2,1:T(8,128)(2,1)} %collective-permute-done, f32[8,128]{1,0:T(8,128)S(1)} %bitcast_convert_fusion), kind=kOutput, calls=%fused_computation.6 | convolution fusion | flops 6586368 | bytes 204800 | tf_op jit(solution)/shard_map/dot_general | solution.py:17
  46.5 1.9 %collective-permute-start.1 = (f32[32,32]{1,0:T(8,128)S(1)}, f32[32,32]{1,0:T(8,128)S(1)}, u32[]{:S(2)}, u32[]{:S(2)}) collective-permute-start(f32[32,32]{1,0:T(8,128)S(1)} %convolution_bitcast_fusion.3), channel_id=1, source_target_pairs={{0,16},{16,32},{32,48},{48,64},{64,80},{80,96},{96,112},{112,128},... | collective-permute-start | bytes 12296 | tf_op jit(solution)/shard_map/ppermute | solution.py:12
  48.4 1.2 %fusion.1 = f32[32,32]{1,0:T(8,128)S(1)} fusion(bf16[32,3,8,128]{3,0,2,1:T(8,128)(2,1)} %collective-permute-done, bf16[32,3,16,8,128]{4,0,3,1,2:T(8,128)(2,1)} %copy-done.1, f32[8,128]{1,0:T(8,128)S(1)} %bitcast_convert_fusion), kind=kOutput, calls=%fused_computation.5 | convolution fusion | flops 6587392 | bytes 401408 | tf_op jit(solution)/shard_map/dot_general | solution.py:17
  49.6 4.0 %collective-permute-done.1 = f32[32,32]{1,0:T(8,128)S(1)} collective-permute-done((f32[32,32]{1,0:T(8,128)S(1)}, f32[32,32]{1,0:T(8,128)S(1)}, u32[]{:S(2)}, u32[]{:S(2)}) %collective-permute-start.1) | collective-permute-done | bytes 4128 | tf_op jit(solution)/shard_map/ppermute | solution.py:12
  53.7 1.2 %add_add_fusion = f32[32,32]{1,0:T(8,128)S(1)} fusion(f32[32,32]{1,0:T(8,128)} %shard_map.37, f32[32,32]{1,0:T(8,128)S(1)} %collective-permute-done.1, bf16[32,3,16,128]{3,0,1,2:T(8,128)(2,1)S(1)} %slice_bitcast_fusion.1, f32[16,128]{1,0:T(8,128)S(1)} %convert_element_type.58, bf16[32,3,16,8,128]{4,0,3,1,2:T(8,128)(2,1)} %copy-done.1), kind=kOutput, calls=%fused_computation.25 | convolution fusion | flops 13174784 | bytes 819200 | tf_op jit(solution)/shard_map/dot_general | solution.py:17
  54.9 0.0 collective-permute-done.3
  54.9 1.4 %fusion = f32[32,32]{1,0:T(8,128)S(1)} fusion(bf16[32,3,16,128]{3,0,1,2:T(8,128)(2,1)} %collective-permute-done.3, bf16[32,3,16,8,128]{4,0,3,1,2:T(8,128)(2,1)} %copy-done.1, f32[16,128]{1,0:T(8,128)S(1)} %get-tuple-element.5), kind=kOutput, calls=%fused_computation.2 | convolution fusion | flops 13173760 | bytes 798720 | tf_op jit(solution)/shard_map/dot_general | solution.py:17
  56.3 0.1 maximum_multiply_fusion
  56.4 21.0 %all_to_all.5 = f32[1,16,32,96]{3,2,0,1:T(8,128)S(1)} all-to-all(f32[1,16,32,96]{3,2,0,1:T(8,128)S(1)} %broadcast_in_dim.2), channel_id=1, replica_groups=mesh['sub'=32,'grp'=16] {'grp'}, dimensions={1} | all-to-all | bytes 393216 | tf_op jit(solution)/shard_map/all_to_all | solution.py:112
  77.4 0.7 copy.49
  (5 shorter events, 0.1 us)
Async XLA Ops:
  0.7 21.6 %copy-start = (bf16[32,3,16,8,128]{4,3,2,1,0:T(8,128)(2,1)S(1)}, bf16[32,3,16,8,128]{4,3,2,1,0:T(8,128)(2,1)}, u32[]{:S(2)}) copy-start(bf16[32,3,16,8,128]{4,3,2,1,0:T(8,128)(2,1)} %param.3) | copy-start | bytes 9437188
  4.4 15.4 %copy-start.1 = (bf16[32,3,16,8,128]{4,0,3,1,2:T(8,128)(2,1)}, bf16[32,3,16,8,128]{4,0,3,1,2:T(8,128)(2,1)S(1)}, u32[]{:S(2)}) copy-start(bf16[32,3,16,8,128]{4,0,3,1,2:T(8,128)(2,1)S(1)} %copy_multiply_fusion) | copy-start | bytes 9437188
  5.2 40.1 %collective-permute-start = (bf16[32,3,8,128]{3,0,2,1:T(8,128)(2,1)}, bf16[32,3,8,128]{3,0,2,1:T(8,128)(2,1)}, u32[]{:S(2)}, u32[]{:S(2)}) collective-permute-start(bf16[32,3,8,128]{3,0,2,1:T(8,128)(2,1)} %slice_bitcast_fusion.4), channel_id=1, source_target_pairs={{16,0},{32,16},{48,32},{64,48},{80,64},{96,80},{112,96},{128,112},... | collective-permute-start | bytes 589832 | tf_op jit(solution)/shard_map/ppermute | solution.py:12
  16.4 28.9 %collective-permute-start.2 = (bf16[16,128]{1,0:T(8,128)(2,1)S(1)}, bf16[16,128]{1,0:T(8,128)(2,1)S(1)}, u32[]{:S(2)}, u32[]{:S(2)}) collective-permute-start(bf16[16,128]{1,0:T(8,128)(2,1)S(1)} %get-tuple-element.6), channel_id=1, source_target_pairs={{0,1},{1,2},{2,3},{3,4},{4,5},{5,6},{6,7},{7,8},{8,9},{9,10},{10,1... | collective-permute-start | bytes 12296 | tf_op jit(solution)/shard_map/ppermute | solution.py:12
  19.9 35.0 %collective-permute-start.3 = (bf16[32,3,16,128]{3,0,1,2:T(8,128)(2,1)S(1)}, bf16[32,3,16,128]{3,0,1,2:T(8,128)(2,1)}, u32[]{:S(2)}, u32[]{:S(2)}) collective-permute-start(bf16[32,3,16,128]{3,0,1,2:T(8,128)(2,1)S(1)} %slice_bitcast_fusion.1), channel_id=1, source_target_pairs={{1,0},{2,1},{3,2},{4,3},{5,4},{6,5},{7,6},{8,7},{9,8},{10,9},{11,1... | collective-permute-start | bytes 1179656 | tf_op jit(solution)/shard_map/ppermute | solution.py:12
  46.5 7.2 %collective-permute-start.1 = (f32[32,32]{1,0:T(8,128)S(1)}, f32[32,32]{1,0:T(8,128)S(1)}, u32[]{:S(2)}, u32[]{:S(2)}) collective-permute-start(f32[32,32]{1,0:T(8,128)S(1)} %convolution_bitcast_fusion.3), channel_id=1, source_target_pairs={{0,16},{16,32},{32,48},{48,64},{64,80},{80,96},{96,112},{112,128},... | collective-permute-start | bytes 12296 | tf_op jit(solution)/shard_map/ppermute | solution.py:12

commit v3 on v0

--- a/solution.py
+++ b/solution.py
@@ -1,6 +1,8 @@
 import jax
 import jax.numpy as jnp
 from jax import lax
+from jax.experimental import pallas as pl
+from jax.experimental.pallas import tpu as pltpu
 from jax.sharding import PartitionSpec as P
 
 
@@ -23,25 +25,63 @@
     return (weight.astype(jnp.float32) * values.astype(jnp.float32)).astype(jnp.bfloat16)
 
 
-def differences(values, dim_index):
-    widened = values.astype(jnp.float32)
-    length = widened.shape[dim_index]
-    following = jnp.concatenate(
-        [
-            lax.slice_in_dim(widened, 1, length, axis=dim_index),
-            jnp.zeros_like(lax.slice_in_dim(widened, 0, 1, axis=dim_index)),
-        ],
-        axis=dim_index,
-    )
-    return (widened - following).astype(jnp.bfloat16)
+def local_kernel(depth_ref, defl_ref, coeff_ref, out_ref):
+    count, comps, rows, cols, depth = defl_ref.shape
+    lane = lax.broadcasted_iota(jnp.int32, (count, depth), 1)
+    live_mask = (lane < depth_ref[0]).astype(jnp.bfloat16)
+    last_z = lane == depth - 1
+
+    def slab(comp, row, col):
+        return (defl_ref[:, comp, row, col, :] * live_mask).astype(jnp.float32)
+
+    def weight(entry, row, col):
+        return coeff_ref[entry, row, pl.ds(col, 1), :].astype(jnp.float32)
+
+    def body(row, acc):
+        has_next = row < rows - 1
+        following_row = jnp.minimum(row + 1, rows - 1)
+        for comp in range(comps):
+            lefts, rights = [], []
+            lives = [slab(comp, row, col) for col in range(cols)]
+            for col in range(cols):
+                live = lives[col]
+                next_x = jnp.where(has_next, slab(comp, following_row, col), 0.0)
+                next_y = lives[col + 1] if col + 1 < cols else jnp.zeros_like(live)
+                next_z = jnp.where(last_z, 0.0, pltpu.roll(live, depth - 1, 1))
+                step_x = (live - next_x).astype(jnp.bfloat16)
+                step_y = (live - next_y).astype(jnp.bfloat16)
+                step_z = (live - next_z).astype(jnp.bfloat16)
+                lefts += [live.astype(jnp.bfloat16), step_x, step_y, step_z]
+                rights += [
+                    (weight(0, row, col) * live).astype(jnp.bfloat16),
+                    (weight(1, row, col) * step_x.astype(jnp.float32)).astype(jnp.bfloat16),
+                    (weight(2, row, col) * step_y.astype(jnp.float32)).astype(jnp.bfloat16),
+                    (weight(3, row, col) * step_z.astype(jnp.float32)).astype(jnp.bfloat16),
+                ]
+            left = jnp.concatenate(lefts, axis=1)
+            right = jnp.concatenate(rights, axis=1)
+            acc = acc + lax.dot_general(
+                left, right, (((1,), (1,)), ((), ())), preferred_element_type=jnp.float32
+            )
+        return acc
+
+    acc = lax.fori_loop(0, rows, body, jnp.zeros((count, count), jnp.float32))
+    out_ref[...] = acc
 
 
-def local_terms(live_field, coefficients):
-    accumulated = gram_of(live_field, weighted(coefficients[0], live_field))
-    for entry in range(3):
-        stepped = differences(live_field, entry + 2)
-        accumulated = accumulated + gram_of(stepped, weighted(coefficients[entry + 1], stepped))
-    return accumulated
+def local_terms(deflation, coefficients, depths):
+    count = deflation.shape[0]
+    return pl.pallas_call(
+        local_kernel,
+        out_shape=jax.ShapeDtypeStruct((count, count), jnp.float32),
+        in_specs=[pl.BlockSpec(memory_space=pltpu.SMEM)] + [pl.BlockSpec(memory_space=pltpu.VMEM)] * 2,
+        out_specs=pl.BlockSpec(memory_space=pltpu.VMEM),
+        cost_estimate=pl.CostEstimate(
+            flops=2 * 4 * count * deflation.size,
+            bytes_accessed=deflation.size * 2 + coefficients.size * 2,
+            transcendentals=0,
+        ),
+    )(depths, deflation, coefficients)
 
 
 def shards(deflation, stiffness, depths):
@@ -49,7 +89,7 @@
     normalizer = 1.0 / (24.0 * cell_count)
     live_mask = (lax.iota(jnp.int32, deflation.shape[4]) < depths[0]).astype(jnp.bfloat16)
     live_field = deflation * live_mask
-    diagonal_block = local_terms(live_field, stiffness)
+    diagonal_block = local_terms(deflation, stiffness, depths)
     top_x = live_field[:, :, -1]
     bottom_x = live_field[:, :, 0]
     weight_top_x = stiffness[1, -1]
@@ -65,7 +105,9 @@
     diagonal_block = diagonal_block + gram_of(bottom_y, weighted(weight_low_y, bottom_y))
     coupling_y = -gram_of(weighted(weight_top_y, live_field[:, :, :, -1]), next_y)
     row_block = normalizer * jnp.concatenate([diagonal_block, coupling_x, coupling_y], axis=1)
-    return lax.all_gather(row_block[None, None], "grp", axis=1, tiled=True)
+    groups = lax.axis_size("grp")
+    copies = jnp.broadcast_to(row_block[None, None], (1, groups) + row_block.shape)
+    return lax.all_to_all(copies, "grp", 1, 1, tiled=True)
 
 
 def solution(mesh):

time: 106 us -> 74.4 us (0.70)
  the two profiles are of different devices: /device:TPU:2 before, /device:TPU:10 now
where the time goes in v3:
time: 74.4 us; the launch traced here: 73.9 us
  blocking collectives  19.8 us (27%)
  Pallas kernels  19.7 us (26%)
  starting transfers between devices  17.8 us (24%)
  other arithmetic  4.99 us (7%)
  matrix products  4.5 us (6%)
  waiting for transfers between devices  4.14 us (6%)
  local copies, waits for them, and re-layouts  2.23 us (3%)
    all_to_all x1, blocking collectives, shards(): return lax.all_to_all(copies, 'grp', 1, 1, tiled=True)  19.8 us
    pallas_call x1, Pallas kernels, local_terms(): pl.pallas_call(local_kernel, out_shape=jax.ShapeDtypeStruct((count, count...  19.7 us
    ppermute x4, starting transfers between devices, from_behind(): return lax.ppermute(x, axis, pairs)  17.8 us
    dot_general x4, matrix products, gram_of(): jnp.dot(left_side.reshape(count, -1), right_side.reshape(count, -1).T, pr...  4.5 us
    ppermute x4, waiting for transfers between devices, from_behind(): return lax.ppermute(x, axis, pairs)  4.14 us
    mul x1, other arithmetic, shards(): live_field = deflation * live_mask  3.62 us
  transfers between devices with their start and end apart: 4, of which 1 were waited for; matrix products, arithmetic and copies ran while one was open for 8% of the time, Pallas kernels for 27%

profile of v3, /device:TPU:10, one launch (start us, length us, event | category | flops | bytes accessed | tf_op | source)
XLA Modules:
  0.0 73.9 jit_solution(17473920973859210141)
XLA Ops:
  0.7 3.6 %copy_multiply_fusion = bf16[32,3,16,8,128]{4,0,3,1,2:T(8,128)(2,1)S(1)} fusion(bf16[32,3,16,8,128]{4,3,2,1,0:T(8,128)(2,1)} %defl_ref.1, bf16[128]{0:T(256)(128)(2,1)S(1)} %compare_convert_fusion), kind=kLoop, calls=%fused_computation | loop fusion | flops 1572864 | bytes 6291712 | tf_op jit(solution)/shard_map/mul | solution.py:91
  4.3 2.4 %collective-permute-start.3 = (bf16[32,3,16,128]{3,0,1,2:T(8,128)(2,1)S(1)}, bf16[32,3,16,128]{3,0,1,2:T(8,128)(2,1)}, u32[]{:S(2)}, u32[]{:S(2)}) collective-permute-start(bf16[32,3,16,128]{3,0,1,2:T(8,128)(2,1)S(1)} %slice_bitcast_fusion.1), channel_id=1, source_target_pairs={{1,0},{2,1},{3,2},{4,3},{5,4},{6,5},{7,6},{8,7},{9,8},{10,9},{11,1... | collective-permute-start | bytes 1179656 | tf_op jit(solution)/shard_map/ppermute | solution.py:12
  6.7 0.7 slice_bitcast_fusion.4
  7.4 10.1 %collective-permute-start = (bf16[32,3,8,128]{3,0,2,1:T(8,128)(2,1)}, bf16[32,3,8,128]{3,0,2,1:T(8,128)(2,1)}, u32[]{:S(2)}, u32[]{:S(2)}) collective-permute-start(bf16[32,3,8,128]{3,0,2,1:T(8,128)(2,1)} %slice_bitcast_fusion.4), channel_id=1, source_target_pairs={{16,0},{32,16},{48,32},{64,48},{80,64},{96,80},{112,96},{128,112},... | collective-permute-start | bytes 589832 | tf_op jit(solution)/shard_map/ppermute | solution.py:12
  17.5 0.8 %slice.21 = bf16[1,16,1,128]{3,2,1,0:T(2,128)(2,1)S(1)} slice(bf16[4,16,8,128]{3,2,1,0:T(8,128)(2,1)} %coeff_ref.1), slice={[2:3], [0:16], [7:8], [0:128]} | slice | bytes 8192 | tf_op jit(solution)/shard_map/slice | solution.py:102
  18.2 3.5 %collective-permute-start.2 = (bf16[16,128]{1,0:T(8,128)(2,1)S(1)}, bf16[16,128]{1,0:T(8,128)(2,1)S(1)}, u32[]{:S(2)}, u32[]{:S(2)}) collective-permute-start(bf16[16,128]{1,0:T(8,128)(2,1)S(1)} %get-tuple-element.6), channel_id=1, source_target_pairs={{0,1},{1,2},{2,3},{3,4},{4,5},{5,6},{6,7},{7,8},{8,9},{9,10},{10,1... | collective-permute-start | bytes 12296 | tf_op jit(solution)/shard_map/ppermute | solution.py:12
  21.7 1.3 %bitcast_convert_fusion = f32[8,128]{1,0:T(8,128)} fusion(bf16[4,16,8,128]{3,2,1,0:T(8,128)(2,1)} %coeff_ref.1), kind=kLoop, calls=%fused_computation.27 | loop fusion | flops 1024 | bytes 6144 | tf_op jit(solution)/shard_map/mul | solution.py:25
  23.0 19.7 %shard_map.37 = f32[32,32]{1,0:T(8,128)} custom-call(s32[1]{0:T(128)} %copy.43.depth_ref, bf16[32,3,16,8,128]{4,3,2,1,0:T(8,128)(2,1)} %defl_ref.1, bf16[4,16,8,128]{3,2,1,0:T(8,128)(2,1)} %coeff_ref.1), custom_call_target="tpu_custom_call" | custom-call | flops 402653184 | bytes 3276800 | tf_op jit(solution)/shard_map/pallas_call | solution.py:74
  42.7 0.0 collective-permute-done.2
  42.7 0.0 collective-permute-done
  42.7 1.2 %convolution_bitcast_fusion.3 = f32[32,32]{1,0:T(8,128)S(1)} fusion(bf16[32,3,8,128]{3,0,2,1:T(8,128)(2,1)} %collective-permute-done, f32[8,128]{1,0:T(8,128)} %bitcast_convert_fusion), kind=kOutput, calls=%fused_computation.6 | convolution fusion | flops 6586368 | bytes 204800 | tf_op jit(solution)/shard_map/dot_general | solution.py:17
  43.9 1.9 %collective-permute-start.1 = (f32[32,32]{1,0:T(8,128)S(1)}, f32[32,32]{1,0:T(8,128)S(1)}, u32[]{:S(2)}, u32[]{:S(2)}) collective-permute-start(f32[32,32]{1,0:T(8,128)S(1)} %convolution_bitcast_fusion.3), channel_id=1, source_target_pairs={{0,16},{16,32},{32,48},{48,64},{64,80},{80,96},{96,112},{112,128},... | collective-permute-start | bytes 12296 | tf_op jit(solution)/shard_map/ppermute | solution.py:12
  45.8 1.1 %fusion.1 = f32[32,32]{1,0:T(8,128)S(1)} fusion(bf16[32,3,8,128]{3,0,2,1:T(8,128)(2,1)} %collective-permute-done, bf16[32,3,16,8,128]{4,0,3,1,2:T(8,128)(2,1)S(1)} %copy_multiply_fusion, f32[8,128]{1,0:T(8,128)} %bitcast_convert_fusion), kind=kOutput, calls=%fused_computation.5 | convolution fusion | flops 6587392 | bytes 401408 | tf_op jit(solution)/shard_map/dot_general | solution.py:17
  47.0 4.1 %collective-permute-done.1 = f32[32,32]{1,0:T(8,128)S(1)} collective-permute-done((f32[32,32]{1,0:T(8,128)S(1)}, f32[32,32]{1,0:T(8,128)S(1)}, u32[]{:S(2)}, u32[]{:S(2)}) %collective-permute-start.1) | collective-permute-done | bytes 4128 | tf_op jit(solution)/shard_map/ppermute | solution.py:12
  51.1 1.0 %add_add_fusion = f32[32,32]{1,0:T(8,128)S(1)} fusion(f32[32,32]{1,0:T(8,128)} %shard_map.37, f32[32,32]{1,0:T(8,128)S(1)} %collective-permute-done.1, bf16[32,3,16,128]{3,0,1,2:T(8,128)(2,1)S(1)} %slice_bitcast_fusion.1, f32[16,128]{1,0:T(8,128)S(1)} %convert_element_type.57, bf16[32,3,16,8,128]{4,0,3,1,2:T(8,128)(2,1)S(1)} %copy_multiply_fusion), kind=kOutput, calls=%fused_computation.25 | convolution fusion | flops 13174784 | bytes 819200 | tf_op jit(solution)/shard_map/dot_general | solution.py:17
  52.1 0.0 collective-permute-done.3
  52.1 1.2 %fusion = f32[32,32]{1,0:T(8,128)S(1)} fusion(bf16[32,3,16,128]{3,0,1,2:T(8,128)(2,1)} %collective-permute-done.3, bf16[32,3,16,8,128]{4,0,3,1,2:T(8,128)(2,1)S(1)} %copy_multiply_fusion, f32[16,128]{1,0:T(8,128)S(1)} %get-tuple-element.5), kind=kOutput, calls=%fused_computation.2 | convolution fusion | flops 13173760 | bytes 798720 | tf_op jit(solution)/shard_map/dot_general | solution.py:17
  53.3 0.1 maximum_multiply_fusion
  53.4 19.8 %all_to_all.5 = f32[1,16,32,96]{3,2,0,1:T(8,128)S(1)} all-to-all(f32[1,16,32,96]{3,2,0,1:T(8,128)S(1)} %broadcast_in_dim.2), channel_id=1, replica_groups=mesh['sub'=32,'grp'=16] {'grp'}, dimensions={1} | all-to-all | bytes 393216 | tf_op jit(solution)/shard_map/all_to_all | solution.py:110
  73.2 0.7 copy.44
  (5 shorter events, 0.1 us)
Async XLA Ops:
  4.3 47.7 %collective-permute-start.3 = (bf16[32,3,16,128]{3,0,1,2:T(8,128)(2,1)S(1)}, bf16[32,3,16,128]{3,0,1,2:T(8,128)(2,1)}, u32[]{:S(2)}, u32[]{:S(2)}) collective-permute-start(bf16[32,3,16,128]{3,0,1,2:T(8,128)(2,1)S(1)} %slice_bitcast_fusion.1), channel_id=1, source_target_pairs={{1,0},{2,1},{3,2},{4,3},{5,4},{6,5},{7,6},{8,7},{9,8},{10,9},{11,1... | collective-permute-start | bytes 1179656 | tf_op jit(solution)/shard_map/ppermute | solution.py:12
  7.4 35.3 %collective-permute-start = (bf16[32,3,8,128]{3,0,2,1:T(8,128)(2,1)}, bf16[32,3,8,128]{3,0,2,1:T(8,128)(2,1)}, u32[]{:S(2)}, u32[]{:S(2)}) collective-permute-start(bf16[32,3,8,128]{3,0,2,1:T(8,128)(2,1)} %slice_bitcast_fusion.4), channel_id=1, source_target_pairs={{16,0},{32,16},{48,32},{64,48},{80,64},{96,80},{112,96},{128,112},... | collective-permute-start | bytes 589832 | tf_op jit(solution)/shard_map/ppermute | solution.py:12
  18.2 24.5 %collective-permute-start.2 = (bf16[16,128]{1,0:T(8,128)(2,1)S(1)}, bf16[16,128]{1,0:T(8,128)(2,1)S(1)}, u32[]{:S(2)}, u32[]{:S(2)}) collective-permute-start(bf16[16,128]{1,0:T(8,128)(2,1)S(1)} %get-tuple-element.6), channel_id=1, source_target_pairs={{0,1},{1,2},{2,3},{3,4},{4,5},{5,6},{6,7},{7,8},{8,9},{9,10},{10,1... | collective-permute-start | bytes 12296 | tf_op jit(solution)/shard_map/ppermute | solution.py:12
  43.9 7.2 %collective-permute-start.1 = (f32[32,32]{1,0:T(8,128)S(1)}, f32[32,32]{1,0:T(8,128)S(1)}, u32[]{:S(2)}, u32[]{:S(2)}) collective-permute-start(f32[32,32]{1,0:T(8,128)S(1)} %convolution_bitcast_fusion.3), channel_id=1, source_target_pairs={{0,16},{16,32},{32,48},{48,64},{64,80},{80,96},{96,112},{112,128},... | collective-permute-start | bytes 12296 | tf_op jit(solution)/shard_map/ppermute | solution.py:12

commit v4 on v3

--- a/solution.py
+++ b/solution.py
@@ -88,22 +88,21 @@
     cell_count = deflation.shape[2] * deflation.shape[3] * deflation.shape[4]
     normalizer = 1.0 / (24.0 * cell_count)
     live_mask = (lax.iota(jnp.int32, deflation.shape[4]) < depths[0]).astype(jnp.bfloat16)
-    live_field = deflation * live_mask
-    diagonal_block = local_terms(deflation, stiffness, depths)
-    top_x = live_field[:, :, -1]
-    bottom_x = live_field[:, :, 0]
+    bottom_x = deflation[:, :, 0] * live_mask
+    bottom_y = deflation[:, :, :, 0] * live_mask
     weight_top_x = stiffness[1, -1]
+    weight_top_y = stiffness[2, :, -1]
     next_x = from_behind(bottom_x, "sub", -1)
-    coupling_x = -gram_of(weighted(weight_top_x, top_x), next_x)
-    face_term = gram_of(next_x, weighted(weight_top_x, next_x))
-    lower_x = from_behind(face_term, "sub", 1)
-    diagonal_block = diagonal_block + lower_x
-    bottom_y = live_field[:, :, :, 0]
-    weight_top_y = stiffness[2, :, -1]
+    weight_low_x = from_behind(weight_top_x, "sub", 1)
     next_y = from_behind(bottom_y, "grp", -1)
     weight_low_y = from_behind(weight_top_y, "grp", 1)
+    diagonal_block = local_terms(deflation, stiffness, depths)
+    top_x = deflation[:, :, -1] * live_mask
+    top_y = deflation[:, :, :, -1] * live_mask
+    coupling_x = -gram_of(weighted(weight_top_x, top_x), next_x)
+    coupling_y = -gram_of(weighted(weight_top_y, top_y), next_y)
+    diagonal_block = diagonal_block + gram_of(bottom_x, weighted(weight_low_x, bottom_x))
     diagonal_block = diagonal_block + gram_of(bottom_y, weighted(weight_low_y, bottom_y))
-    coupling_y = -gram_of(weighted(weight_top_y, live_field[:, :, :, -1]), next_y)
     row_block = normalizer * jnp.concatenate([diagonal_block, coupling_x, coupling_y], axis=1)
     groups = lax.axis_size("grp")
     copies = jnp.broadcast_to(row_block[None, None], (1, groups) + row_block.shape)

time: 74.4 us -> 69.5 us (0.934)
  local copies, waits for them, and re-layouts: 2.23 us -> 6.93 us
  waiting for transfers between devices: 4.14 us -> 0.02 us
  other arithmetic: 4.99 us -> 1.04 us
  matrix products: 4.5 us -> 1.81 us
  blocking collectives: 19.8 us -> 21 us
    slice x0 -> x2, local copies, waits for them, and re-layouts: none -> 5.43 us  [the longest x1 4.35 us: shards(): top_y = deflation[:, :, :, -1] * live_mask]
    mul x2, other arithmetic: 4.89 us -> 0.27 us  [the longest x1 0.24 us: shards(): bottom_y = deflation[:, :, :, 0] * live_mask]
    ppermute x4, waiting for transfers between devices: 4.14 us -> 0.02 us  [from_behind(): return lax.ppermute(x, axis, pairs)]
    dot_general x4, matrix products: 4.5 us -> 1.81 us  [gram_of(): jnp.dot(left_side.reshape(count, -1), right_side.reshape(count, -1).T, pr...]
    all_to_all x1, blocking collectives: 19.8 us -> 21 us  [shards(): return lax.all_to_all(copies, 'grp', 1, 1, tiled=True)]
  transfers between devices with their start and end apart: 4 -> 4, of which waited for: 1 -> 0; matrix products, arithmetic and copies ran while one was open for 8% -> 11% of each run, Pallas kernels for 27% -> 29%
where the time goes in v4:
time: 69.5 us; the launch traced here: 69.1 us
  blocking collectives  21 us (30%)
  Pallas kernels  19.7 us (28%)
  starting transfers between devices  17.8 us (26%)
  local copies, waits for them, and re-layouts  6.93 us (10%)
  matrix products  1.81 us (3%)
  other arithmetic  1.04 us (1%)
  between operations  0.77 us (1%)
    all_to_all x1, blocking collectives, shards(): return lax.all_to_all(copies, 'grp', 1, 1, tiled=True)  21 us
    pallas_call x1, Pallas kernels, local_terms(): pl.pallas_call(local_kernel, out_shape=jax.ShapeDtypeStruct((count, count...  19.7 us
    ppermute x4, starting transfers between devices, from_behind(): return lax.ppermute(x, axis, pairs)  17.8 us
    slice x1, local copies, waits for them, and re-layouts, shards(): top_y = deflation[:, :, :, -1] * live_mask  4.35 us
    dot_general x4, matrix products, gram_of(): jnp.dot(left_side.reshape(count, -1), right_side.reshape(count, -1).T, pr...  1.81 us
  transfers between devices with their start and end apart: 4, of which 0 were waited for; matrix products, arithmetic and copies ran while one was open for 11% of the time, Pallas kernels for 29%

profile of v4, /device:TPU:10, one launch (start us, length us, event | category | flops | bytes accessed | tf_op | source)
XLA Modules:
  0.0 69.1 jit_solution(8994679190702121463)
XLA Ops:
  0.0 0.7 slice_bitcast_fusion
  0.7 1.9 %collective-permute-start = (bf16[8,128]{1,0:T(8,128)(2,1)S(1)}, bf16[8,128]{1,0:T(8,128)(2,1)S(1)}, u32[]{:S(2)}, u32[]{:S(2)}) collective-permute-start(bf16[8,128]{1,0:T(8,128)(2,1)S(1)} %get-tuple-element.11), channel_id=1, source_target_pairs={{0,16},{16,32},{32,48},{48,64},{64,80},{80,96},{96,112},{112,128},... | collective-permute-start | bytes 6152 | tf_op jit(solution)/shard_map/ppermute | solution.py:12
  2.6 0.8 %slice.21 = bf16[1,16,1,128]{3,2,1,0:T(2,128)(2,1)S(1)} slice(bf16[4,16,8,128]{3,2,1,0:T(8,128)(2,1)} %coeff_ref.1), slice={[2:3], [0:16], [7:8], [0:128]} | slice | bytes 8192 | tf_op jit(solution)/shard_map/slice | solution.py:94
  3.4 3.5 %collective-permute-start.1 = (bf16[16,128]{1,0:T(8,128)(2,1)S(1)}, bf16[16,128]{1,0:T(8,128)(2,1)S(1)}, u32[]{:S(2)}, u32[]{:S(2)}) collective-permute-start(bf16[16,128]{1,0:T(8,128)(2,1)S(1)} %get-tuple-element.6), channel_id=1, source_target_pairs={{0,1},{1,2},{2,3},{3,4},{4,5},{5,6},{6,7},{7,8},{8,9},{9,10},{10,1... | collective-permute-start | bytes 12296 | tf_op jit(solution)/shard_map/ppermute | solution.py:12
  7.5 1.1 %fusion.28 = (bf16[32,3,1,8,128]{4,3,2,1,0:T(8,128)(2,1)S(1)}, bf16[32,3,1,8,128]{4,3,2,1,0:T(8,128)(2,1)S(1)}) fusion(bf16[32,3,16,8,128]{4,3,2,1,0:T(8,128)(2,1)} %defl_ref.1), kind=kLoop, calls=%fused_computation.40 | loop fusion | bytes 786432 | tf_op jit(solution)/shard_map/slice | solution.py:100
  8.7 10.1 %collective-permute-start.2 = (bf16[32,3,8,128]{3,0,2,1:T(8,128)(2,1)S(1)}, bf16[32,3,8,128]{3,0,2,1:T(8,128)(2,1)S(1)}, u32[]{:S(2)}, u32[]{:S(2)}) collective-permute-start(bf16[32,3,8,128]{3,0,2,1:T(8,128)(2,1)S(1)} %bitcast_multiply_fusion.1), channel_id=1, source_target_pairs={{16,0},{32,16},{48,32},{64,48},{80,64},{96,80},{112,96},{128,112},... | collective-permute-start | bytes 589832 | tf_op jit(solution)/shard_map/ppermute | solution.py:12
  18.7 4.4 %fusion.29 = (bf16[32,3,16,1,128]{4,3,2,1,0:T(2,128)(2,1)S(1)}, bf16[32,3,16,1,128]{4,3,2,1,0:T(2,128)(2,1)S(1)}) fusion(bf16[32,3,16,8,128]{4,3,2,1,0:T(8,128)(2,1)} %defl_ref.1), kind=kLoop, calls=%fused_computation.41 | loop fusion | bytes 1572864 | tf_op jit(solution)/shard_map/slice | solution.py:101
  23.1 0.2 bitcast_multiply_fusion
  23.3 2.4 %collective-permute-start.3 = (bf16[32,3,16,128]{3,0,2,1:T(8,128)(2,1)S(1)}, bf16[32,3,16,128]{3,0,2,1:T(8,128)(2,1)S(1)}, u32[]{:S(2)}, u32[]{:S(2)}) collective-permute-start(bf16[32,3,16,128]{3,0,2,1:T(8,128)(2,1)S(1)} %bitcast_multiply_fusion), channel_id=1, source_target_pairs={{1,0},{2,1},{3,2},{4,3},{5,4},{6,5},{7,6},{8,7},{9,8},{10,9},{11,1... | collective-permute-start | bytes 1179656 | tf_op jit(solution)/shard_map/ppermute | solution.py:12
  25.7 19.7 %shard_map.37 = f32[32,32]{1,0:T(8,128)} custom-call(s32[1]{0:T(128)} %copy.57.depth_ref, bf16[32,3,16,8,128]{4,3,2,1,0:T(8,128)(2,1)} %defl_ref.1, bf16[4,16,8,128]{3,2,1,0:T(8,128)(2,1)} %coeff_ref.1), custom_call_target="tpu_custom_call" | custom-call | flops 402653184 | bytes 3276800 | tf_op jit(solution)/shard_map/pallas_call | solution.py:74
  45.4 0.0 collective-permute-done
  45.4 0.0 collective-permute-done.1
  45.4 0.4 convolution_bitcast_fusion.1
  45.8 0.9 %fusion.3 = f32[32,32]{1,0:T(8,128)S(1)} fusion(f32[32,32]{1,0:T(8,128)S(1)} %convolution_bitcast_fusion.1, f32[32,32]{1,0:T(8,128)} %shard_map.37, f32[8,128]{1,0:T(8,128)S(1)} %convert_element_type.55, bf16[32,3,1,8,128]{4,3,2,1,0:T(8,128)(2,1)S(1)} %get-tuple-element.8, bf16[128]{0:T(256)(128)(2,1)S(1)} %compare_convert_fusion), kind=kOutput, calls=%fused_computation.7 | convolution fusion | flops 6785024 | bytes 213248 | tf_op jit(solution)/shard_map/dot_general | solution.py:17
  46.7 0.0 collective-permute-done.2
  46.7 0.2 fusion.1
  46.9 0.0 collective-permute-done.3
  46.9 0.4 fusion
  47.3 0.1 maximum_multiply_fusion
  47.4 21.0 %all_to_all.5 = f32[1,16,32,96]{3,2,0,1:T(8,128)S(1)} all-to-all(f32[1,16,32,96]{3,2,0,1:T(8,128)S(1)} %broadcast_in_dim.2), channel_id=1, replica_groups=mesh['sub'=32,'grp'=16] {'grp'}, dimensions={1} | all-to-all | bytes 393216 | tf_op jit(solution)/shard_map/all_to_all | solution.py:109
  68.4 0.7 %copy.58 = f32[1,16,32,96]{3,2,1,0:T(8,128)} copy(f32[1,16,32,96]{3,2,1,0:T(8,128)S(1)} %bitcast.66) | data formatting | bytes 393216
  (6 shorter events, 0.1 us)
Async XLA Ops:
  0.7 44.7 %collective-permute-start = (bf16[8,128]{1,0:T(8,128)(2,1)S(1)}, bf16[8,128]{1,0:T(8,128)(2,1)S(1)}, u32[]{:S(2)}, u32[]{:S(2)}) collective-permute-start(bf16[8,128]{1,0:T(8,128)(2,1)S(1)} %get-tuple-element.11), channel_id=1, source_target_pairs={{0,16},{16,32},{32,48},{48,64},{64,80},{80,96},{96,112},{112,128},... | collective-permute-start | bytes 6152 | tf_op jit(solution)/shard_map/ppermute | solution.py:12
  3.4 42.0 %collective-permute-start.1 = (bf16[16,128]{1,0:T(8,128)(2,1)S(1)}, bf16[16,128]{1,0:T(8,128)(2,1)S(1)}, u32[]{:S(2)}, u32[]{:S(2)}) collective-permute-start(bf16[16,128]{1,0:T(8,128)(2,1)S(1)} %get-tuple-element.6), channel_id=1, source_target_pairs={{0,1},{1,2},{2,3},{3,4},{4,5},{5,6},{6,7},{7,8},{8,9},{9,10},{10,1... | collective-permute-start | bytes 12296 | tf_op jit(solution)/shard_map/ppermute | solution.py:12
  8.7 38.1 %collective-permute-start.2 = (bf16[32,3,8,128]{3,0,2,1:T(8,128)(2,1)S(1)}, bf16[32,3,8,128]{3,0,2,1:T(8,128)(2,1)S(1)}, u32[]{:S(2)}, u32[]{:S(2)}) collective-permute-start(bf16[32,3,8,128]{3,0,2,1:T(8,128)(2,1)S(1)} %bitcast_multiply_fusion.1), channel_id=1, source_target_pairs={{16,0},{32,16},{48,32},{64,48},{80,64},{96,80},{112,96},{128,112},... | collective-permute-start | bytes 589832 | tf_op jit(solution)/shard_map/ppermute | solution.py:12
  23.3 23.6 %collective-permute-start.3 = (bf16[32,3,16,128]{3,0,2,1:T(8,128)(2,1)S(1)}, bf16[32,3,16,128]{3,0,2,1:T(8,128)(2,1)S(1)}, u32[]{:S(2)}, u32[]{:S(2)}) collective-permute-start(bf16[32,3,16,128]{3,0,2,1:T(8,128)(2,1)S(1)} %bitcast_multiply_fusion), channel_id=1, source_target_pairs={{1,0},{2,1},{3,2},{4,3},{5,4},{6,5},{7,6},{8,7},{9,8},{10,9},{11,1... | collective-permute-start | bytes 1179656 | tf_op jit(solution)/shard_map/ppermute | solution.py:12

commit v5 on v4

--- a/solution.py
+++ b/solution.py
@@ -25,63 +25,70 @@
     return (weight.astype(jnp.float32) * values.astype(jnp.float32)).astype(jnp.bfloat16)
 
 
-def local_kernel(depth_ref, defl_ref, coeff_ref, out_ref):
+def block_kernel(depth_ref, defl_ref, coeff_ref, out_ref, acc_ref):
     count, comps, rows, cols, depth = defl_ref.shape
-    lane = lax.broadcasted_iota(jnp.int32, (count, depth), 1)
+    tall = count * cols
+    lane = lax.broadcasted_iota(jnp.int32, (count, cols, depth), 2)
+    sub = lax.broadcasted_iota(jnp.int32, (count, cols, depth), 1)
     live_mask = (lane < depth_ref[0]).astype(jnp.bfloat16)
     last_z = lane == depth - 1
+    last_y = sub == cols - 1
+    acc_ref[...] = jnp.zeros_like(acc_ref)
 
-    def slab(comp, row, col):
-        return (defl_ref[:, comp, row, col, :] * live_mask).astype(jnp.float32)
+    def tiles(comp, row):
+        return (defl_ref[:, comp, row] * live_mask).astype(jnp.float32)
 
-    def weight(entry, row, col):
-        return coeff_ref[entry, row, pl.ds(col, 1), :].astype(jnp.float32)
-
-    def body(row, acc):
+    def body(row, carry):
         has_next = row < rows - 1
         following_row = jnp.minimum(row + 1, rows - 1)
+        w = [coeff_ref[e, row].astype(jnp.float32)[None] for e in range(4)]
+        lefts, rights = [], []
         for comp in range(comps):
-            lefts, rights = [], []
-            lives = [slab(comp, row, col) for col in range(cols)]
-            for col in range(cols):
-                live = lives[col]
-                next_x = jnp.where(has_next, slab(comp, following_row, col), 0.0)
-                next_y = lives[col + 1] if col + 1 < cols else jnp.zeros_like(live)
-                next_z = jnp.where(last_z, 0.0, pltpu.roll(live, depth - 1, 1))
-                step_x = (live - next_x).astype(jnp.bfloat16)
-                step_y = (live - next_y).astype(jnp.bfloat16)
-                step_z = (live - next_z).astype(jnp.bfloat16)
-                lefts += [live.astype(jnp.bfloat16), step_x, step_y, step_z]
-                rights += [
-                    (weight(0, row, col) * live).astype(jnp.bfloat16),
-                    (weight(1, row, col) * step_x.astype(jnp.float32)).astype(jnp.bfloat16),
-                    (weight(2, row, col) * step_y.astype(jnp.float32)).astype(jnp.bfloat16),
-                    (weight(3, row, col) * step_z.astype(jnp.float32)).astype(jnp.bfloat16),
-                ]
-            left = jnp.concatenate(lefts, axis=1)
-            right = jnp.concatenate(rights, axis=1)
-            acc = acc + lax.dot_general(
-                left, right, (((1,), (1,)), ((), ())), preferred_element_type=jnp.float32
-            )
-        return acc
+            live = tiles(comp, row)
+            next_x = jnp.where(has_next, tiles(comp, following_row), 0.0)
+            next_y = jnp.where(last_y, 0.0, pltpu.roll(live, cols - 1, 1))
+            next_z = jnp.where(last_z, 0.0, pltpu.roll(live, depth - 1, 2))
+            step_x = (live - next_x).astype(jnp.bfloat16)
+            step_y = (live - next_y).astype(jnp.bfloat16)
+            step_z = (live - next_z).astype(jnp.bfloat16)
+            lefts += [live.astype(jnp.bfloat16), step_x, step_y, step_z]
+            rights += [
+                (w[0] * live).astype(jnp.bfloat16),
+                (w[1] * step_x.astype(jnp.float32)).astype(jnp.bfloat16),
+                (w[2] * step_y.astype(jnp.float32)).astype(jnp.bfloat16),
+                (w[3] * step_z.astype(jnp.float32)).astype(jnp.bfloat16),
+            ]
+        left = jnp.concatenate([v.reshape(tall, depth) for v in lefts], axis=1)
+        right = jnp.concatenate([v.reshape(tall, depth) for v in rights], axis=1)
+        acc_ref[...] += lax.dot_general(
+            left, right, (((1,), (1,)), ((), ())), preferred_element_type=jnp.float32
+        )
+        return carry
 
-    acc = lax.fori_loop(0, rows, body, jnp.zeros((count, count), jnp.float32))
-    out_ref[...] = acc
+    lax.fori_loop(0, rows, body, 0)
+    r = lax.broadcasted_iota(jnp.int32, (tall, tall), 0)
+    c = lax.broadcasted_iota(jnp.int32, (tall, tall), 1)
+    same = (r & (cols - 1)) == (c & (cols - 1))
+    kept = jnp.where(same, acc_ref[...], 0.0)
+    out_ref[...] = kept.reshape(count, cols, tall).sum(axis=1)
 
 
 def local_terms(deflation, coefficients, depths):
-    count = deflation.shape[0]
-    return pl.pallas_call(
-        local_kernel,
-        out_shape=jax.ShapeDtypeStruct((count, count), jnp.float32),
+    count, comps, rows, cols, depth = deflation.shape
+    tall = count * cols
+    partial = pl.pallas_call(
+        block_kernel,
+        out_shape=jax.ShapeDtypeStruct((count, tall), jnp.float32),
         in_specs=[pl.BlockSpec(memory_space=pltpu.SMEM)] + [pl.BlockSpec(memory_space=pltpu.VMEM)] * 2,
         out_specs=pl.BlockSpec(memory_space=pltpu.VMEM),
+        scratch_shapes=[pltpu.VMEM((tall, tall), jnp.float32)],
         cost_estimate=pl.CostEstimate(
-            flops=2 * 4 * count * deflation.size,
+            flops=2 * 4 * tall * tall * comps * rows * depth,
             bytes_accessed=deflation.size * 2 + coefficients.size * 2,
             transcendentals=0,
         ),
     )(depths, deflation, coefficients)
+    return partial.reshape(count, count, cols).sum(axis=2)
 
 
 def shards(deflation, stiffness, depths):

time: 69.5 us -> 61.5 us (0.88)
  Pallas kernels: 19.7 us -> 11.5 us
  local copies, waits for them, and re-layouts: 6.93 us -> 7.86 us
  matrix products: 1.81 us -> 1.1 us
    pallas_call x1, Pallas kernels: 19.7 us -> 11.5 us  [local_terms(): pl.pallas_call(block_kernel, out_shape=jax.ShapeDtypeStruct((count, tall)...]
    pallas_call x0 -> x1, local copies, waits for them, and re-layouts: none -> 0.85 us  [local_terms(): pl.pallas_call(block_kernel, out_shape=jax.ShapeDtypeStruct((count, tall)...]
    dot_general x4, matrix products: 1.81 us -> 1.1 us  [gram_of(): jnp.dot(left_side.reshape(count, -1), right_side.reshape(count, -1).T, pr...]
  transfers between devices with their start and end apart: 4 -> 4, of which waited for: 0 -> 0; matrix products, arithmetic and copies ran while one was open for 11% -> 13% of each run, Pallas kernels for 29% -> 19%
where the time goes in v5:
time: 61.5 us; the launch traced here: 61.1 us
  blocking collectives  21 us (34%)
  starting transfers between devices  17.8 us (29%)
  Pallas kernels  11.5 us (19%)
  local copies, waits for them, and re-layouts  7.86 us (13%)
  matrix products  1.1 us (2%)
  other arithmetic  1.08 us (2%)
  between operations  0.79 us (1%)
    all_to_all x1, blocking collectives, shards(): return lax.all_to_all(copies, 'grp', 1, 1, tiled=True)  21 us
    ppermute x4, starting transfers between devices, from_behind(): return lax.ppermute(x, axis, pairs)  17.8 us
    pallas_call x1, Pallas kernels, local_terms(): pl.pallas_call(block_kernel, out_shape=jax.ShapeDtypeStruct((count, tall)...  11.5 us
    slice x1, local copies, waits for them, and re-layouts, shards(): top_y = deflation[:, :, :, -1] * live_mask  4.35 us
  transfers between devices with their start and end apart: 4, of which 0 were waited for; matrix products, arithmetic and copies ran while one was open for 13% of the time, Pallas kernels for 19%

profile of v5, /device:TPU:10, one launch (start us, length us, event | category | flops | bytes accessed | tf_op | source)
XLA Modules:
  0.0 61.1 jit_solution(15994765178314343528)
XLA Ops:
  0.0 0.7 %slice_bitcast_fusion = (bf16[8,128]{1,0:T(8,128)(2,1)S(1)}, f32[8,128]{1,0:T(8,128)S(1)}) fusion(bf16[4,16,8,128]{3,2,1,0:T(8,128)(2,1)} %coeff_ref.1), kind=kLoop, calls=%fused_computation.37 | loop fusion | flops 1024 | bytes 8192 | tf_op jit(solution)/shard_map/squeeze | solution.py:100
  0.7 1.9 %collective-permute-start = (bf16[8,128]{1,0:T(8,128)(2,1)S(1)}, bf16[8,128]{1,0:T(8,128)(2,1)S(1)}, u32[]{:S(2)}, u32[]{:S(2)}) collective-permute-start(bf16[8,128]{1,0:T(8,128)(2,1)S(1)} %get-tuple-element.11), channel_id=1, source_target_pairs={{0,16},{16,32},{32,48},{48,64},{64,80},{80,96},{96,112},{112,128},... | collective-permute-start | bytes 6152 | tf_op jit(solution)/shard_map/ppermute | solution.py:12
  2.6 0.8 %slice.21 = bf16[1,16,1,128]{3,2,1,0:T(2,128)(2,1)S(1)} slice(bf16[4,16,8,128]{3,2,1,0:T(8,128)(2,1)} %coeff_ref.1), slice={[2:3], [0:16], [7:8], [0:128]} | slice | bytes 8192 | tf_op jit(solution)/shard_map/slice | solution.py:101
  3.4 3.5 %collective-permute-start.1 = (bf16[16,128]{1,0:T(8,128)(2,1)S(1)}, bf16[16,128]{1,0:T(8,128)(2,1)S(1)}, u32[]{:S(2)}, u32[]{:S(2)}) collective-permute-start(bf16[16,128]{1,0:T(8,128)(2,1)S(1)} %get-tuple-element.6), channel_id=1, source_target_pairs={{0,1},{1,2},{2,3},{3,4},{4,5},{5,6},{6,7},{7,8},{8,9},{9,10},{10,1... | collective-permute-start | bytes 12296 | tf_op jit(solution)/shard_map/ppermute | solution.py:12
  7.5 1.1 %fusion.28 = (bf16[32,3,1,8,128]{4,3,2,1,0:T(8,128)(2,1)S(1)}, bf16[32,3,1,8,128]{4,3,2,1,0:T(8,128)(2,1)S(1)}) fusion(bf16[32,3,16,8,128]{4,3,2,1,0:T(8,128)(2,1)} %defl_ref.1), kind=kLoop, calls=%fused_computation.41 | loop fusion | bytes 786432 | tf_op jit(solution)/shard_map/slice | solution.py:107
  8.7 10.1 %collective-permute-start.2 = (bf16[32,3,8,128]{3,0,2,1:T(8,128)(2,1)S(1)}, bf16[32,3,8,128]{3,0,2,1:T(8,128)(2,1)S(1)}, u32[]{:S(2)}, u32[]{:S(2)}) collective-permute-start(bf16[32,3,8,128]{3,0,2,1:T(8,128)(2,1)S(1)} %bitcast_multiply_fusion.1), channel_id=1, source_target_pairs={{16,0},{32,16},{48,32},{64,48},{80,64},{96,80},{112,96},{128,112},... | collective-permute-start | bytes 589832 | tf_op jit(solution)/shard_map/ppermute | solution.py:12
  18.7 4.4 %fusion.29 = (bf16[32,3,16,1,128]{4,3,2,1,0:T(2,128)(2,1)S(1)}, bf16[32,3,16,1,128]{4,3,2,1,0:T(2,128)(2,1)S(1)}) fusion(bf16[32,3,16,8,128]{4,3,2,1,0:T(8,128)(2,1)} %defl_ref.1), kind=kLoop, calls=%fused_computation.42 | loop fusion | bytes 1572864 | tf_op jit(solution)/shard_map/slice | solution.py:108
  23.1 0.2 bitcast_multiply_fusion
  23.3 2.4 %collective-permute-start.3 = (bf16[32,3,16,128]{3,0,2,1:T(8,128)(2,1)S(1)}, bf16[32,3,16,128]{3,0,2,1:T(8,128)(2,1)S(1)}, u32[]{:S(2)}, u32[]{:S(2)}) collective-permute-start(bf16[32,3,16,128]{3,0,2,1:T(8,128)(2,1)S(1)} %bitcast_multiply_fusion), channel_id=1, source_target_pairs={{1,0},{2,1},{3,2},{4,3},{5,4},{6,5},{7,6},{8,7},{9,8},{10,9},{11,1... | collective-permute-start | bytes 1179656 | tf_op jit(solution)/shard_map/ppermute | solution.py:12
  25.7 11.5 %shard_map.37 = f32[32,256]{1,0:T(8,128)} custom-call(s32[1]{0:T(128)} %copy.60.depth_ref, bf16[32,3,16,8,128]{4,3,2,1,0:T(8,128)(2,1)} %defl_ref.1, bf16[4,16,8,128]{3,2,1,0:T(8,128)(2,1)} %coeff_ref.1), custom_call_target="tpu_custom_call" | custom-call | flops 3221225472 | bytes 3276800 | tf_op jit(solution)/shard_map/pallas_call | solution.py:79
  37.2 0.9 %copy.14 = f32[32,256]{0,1:T(8,128)S(1)} copy(f32[32,256]{1,0:T(8,128)} %shard_map.37) | data formatting | bytes 65536 | tf_op jit(solution)/shard_map/pallas_call | solution.py:79
  38.1 0.1 copy.16
  38.1 0.0 collective-permute-done
  38.1 0.0 collective-permute-done.1
  38.2 0.4 convolution_bitcast_fusion.1
  38.5 0.2 fusion.3
  38.7 0.0 collective-permute-done.2
  38.7 0.2 fusion.1
  38.9 0.0 collective-permute-done.3
  38.9 0.4 fusion
  39.3 0.1 maximum_multiply_fusion
  39.4 21.0 %all_to_all.5 = f32[1,16,32,96]{3,2,0,1:T(8,128)S(1)} all-to-all(f32[1,16,32,96]{3,2,0,1:T(8,128)S(1)} %broadcast_in_dim.2), channel_id=1, replica_groups=mesh['sub'=32,'grp'=16] {'grp'}, dimensions={1} | all-to-all | bytes 393216 | tf_op jit(solution)/shard_map/all_to_all | solution.py:116
  60.4 0.7 %copy.61 = f32[1,16,32,96]{3,2,1,0:T(8,128)} copy(f32[1,16,32,96]{3,2,1,0:T(8,128)S(1)} %bitcast.68) | data formatting | bytes 393216
  (7 shorter events, 0.1 us)
Async XLA Ops:
  0.7 37.5 %collective-permute-start = (bf16[8,128]{1,0:T(8,128)(2,1)S(1)}, bf16[8,128]{1,0:T(8,128)(2,1)S(1)}, u32[]{:S(2)}, u32[]{:S(2)}) collective-permute-start(bf16[8,128]{1,0:T(8,128)(2,1)S(1)} %get-tuple-element.11), channel_id=1, source_target_pairs={{0,16},{16,32},{32,48},{48,64},{64,80},{80,96},{96,112},{112,128},... | collective-permute-start | bytes 6152 | tf_op jit(solution)/shard_map/ppermute | solution.py:12
  3.4 34.8 %collective-permute-start.1 = (bf16[16,128]{1,0:T(8,128)(2,1)S(1)}, bf16[16,128]{1,0:T(8,128)(2,1)S(1)}, u32[]{:S(2)}, u32[]{:S(2)}) collective-permute-start(bf16[16,128]{1,0:T(8,128)(2,1)S(1)} %get-tuple-element.6), channel_id=1, source_target_pairs={{0,1},{1,2},{2,3},{3,4},{4,5},{5,6},{6,7},{7,8},{8,9},{9,10},{10,1... | collective-permute-start | bytes 12296 | tf_op jit(solution)/shard_map/ppermute | solution.py:12
  8.7 30.1 %collective-permute-start.2 = (bf16[32,3,8,128]{3,0,2,1:T(8,128)(2,1)S(1)}, bf16[32,3,8,128]{3,0,2,1:T(8,128)(2,1)S(1)}, u32[]{:S(2)}, u32[]{:S(2)}) collective-permute-start(bf16[32,3,8,128]{3,0,2,1:T(8,128)(2,1)S(1)} %bitcast_multiply_fusion.1), channel_id=1, source_target_pairs={{16,0},{32,16},{48,32},{64,48},{80,64},{96,80},{112,96},{128,112},... | collective-permute-start | bytes 589832 | tf_op jit(solution)/shard_map/ppermute | solution.py:12
  23.3 15.6 %collective-permute-start.3 = (bf16[32,3,16,128]{3,0,2,1:T(8,128)(2,1)S(1)}, bf16[32,3,16,128]{3,0,2,1:T(8,128)(2,1)S(1)}, u32[]{:S(2)}, u32[]{:S(2)}) collective-permute-start(bf16[32,3,16,128]{3,0,2,1:T(8,128)(2,1)S(1)} %bitcast_multiply_fusion), channel_id=1, source_target_pairs={{1,0},{2,1},{3,2},{4,3},{5,4},{6,5},{7,6},{8,7},{9,8},{10,9},{11,1... | collective-permute-start | bytes 1179656 | tf_op jit(solution)/shard_map/ppermute | solution.py:12

commit v6 on v5

--- a/solution.py
+++ b/solution.py
@@ -35,29 +35,22 @@
     last_y = sub == cols - 1
     acc_ref[...] = jnp.zeros_like(acc_ref)
 
-    def tiles(comp, row):
-        return (defl_ref[:, comp, row] * live_mask).astype(jnp.float32)
-
     def body(row, carry):
         has_next = row < rows - 1
         following_row = jnp.minimum(row + 1, rows - 1)
-        w = [coeff_ref[e, row].astype(jnp.float32)[None] for e in range(4)]
+        w = [coeff_ref[e, row][None] for e in range(4)]
         lefts, rights = [], []
         for comp in range(comps):
-            live = tiles(comp, row)
-            next_x = jnp.where(has_next, tiles(comp, following_row), 0.0)
-            next_y = jnp.where(last_y, 0.0, pltpu.roll(live, cols - 1, 1))
-            next_z = jnp.where(last_z, 0.0, pltpu.roll(live, depth - 1, 2))
-            step_x = (live - next_x).astype(jnp.bfloat16)
-            step_y = (live - next_y).astype(jnp.bfloat16)
-            step_z = (live - next_z).astype(jnp.bfloat16)
-            lefts += [live.astype(jnp.bfloat16), step_x, step_y, step_z]
-            rights += [
-                (w[0] * live).astype(jnp.bfloat16),
-                (w[1] * step_x.astype(jnp.float32)).astype(jnp.bfloat16),
-                (w[2] * step_y.astype(jnp.float32)).astype(jnp.bfloat16),
-                (w[3] * step_z.astype(jnp.float32)).astype(jnp.bfloat16),
-            ]
+            live = defl_ref[:, comp, row] * live_mask
+            next_x = jnp.where(has_next, defl_ref[:, comp, following_row] * live_mask, 0)
+            wide = live.astype(jnp.float32)
+            next_y = jnp.where(last_y, 0.0, pltpu.roll(wide, cols - 1, 1))
+            next_z = jnp.where(last_z, 0, pltpu.roll(live, depth - 1, 2))
+            step_x = live - next_x
+            step_y = (wide - next_y).astype(jnp.bfloat16)
+            step_z = live - next_z
+            lefts += [live, step_x, step_y, step_z]
+            rights += [w[0] * live, w[1] * step_x, w[2] * step_y, w[3] * step_z]
         left = jnp.concatenate([v.reshape(tall, depth) for v in lefts], axis=1)
         right = jnp.concatenate([v.reshape(tall, depth) for v in rights], axis=1)
         acc_ref[...] += lax.dot_general(
@@ -101,7 +94,7 @@
     weight_top_y = stiffness[2, :, -1]
     next_x = from_behind(bottom_x, "sub", -1)
     weight_low_x = from_behind(weight_top_x, "sub", 1)
-    next_y = from_behind(bottom_y, "grp", -1)
+    next_y = from_behind(deflation[:, :, :, :2] * live_mask, "grp", -1)[:, :, :, 0]
     weight_low_y = from_behind(weight_top_y, "grp", 1)
     diagonal_block = local_terms(deflation, stiffness, depths)
     top_x = deflation[:, :, -1] * live_mask

time: 61.5 us -> 60.9 us (level)
  matrix products: 1.1 us -> 2.8 us
  local copies, waits for them, and re-layouts: 7.86 us -> 6.19 us
  Pallas kernels: 11.5 us -> 10.4 us
    dot_general x4, matrix products: 1.1 us -> 2.8 us  [gram_of(): jnp.dot(left_side.reshape(count, -1), right_side.reshape(count, -1).T, pr...]
    pallas_call x1, Pallas kernels: 11.5 us -> 10.4 us  [local_terms(): pl.pallas_call(block_kernel, out_shape=jax.ShapeDtypeStruct((count, tall)...]
    slice x1, local copies, waits for them, and re-layouts: 1.07 us -> 0.07 us  [shards(): top_x = deflation[:, :, -1] * live_mask]
    slice x1 -> x2, local copies, waits for them, and re-layouts: 4.35 us -> 3.54 us  [the longest x1 2.46 us: shards(): deflation[:, :, :, :2] * live_mask]
  transfers between devices with their start and end apart: 4 -> 4, of which waited for: 0 -> 0; matrix products, arithmetic and copies ran while one was open for 13% -> 13% of each run, Pallas kernels for 19% -> 17%
where the time goes in v6:
time: 60.9 us; the launch traced here: 60.5 us
  blocking collectives  21 us (34%)
  starting transfers between devices  17.7 us (29%)
  Pallas kernels  10.4 us (17%)
  local copies, waits for them, and re-layouts  6.19 us (10%)
  matrix products  2.8 us (5%)
  other arithmetic  1.59 us (3%)
  between operations  0.82 us (1%)
    all_to_all x1, blocking collectives, shards(): return lax.all_to_all(copies, 'grp', 1, 1, tiled=True)  21 us
    ppermute x4, starting transfers between devices, from_behind(): return lax.ppermute(x, axis, pairs)  17.7 us
    pallas_call x1, Pallas kernels, local_terms(): pl.pallas_call(block_kernel, out_shape=jax.ShapeDtypeStruct((count, tall)...  10.4 us
    dot_general x4, matrix products, gram_of(): jnp.dot(left_side.reshape(count, -1), right_side.reshape(count, -1).T, pr...  2.8 us
    slice x1, local copies, waits for them, and re-layouts, shards(): deflation[:, :, :, :2] * live_mask  2.46 us
  transfers between devices with their start and end apart: 4, of which 0 were waited for; matrix products, arithmetic and copies ran while one was open for 13% of the time, Pallas kernels for 17%

profile of v6, /device:TPU:10, one launch (start us, length us, event | category | flops | bytes accessed | tf_op | source)
XLA Modules:
  0.0 60.5 jit_solution(15048103749885089105)
XLA Ops:
  0.0 0.0 copy-start
  0.0 0.9 %slice.27 = bf16[1,16,1,128]{3,2,1,0:T(2,128)(2,1)S(1)} slice(bf16[4,16,8,128]{3,2,1,0:T(8,128)(2,1)} %coeff_ref.1), slice={[2:3], [0:16], [7:8], [0:128]} | slice | bytes 8192 | tf_op jit(solution)/shard_map/slice | solution.py:94
  0.9 3.6 %collective-permute-start.1 = (bf16[16,128]{1,0:T(8,128)(2,1)S(1)}, bf16[16,128]{1,0:T(8,128)(2,1)S(1)}, u32[]{:S(2)}, u32[]{:S(2)}) collective-permute-start(bf16[16,128]{1,0:T(8,128)(2,1)S(1)} %get-tuple-element.6), channel_id=1, source_target_pairs={{0,1},{1,2},{2,3},{3,4},{4,5},{5,6},{6,7},{7,8},{8,9},{9,10},{10,1... | collective-permute-start | bytes 12296 | tf_op jit(solution)/shard_map/ppermute | solution.py:12
  4.6 0.7 %slice_bitcast_fusion.2 = (bf16[8,128]{1,0:T(8,128)(2,1)S(1)}, f32[8,128]{1,0:T(8,128)S(1)}) fusion(bf16[4,16,8,128]{3,2,1,0:T(8,128)(2,1)} %coeff_ref.1), kind=kLoop, calls=%fused_computation.36 | loop fusion | flops 1024 | bytes 8192 | tf_op jit(solution)/shard_map/squeeze | solution.py:93
  5.2 1.9 %collective-permute-start = (bf16[8,128]{1,0:T(8,128)(2,1)S(1)}, bf16[8,128]{1,0:T(8,128)(2,1)S(1)}, u32[]{:S(2)}, u32[]{:S(2)}) collective-permute-start(bf16[8,128]{1,0:T(8,128)(2,1)S(1)} %get-tuple-element.11), channel_id=1, source_target_pairs={{0,16},{16,32},{32,48},{48,64},{64,80},{80,96},{96,112},{112,128},... | collective-permute-start | bytes 6152 | tf_op jit(solution)/shard_map/ppermute | solution.py:12
  7.8 2.5 %slice.30 = bf16[32,3,16,2,128]{4,3,2,1,0:T(2,128)(2,1)S(1)} slice(bf16[32,3,16,8,128]{4,3,2,1,0:T(8,128)(2,1)} %defl_ref.1), slice={[0:32], [0:3], [0:16], [0:2], [0:128]} | slice | bytes 1572864 | tf_op jit(solution)/shard_map/slice | solution.py:97
  10.3 0.5 copy_multiply_fusion
  10.8 2.4 %collective-permute-start.3 = (bf16[32,3,16,2,128]{4,0,2,1,3:T(8,128)(2,1)S(1)}, bf16[32,3,16,2,128]{4,0,2,1,3:T(8,128)(2,1)}, u32[]{:S(2)}, u32[]{:S(2)}) collective-permute-start(bf16[32,3,16,2,128]{4,0,2,1,3:T(8,128)(2,1)S(1)} %copy_multiply_fusion), channel_id=1, source_target_pairs={{1,0},{2,1},{3,2},{4,3},{5,4},{6,5},{7,6},{8,7},{9,8},{10,9},{11,1... | collective-permute-start | bytes 2359304 | tf_op jit(solution)/shard_map/ppermute | solution.py:12
  13.1 0.0 copy-done
  13.1 0.1 fusion.24
  13.2 9.8 %collective-permute-start.2 = (bf16[32,3,8,128]{3,0,2,1:T(8,128)(2,1)S(1)}, bf16[32,3,8,128]{3,0,2,1:T(8,128)(2,1)}, u32[]{:S(2)}, u32[]{:S(2)}) collective-permute-start(bf16[32,3,8,128]{3,0,2,1:T(8,128)(2,1)S(1)} %bitcast_multiply_fusion), channel_id=1, source_target_pairs={{16,0},{32,16},{48,32},{64,48},{80,64},{96,80},{112,96},{128,112},... | collective-permute-start | bytes 589832 | tf_op jit(solution)/shard_map/ppermute | solution.py:12
  23.1 1.1 %fusion.23 = (bf16[32,3,16,1,128]{4,3,2,1,0:T(2,128)(2,1)S(1)}, bf16[32,3,16,1,128]{4,3,2,1,0:T(2,128)(2,1)S(1)}) fusion(bf16[32,3,16,8,128]{4,3,2,1,0:T(8,128)(2,1)S(1)} %copy-done), kind=kLoop, calls=%fused_computation.40 | loop fusion | bytes 1572864 | tf_op jit(solution)/shard_map/slice | solution.py:92
  24.1 10.4 %shard_map.37 = f32[32,256]{1,0:T(8,128)} custom-call(s32[1]{0:T(128)} %copy.73.depth_ref, bf16[32,3,16,8,128]{4,3,2,1,0:T(8,128)(2,1)} %defl_ref.1, bf16[4,16,8,128]{3,2,1,0:T(8,128)(2,1)} %coeff_ref.1), custom_call_target="tpu_custom_call" | custom-call | flops 3221225472 | bytes 3276800 | tf_op jit(solution)/shard_map/pallas_call | solution.py:72
  34.5 0.1 fusion.18
  34.6 0.9 %copy.20 = f32[32,256]{0,1:T(8,128)S(1)} copy(f32[32,256]{1,0:T(8,128)} %shard_map.37) | data formatting | bytes 65536 | tf_op jit(solution)/shard_map/pallas_call | solution.py:72
  35.5 0.1 copy.22
  35.6 0.0 collective-permute-done
  35.6 0.0 collective-permute-done.1
  35.6 0.2 fusion.4
  35.8 0.3 convolution_bitcast_fusion.1
  36.1 0.2 fusion.3
  36.3 0.0 collective-permute-done.2
  36.3 1.1 %fusion.1 = f32[32,32]{1,0:T(8,128)S(1)} fusion(bf16[32,3,8,128]{3,0,2,1:T(8,128)(2,1)} %collective-permute-done.2, bf16[32,3,1,8,128]{4,3,2,1,0:T(8,128)(2,1)S(1)} %get-tuple-element.9, f32[8,128]{1,0:T(8,128)S(1)} %get-tuple-element.12, bf16[128]{0:T(256)(128)(2,1)S(1)} %compare_convert_fusion), kind=kOutput, calls=%fused_computation.4 | convolution fusion | flops 6685696 | bytes 401664 | tf_op jit(solution)/shard_map/dot_general | solution.py:17
  37.4 0.0 collective-permute-done.3
  37.4 1.2 %fusion = f32[32,32]{1,0:T(8,128)S(1)} fusion(bf16[32,3,16,2,128]{4,0,2,1,3:T(8,128)(2,1)} %collective-permute-done.3, bf16[32,3,16,128]{3,2,1,0:T(8,128)(2,1)S(1)} %get-tuple-element.14), kind=kOutput, calls=%fused_computation.1 | convolution fusion | flops 12583936 | bytes 790528 | tf_op jit(solution)/shard_map/dot_general | solution.py:17
  38.7 0.1 maximum_multiply_fusion
  38.8 21.0 %all_to_all.5 = f32[1,16,32,96]{3,2,0,1:T(8,128)S(1)} all-to-all(f32[1,16,32,96]{3,2,0,1:T(8,128)S(1)} %broadcast_in_dim.2), channel_id=1, replica_groups=mesh['sub'=32,'grp'=16] {'grp'}, dimensions={1} | all-to-all | bytes 393216 | tf_op jit(solution)/shard_map/all_to_all | solution.py:109
  59.8 0.7 %copy.74 = f32[1,16,32,96]{3,2,1,0:T(8,128)} copy(f32[1,16,32,96]{3,2,1,0:T(8,128)S(1)} %bitcast.61) | data formatting | bytes 393216
  (7 shorter events, 0.1 us)
Async XLA Ops:
  0.0 13.1 %copy-start = (bf16[32,3,16,8,128]{4,3,2,1,0:T(8,128)(2,1)S(1)}, bf16[32,3,16,8,128]{4,3,2,1,0:T(8,128)(2,1)}, u32[]{:S(2)}) copy-start(bf16[32,3,16,8,128]{4,3,2,1,0:T(8,128)(2,1)} %defl_ref.1) | copy-start | bytes 9437188
  0.9 34.6 %collective-permute-start.1 = (bf16[16,128]{1,0:T(8,128)(2,1)S(1)}, bf16[16,128]{1,0:T(8,128)(2,1)S(1)}, u32[]{:S(2)}, u32[]{:S(2)}) collective-permute-start(bf16[16,128]{1,0:T(8,128)(2,1)S(1)} %get-tuple-element.6), channel_id=1, source_target_pairs={{0,1},{1,2},{2,3},{3,4},{4,5},{5,6},{6,7},{7,8},{8,9},{9,10},{10,1... | collective-permute-start | bytes 12296 | tf_op jit(solution)/shard_map/ppermute | solution.py:12
  5.2 30.3 %collective-permute-start = (bf16[8,128]{1,0:T(8,128)(2,1)S(1)}, bf16[8,128]{1,0:T(8,128)(2,1)S(1)}, u32[]{:S(2)}, u32[]{:S(2)}) collective-permute-start(bf16[8,128]{1,0:T(8,128)(2,1)S(1)} %get-tuple-element.11), channel_id=1, source_target_pairs={{0,16},{16,32},{32,48},{48,64},{64,80},{80,96},{96,112},{112,128},... | collective-permute-start | bytes 6152 | tf_op jit(solution)/shard_map/ppermute | solution.py:12
  10.8 26.7 %collective-permute-start.3 = (bf16[32,3,16,2,128]{4,0,2,1,3:T(8,128)(2,1)S(1)}, bf16[32,3,16,2,128]{4,0,2,1,3:T(8,128)(2,1)}, u32[]{:S(2)}, u32[]{:S(2)}) collective-permute-start(bf16[32,3,16,2,128]{4,0,2,1,3:T(8,128)(2,1)S(1)} %copy_multiply_fusion), channel_id=1, source_target_pairs={{1,0},{2,1},{3,2},{4,3},{5,4},{6,5},{7,6},{8,7},{9,8},{10,9},{11,1... | collective-permute-start | bytes 2359304 | tf_op jit(solution)/shard_map/ppermute | solution.py:12
  13.2 23.0 %collective-permute-start.2 = (bf16[32,3,8,128]{3,0,2,1:T(8,128)(2,1)S(1)}, bf16[32,3,8,128]{3,0,2,1:T(8,128)(2,1)}, u32[]{:S(2)}, u32[]{:S(2)}) collective-permute-start(bf16[32,3,8,128]{3,0,2,1:T(8,128)(2,1)S(1)} %bitcast_multiply_fusion), channel_id=1, source_target_pairs={{16,0},{32,16},{48,32},{64,48},{80,64},{96,80},{112,96},{128,112},... | collective-permute-start | bytes 589832 | tf_op jit(solution)/shard_map/ppermute | solution.py:12

commit v7 on v4

--- a/solution.py
+++ b/solution.py
@@ -27,46 +27,44 @@
 
 def local_kernel(depth_ref, defl_ref, coeff_ref, out_ref):
     count, comps, rows, cols, depth = defl_ref.shape
-    lane = lax.broadcasted_iota(jnp.int32, (count, depth), 1)
+    width = cols * depth
+    lane = lax.broadcasted_iota(jnp.int32, (count, cols, depth), 2)
     live_mask = (lane < depth_ref[0]).astype(jnp.bfloat16)
-    last_z = lane == depth - 1
+    wide_lane = lax.broadcasted_iota(jnp.int32, (count, width), 1)
+    last_z = (wide_lane & (depth - 1)) == depth - 1
+    zero_slab = jnp.zeros((count, depth), jnp.float32)
 
-    def slab(comp, row, col):
-        return (defl_ref[:, comp, row, col, :] * live_mask).astype(jnp.float32)
+    def flat(row, comp):
+        tiles = (defl_ref[:, comp, row] * live_mask).astype(jnp.float32)
+        turned = pltpu.einshape("kyz->ykz", tiles)
+        return jnp.concatenate([turned[col] for col in range(cols)], axis=1).astype(jnp.bfloat16)
 
-    def weight(entry, row, col):
-        return coeff_ref[entry, row, pl.ds(col, 1), :].astype(jnp.float32)
+    def weight(entry, row):
+        w = coeff_ref[entry, row]
+        return jnp.concatenate([w[col:col + 1] for col in range(cols)], axis=1)
 
     def body(row, acc):
         has_next = row < rows - 1
         following_row = jnp.minimum(row + 1, rows - 1)
+        w = [weight(e, row) for e in range(4)]
+        lefts, rights = [], []
         for comp in range(comps):
-            lefts, rights = [], []
-            lives = [slab(comp, row, col) for col in range(cols)]
-            for col in range(cols):
-                live = lives[col]
-                next_x = jnp.where(has_next, slab(comp, following_row, col), 0.0)
-                next_y = lives[col + 1] if col + 1 < cols else jnp.zeros_like(live)
-                next_z = jnp.where(last_z, 0.0, pltpu.roll(live, depth - 1, 1))
-                step_x = (live - next_x).astype(jnp.bfloat16)
-                step_y = (live - next_y).astype(jnp.bfloat16)
-                step_z = (live - next_z).astype(jnp.bfloat16)
-                lefts += [live.astype(jnp.bfloat16), step_x, step_y, step_z]
-                rights += [
-                    (weight(0, row, col) * live).astype(jnp.bfloat16),
-                    (weight(1, row, col) * step_x.astype(jnp.float32)).astype(jnp.bfloat16),
-                    (weight(2, row, col) * step_y.astype(jnp.float32)).astype(jnp.bfloat16),
-                    (weight(3, row, col) * step_z.astype(jnp.float32)).astype(jnp.bfloat16),
-                ]
-            left = jnp.concatenate(lefts, axis=1)
-            right = jnp.concatenate(rights, axis=1)
-            acc = acc + lax.dot_general(
-                left, right, (((1,), (1,)), ((), ())), preferred_element_type=jnp.float32
-            )
-        return acc
+            live = flat(row, comp)
+            next_x = jnp.where(has_next, flat(following_row, comp), 0)
+            next_y = jnp.concatenate([live[:, depth:], jnp.zeros_like(live[:, :depth])], axis=1)
+            next_z = jnp.where(last_z, 0, pltpu.roll(live, width - 1, 1))
+            step_x = live - next_x
+            step_y = live - next_y
+            step_z = live - next_z
+            lefts += [live, step_x, step_y, step_z]
+            rights += [w[0] * live, w[1] * step_x, w[2] * step_y, w[3] * step_z]
+        left = jnp.concatenate(lefts, axis=1)
+        right = jnp.concatenate(rights, axis=1)
+        return acc + lax.dot_general(
+            left, right, (((1,), (1,)), ((), ())), preferred_element_type=jnp.float32
+        )
 
-    acc = lax.fori_loop(0, rows, body, jnp.zeros((count, count), jnp.float32))
-    out_ref[...] = acc
+    out_ref[...] = lax.fori_loop(0, rows, body, jnp.zeros((count, count), jnp.float32))
 
 
 def local_terms(deflation, coefficients, depths):

time: 69.5 us -> 60.3 us (0.87)
  Pallas kernels: 19.7 us -> 10.6 us
    pallas_call x1, Pallas kernels: 19.7 us -> 10.6 us  [local_terms(): pl.pallas_call(local_kernel, out_shape=jax.ShapeDtypeStruct((count, count...]
  transfers between devices with their start and end apart: 4 -> 4, of which waited for: 0 -> 0; matrix products, arithmetic and copies ran while one was open for 11% -> 13% of each run, Pallas kernels for 29% -> 18%
where the time goes in v7:
time: 60.3 us; the launch traced here: 59.9 us
  blocking collectives  21 us (35%)
  starting transfers between devices  17.8 us (30%)
  Pallas kernels  10.6 us (18%)
  local copies, waits for them, and re-layouts  6.93 us (11%)
  matrix products  1.82 us (3%)
  other arithmetic  1.04 us (2%)
  between operations  0.77 us (1%)
    all_to_all x1, blocking collectives, shards(): return lax.all_to_all(copies, 'grp', 1, 1, tiled=True)  21 us
    ppermute x4, starting transfers between devices, from_behind(): return lax.ppermute(x, axis, pairs)  17.8 us
    pallas_call x1, Pallas kernels, local_terms(): pl.pallas_call(local_kernel, out_shape=jax.ShapeDtypeStruct((count, count...  10.6 us
    slice x1, local copies, waits for them, and re-layouts, shards(): top_y = deflation[:, :, :, -1] * live_mask  4.35 us
    dot_general x4, matrix products, gram_of(): jnp.dot(left_side.reshape(count, -1), right_side.reshape(count, -1).T, pr...  1.82 us
  transfers between devices with their start and end apart: 4, of which 0 were waited for; matrix products, arithmetic and copies ran while one was open for 13% of the time, Pallas kernels for 18%

profile of v7, /device:TPU:10, one launch (start us, length us, event | category | flops | bytes accessed | tf_op | source)
XLA Modules:
  0.0 59.9 jit_solution(12269879843420997721)
XLA Ops:
  0.0 0.7 %slice_bitcast_fusion = (bf16[8,128]{1,0:T(8,128)(2,1)S(1)}, f32[8,128]{1,0:T(8,128)S(1)}) fusion(bf16[4,16,8,128]{3,2,1,0:T(8,128)(2,1)} %coeff_ref.1), kind=kLoop, calls=%fused_computation.36 | loop fusion | flops 1024 | bytes 8192 | tf_op jit(solution)/shard_map/squeeze | solution.py:91
  0.7 1.9 %collective-permute-start = (bf16[8,128]{1,0:T(8,128)(2,1)S(1)}, bf16[8,128]{1,0:T(8,128)(2,1)S(1)}, u32[]{:S(2)}, u32[]{:S(2)}) collective-permute-start(bf16[8,128]{1,0:T(8,128)(2,1)S(1)} %get-tuple-element.11), channel_id=1, source_target_pairs={{0,16},{16,32},{32,48},{48,64},{64,80},{80,96},{96,112},{112,128},... | collective-permute-start | bytes 6152 | tf_op jit(solution)/shard_map/ppermute | solution.py:12
  2.6 0.8 %slice.21 = bf16[1,16,1,128]{3,2,1,0:T(2,128)(2,1)S(1)} slice(bf16[4,16,8,128]{3,2,1,0:T(8,128)(2,1)} %coeff_ref.1), slice={[2:3], [0:16], [7:8], [0:128]} | slice | bytes 8192 | tf_op jit(solution)/shard_map/slice | solution.py:92
  3.4 3.5 %collective-permute-start.1 = (bf16[16,128]{1,0:T(8,128)(2,1)S(1)}, bf16[16,128]{1,0:T(8,128)(2,1)S(1)}, u32[]{:S(2)}, u32[]{:S(2)}) collective-permute-start(bf16[16,128]{1,0:T(8,128)(2,1)S(1)} %get-tuple-element.6), channel_id=1, source_target_pairs={{0,1},{1,2},{2,3},{3,4},{4,5},{5,6},{6,7},{7,8},{8,9},{9,10},{10,1... | collective-permute-start | bytes 12296 | tf_op jit(solution)/shard_map/ppermute | solution.py:12
  7.5 1.1 %fusion.28 = (bf16[32,3,1,8,128]{4,3,2,1,0:T(8,128)(2,1)S(1)}, bf16[32,3,1,8,128]{4,3,2,1,0:T(8,128)(2,1)S(1)}) fusion(bf16[32,3,16,8,128]{4,3,2,1,0:T(8,128)(2,1)} %defl_ref.1), kind=kLoop, calls=%fused_computation.40 | loop fusion | bytes 786432 | tf_op jit(solution)/shard_map/slice | solution.py:98
  8.7 10.1 %collective-permute-start.2 = (bf16[32,3,8,128]{3,0,2,1:T(8,128)(2,1)S(1)}, bf16[32,3,8,128]{3,0,2,1:T(8,128)(2,1)S(1)}, u32[]{:S(2)}, u32[]{:S(2)}) collective-permute-start(bf16[32,3,8,128]{3,0,2,1:T(8,128)(2,1)S(1)} %bitcast_multiply_fusion.1), channel_id=1, source_target_pairs={{16,0},{32,16},{48,32},{64,48},{80,64},{96,80},{112,96},{128,112},... | collective-permute-start | bytes 589832 | tf_op jit(solution)/shard_map/ppermute | solution.py:12
  18.7 4.4 %fusion.29 = (bf16[32,3,16,1,128]{4,3,2,1,0:T(2,128)(2,1)S(1)}, bf16[32,3,16,1,128]{4,3,2,1,0:T(2,128)(2,1)S(1)}) fusion(bf16[32,3,16,8,128]{4,3,2,1,0:T(8,128)(2,1)} %defl_ref.1), kind=kLoop, calls=%fused_computation.41 | loop fusion | bytes 1572864 | tf_op jit(solution)/shard_map/slice | solution.py:99
  23.1 0.2 bitcast_multiply_fusion
  23.3 2.4 %collective-permute-start.3 = (bf16[32,3,16,128]{3,0,2,1:T(8,128)(2,1)S(1)}, bf16[32,3,16,128]{3,0,2,1:T(8,128)(2,1)S(1)}, u32[]{:S(2)}, u32[]{:S(2)}) collective-permute-start(bf16[32,3,16,128]{3,0,2,1:T(8,128)(2,1)S(1)} %bitcast_multiply_fusion), channel_id=1, source_target_pairs={{1,0},{2,1},{3,2},{4,3},{5,4},{6,5},{7,6},{8,7},{9,8},{10,9},{11,1... | collective-permute-start | bytes 1179656 | tf_op jit(solution)/shard_map/ppermute | solution.py:12
  25.7 10.6 %shard_map.37 = f32[32,32]{1,0:T(8,128)} custom-call(s32[1]{0:T(128)} %copy.57.depth_ref, bf16[32,3,16,8,128]{4,3,2,1,0:T(8,128)(2,1)} %defl_ref.1, bf16[4,16,8,128]{3,2,1,0:T(8,128)(2,1)} %coeff_ref.1), custom_call_target="tpu_custom_call" | custom-call | flops 402653184 | bytes 3276800 | tf_op jit(solution)/shard_map/pallas_call | solution.py:72
  36.3 0.0 collective-permute-done
  36.3 0.0 collective-permute-done.1
  36.3 0.4 convolution_bitcast_fusion.1
  36.7 0.9 %fusion.3 = f32[32,32]{1,0:T(8,128)S(1)} fusion(f32[32,32]{1,0:T(8,128)S(1)} %convolution_bitcast_fusion.1, f32[32,32]{1,0:T(8,128)} %shard_map.37, f32[8,128]{1,0:T(8,128)S(1)} %convert_element_type.55, bf16[32,3,1,8,128]{4,3,2,1,0:T(8,128)(2,1)S(1)} %get-tuple-element.8, bf16[128]{0:T(256)(128)(2,1)S(1)} %compare_convert_fusion), kind=kOutput, calls=%fused_computation.7 | convolution fusion | flops 6785024 | bytes 213248 | tf_op jit(solution)/shard_map/dot_general | solution.py:17
  37.6 0.0 collective-permute-done.2
  37.6 0.2 fusion.1
  37.8 0.0 collective-permute-done.3
  37.8 0.4 fusion
  38.2 0.1 maximum_multiply_fusion
  38.3 21.0 %all_to_all.5 = f32[1,16,32,96]{3,2,0,1:T(8,128)S(1)} all-to-all(f32[1,16,32,96]{3,2,0,1:T(8,128)S(1)} %broadcast_in_dim.2), channel_id=1, replica_groups=mesh['sub'=32,'grp'=16] {'grp'}, dimensions={1} | all-to-all | bytes 393216 | tf_op jit(solution)/shard_map/all_to_all | solution.py:107
  59.2 0.7 %copy.58 = f32[1,16,32,96]{3,2,1,0:T(8,128)} copy(f32[1,16,32,96]{3,2,1,0:T(8,128)S(1)} %bitcast.66) | data formatting | bytes 393216
  (6 shorter events, 0.1 us)
Async XLA Ops:
  0.7 35.6 %collective-permute-start = (bf16[8,128]{1,0:T(8,128)(2,1)S(1)}, bf16[8,128]{1,0:T(8,128)(2,1)S(1)}, u32[]{:S(2)}, u32[]{:S(2)}) collective-permute-start(bf16[8,128]{1,0:T(8,128)(2,1)S(1)} %get-tuple-element.11), channel_id=1, source_target_pairs={{0,16},{16,32},{32,48},{48,64},{64,80},{80,96},{96,112},{112,128},... | collective-permute-start | bytes 6152 | tf_op jit(solution)/shard_map/ppermute | solution.py:12
  3.4 32.9 %collective-permute-start.1 = (bf16[16,128]{1,0:T(8,128)(2,1)S(1)}, bf16[16,128]{1,0:T(8,128)(2,1)S(1)}, u32[]{:S(2)}, u32[]{:S(2)}) collective-permute-start(bf16[16,128]{1,0:T(8,128)(2,1)S(1)} %get-tuple-element.6), channel_id=1, source_target_pairs={{0,1},{1,2},{2,3},{3,4},{4,5},{5,6},{6,7},{7,8},{8,9},{9,10},{10,1... | collective-permute-start | bytes 12296 | tf_op jit(solution)/shard_map/ppermute | solution.py:12
  8.7 28.9 %collective-permute-start.2 = (bf16[32,3,8,128]{3,0,2,1:T(8,128)(2,1)S(1)}, bf16[32,3,8,128]{3,0,2,1:T(8,128)(2,1)S(1)}, u32[]{:S(2)}, u32[]{:S(2)}) collective-permute-start(bf16[32,3,8,128]{3,0,2,1:T(8,128)(2,1)S(1)} %bitcast_multiply_fusion.1), channel_id=1, source_target_pairs={{16,0},{32,16},{48,32},{64,48},{80,64},{96,80},{112,96},{128,112},... | collective-permute-start | bytes 589832 | tf_op jit(solution)/shard_map/ppermute | solution.py:12
  23.3 14.4 %collective-permute-start.3 = (bf16[32,3,16,128]{3,0,2,1:T(8,128)(2,1)S(1)}, bf16[32,3,16,128]{3,0,2,1:T(8,128)(2,1)S(1)}, u32[]{:S(2)}, u32[]{:S(2)}) collective-permute-start(bf16[32,3,16,128]{3,0,2,1:T(8,128)(2,1)S(1)} %bitcast_multiply_fusion), channel_id=1, source_target_pairs={{1,0},{2,1},{3,2},{4,3},{5,4},{6,5},{7,6},{8,7},{9,8},{10,9},{11,1... | collective-permute-start | bytes 1179656 | tf_op jit(solution)/shard_map/ppermute | solution.py:12

commit v8 on v7

--- a/solution.py
+++ b/solution.py
@@ -25,19 +25,29 @@
     return (weight.astype(jnp.float32) * values.astype(jnp.float32)).astype(jnp.bfloat16)
 
 
-def local_kernel(depth_ref, defl_ref, coeff_ref, out_ref):
+def turn_kernel(depth_ref, defl_ref, live_ref, edge_ref):
     count, comps, rows, cols, depth = defl_ref.shape
-    width = cols * depth
     lane = lax.broadcasted_iota(jnp.int32, (count, cols, depth), 2)
     live_mask = (lane < depth_ref[0]).astype(jnp.bfloat16)
-    wide_lane = lax.broadcasted_iota(jnp.int32, (count, width), 1)
-    last_z = (wide_lane & (depth - 1)) == depth - 1
-    zero_slab = jnp.zeros((count, depth), jnp.float32)
 
-    def flat(row, comp):
-        tiles = (defl_ref[:, comp, row] * live_mask).astype(jnp.float32)
-        turned = pltpu.einshape("kyz->ykz", tiles)
-        return jnp.concatenate([turned[col] for col in range(cols)], axis=1).astype(jnp.bfloat16)
+    def body(row, carry):
+        for comp in range(comps):
+            tiles = (defl_ref[:, comp, row] * live_mask).astype(jnp.float32)
+            turned = pltpu.einshape("kyz->ykz", tiles).astype(jnp.bfloat16)
+            for col in range(cols):
+                live_ref[comp, row, :, pl.ds(col * depth, depth)] = turned[col]
+            edge_ref[0, comp, row] = turned[0]
+            edge_ref[1, comp, row] = turned[cols - 1]
+        return carry
+
+    lax.fori_loop(0, rows, body, 0)
+
+
+def local_kernel(live_ref, coeff_ref, out_ref):
+    comps, rows, count, width = live_ref.shape
+    cols, depth = coeff_ref.shape[2:]
+    lane = lax.broadcasted_iota(jnp.int32, (count, width), 1)
+    last_z = (lane & (depth - 1)) == depth - 1
 
     def weight(entry, row):
         w = coeff_ref[entry, row]
@@ -49,8 +59,8 @@
         w = [weight(e, row) for e in range(4)]
         lefts, rights = [], []
         for comp in range(comps):
-            live = flat(row, comp)
-            next_x = jnp.where(has_next, flat(following_row, comp), 0)
+            live = live_ref[comp, row]
+            next_x = jnp.where(has_next, live_ref[comp, following_row], 0)
             next_y = jnp.concatenate([live[:, depth:], jnp.zeros_like(live[:, :depth])], axis=1)
             next_z = jnp.where(last_z, 0, pltpu.roll(live, width - 1, 1))
             step_x = live - next_x
@@ -67,19 +77,37 @@
     out_ref[...] = lax.fori_loop(0, rows, body, jnp.zeros((count, count), jnp.float32))
 
 
-def local_terms(deflation, coefficients, depths):
-    count = deflation.shape[0]
+def turned_field(deflation, depths):
+    count, comps, rows, cols, depth = deflation.shape
+    return pl.pallas_call(
+        turn_kernel,
+        out_shape=(
+            jax.ShapeDtypeStruct((comps, rows, count, cols * depth), jnp.bfloat16),
+            jax.ShapeDtypeStruct((2, comps, rows, count, depth), jnp.bfloat16),
+        ),
+        in_specs=[pl.BlockSpec(memory_space=pltpu.SMEM), pl.BlockSpec(memory_space=pltpu.VMEM)],
+        out_specs=(pl.BlockSpec(memory_space=pltpu.VMEM), pl.BlockSpec(memory_space=pltpu.VMEM)),
+        cost_estimate=pl.CostEstimate(flops=0, bytes_accessed=deflation.size * 5, transcendentals=0),
+    )(depths, deflation)
+
+
+def local_terms(live_t, coefficients):
+    count = live_t.shape[2]
     return pl.pallas_call(
         local_kernel,
         out_shape=jax.ShapeDtypeStruct((count, count), jnp.float32),
-        in_specs=[pl.BlockSpec(memory_space=pltpu.SMEM)] + [pl.BlockSpec(memory_space=pltpu.VMEM)] * 2,
+        in_specs=[pl.BlockSpec(memory_space=pltpu.VMEM)] * 2,
         out_specs=pl.BlockSpec(memory_space=pltpu.VMEM),
         cost_estimate=pl.CostEstimate(
-            flops=2 * 4 * count * deflation.size,
-            bytes_accessed=deflation.size * 2 + coefficients.size * 2,
+            flops=2 * 4 * count * live_t.size,
+            bytes_accessed=live_t.size * 2 + coefficients.size * 2,
             transcendentals=0,
         ),
-    )(depths, deflation, coefficients)
+    )(live_t, coefficients)
+
+
+def face_gram(left_side, right_side):
+    return jnp.einsum("cxkz,cxlz->kl", left_side, right_side, preferred_element_type=jnp.float32)
 
 
 def shards(deflation, stiffness, depths):
@@ -87,20 +115,20 @@
     normalizer = 1.0 / (24.0 * cell_count)
     live_mask = (lax.iota(jnp.int32, deflation.shape[4]) < depths[0]).astype(jnp.bfloat16)
     bottom_x = deflation[:, :, 0] * live_mask
-    bottom_y = deflation[:, :, :, 0] * live_mask
     weight_top_x = stiffness[1, -1]
     weight_top_y = stiffness[2, :, -1]
     next_x = from_behind(bottom_x, "sub", -1)
     weight_low_x = from_behind(weight_top_x, "sub", 1)
+    weight_low_y = from_behind(weight_top_y, "grp", 1)
+    live_t, edges = turned_field(deflation, depths)
+    bottom_y, top_y = edges[0], edges[1]
     next_y = from_behind(bottom_y, "grp", -1)
-    weight_low_y = from_behind(weight_top_y, "grp", 1)
-    diagonal_block = local_terms(deflation, stiffness, depths)
+    diagonal_block = local_terms(live_t, stiffness)
     top_x = deflation[:, :, -1] * live_mask
-    top_y = deflation[:, :, :, -1] * live_mask
     coupling_x = -gram_of(weighted(weight_top_x, top_x), next_x)
-    coupling_y = -gram_of(weighted(weight_top_y, top_y), next_y)
+    coupling_y = -face_gram(weighted(weight_top_y[None, :, None], top_y), next_y)
     diagonal_block = diagonal_block + gram_of(bottom_x, weighted(weight_low_x, bottom_x))
-    diagonal_block = diagonal_block + gram_of(bottom_y, weighted(weight_low_y, bottom_y))
+    diagonal_block = diagonal_block + face_gram(bottom_y, weighted(weight_low_y[None, :, None], bottom_y))
     row_block = normalizer * jnp.concatenate([diagonal_block, coupling_x, coupling_y], axis=1)
     groups = lax.axis_size("grp")
     copies = jnp.broadcast_to(row_block[None, None], (1, groups) + row_block.shape)

time: 60.3 us -> 60.6 us (level)
  Pallas kernels: 10.6 us -> 14.5 us
  local copies, waits for them, and re-layouts: 6.93 us -> 3.67 us
    pallas_call x0 -> x1, Pallas kernels: none -> 5.59 us  [turned_field(): pl.pallas_call(turn_kernel, out_shape=(jax.ShapeDtypeStruct((comps, rows,...]
    slice x1 -> x0, local copies, waits for them, and re-layouts: 4.35 us -> none  [shards(): top_y = deflation[:, :, :, -1] * live_mask]
    pallas_call x1, Pallas kernels: 10.6 us -> 8.9 us  [local_terms(): pl.pallas_call(local_kernel, out_shape=jax.ShapeDtypeStruct((count, count...]
    squeeze x0 -> x1, local copies, waits for them, and re-layouts: none -> 1.09 us  [shards(): bottom_y, top_y = (edges[0], edges[1])]
    dot_general x4 -> x2, matrix products: 1.82 us -> 1.11 us  [gram_of(): jnp.dot(left_side.reshape(count, -1), right_side.reshape(count, -1).T, pr...]
  transfers between devices with their start and end apart: 4 -> 4, of which waited for: 0 -> 0; matrix products, arithmetic and copies ran while one was open for 13% -> 7% of each run, Pallas kernels for 18% -> 24%
where the time goes in v8:
time: 60.6 us; the launch traced here: 60.2 us
  blocking collectives  21 us (35%)
  starting transfers between devices  17.8 us (29%)
  Pallas kernels  14.5 us (24%)
  local copies, waits for them, and re-layouts  3.67 us (6%)
  matrix products  1.6 us (3%)
  other arithmetic  0.82 us (1%)
  between operations  0.77 us (1%)
    all_to_all x1, blocking collectives, shards(): return lax.all_to_all(copies, 'grp', 1, 1, tiled=True)  21 us
    ppermute x4, starting transfers between devices, from_behind(): return lax.ppermute(x, axis, pairs)  17.8 us
    pallas_call x1, Pallas kernels, local_terms(): pl.pallas_call(local_kernel, out_shape=jax.ShapeDtypeStruct((count, count...  8.9 us
    pallas_call x1, Pallas kernels, turned_field(): pl.pallas_call(turn_kernel, out_shape=(jax.ShapeDtypeStruct((comps, rows,...  5.59 us
  transfers between devices with their start and end apart: 4, of which 0 were waited for; matrix products, arithmetic and copies ran while one was open for 7% of the time, Pallas kernels for 24%

profile of v8, /device:TPU:10, one launch (start us, length us, event | category | flops | bytes accessed | tf_op | source)
XLA Modules:
  0.0 60.2 jit_solution(7555503816045731302)
XLA Ops:
  0.0 0.8 %slice.21 = bf16[1,16,1,128]{3,2,1,0:T(2,128)(2,1)S(1)} slice(bf16[4,16,8,128]{3,2,1,0:T(8,128)(2,1)} %coeff_ref.1), slice={[2:3], [0:16], [7:8], [0:128]} | slice | bytes 8192 | tf_op jit(solution)/shard_map/slice | solution.py:119
  0.8 3.5 %collective-permute-start.1 = (bf16[16,128]{1,0:T(8,128)(2,1)S(1)}, bf16[16,128]{1,0:T(8,128)(2,1)S(1)}, u32[]{:S(2)}, u32[]{:S(2)}) collective-permute-start(bf16[16,128]{1,0:T(8,128)(2,1)S(1)} %get-tuple-element.10), channel_id=1, source_target_pairs={{0,1},{1,2},{2,3},{3,4},{4,5},{5,6},{6,7},{7,8},{8,9},{9,10},{10,1... | collective-permute-start | bytes 12296 | tf_op jit(solution)/shard_map/ppermute | solution.py:12
  4.3 0.7 %slice_bitcast_fusion.1 = (bf16[8,128]{1,0:T(8,128)(2,1)S(1)}, f32[8,128]{1,0:T(8,128)S(1)}) fusion(bf16[4,16,8,128]{3,2,1,0:T(8,128)(2,1)} %coeff_ref.1), kind=kLoop, calls=%fused_computation.33 | loop fusion | flops 1024 | bytes 8192 | tf_op jit(solution)/shard_map/squeeze | solution.py:118
  5.0 1.9 %collective-permute-start = (bf16[8,128]{1,0:T(8,128)(2,1)S(1)}, bf16[8,128]{1,0:T(8,128)(2,1)S(1)}, u32[]{:S(2)}, u32[]{:S(2)}) collective-permute-start(bf16[8,128]{1,0:T(8,128)(2,1)S(1)} %get-tuple-element.13), channel_id=1, source_target_pairs={{0,16},{16,32},{32,48},{48,64},{64,80},{80,96},{96,112},{112,128},... | collective-permute-start | bytes 6152 | tf_op jit(solution)/shard_map/ppermute | solution.py:12
  7.5 1.1 %fusion.26 = (bf16[32,3,1,8,128]{4,3,2,1,0:T(8,128)(2,1)S(1)}, bf16[32,3,1,8,128]{4,3,2,1,0:T(8,128)(2,1)S(1)}) fusion(bf16[32,3,16,8,128]{4,3,2,1,0:T(8,128)(2,1)} %defl_ref.1), kind=kLoop, calls=%fused_computation.37 | loop fusion | bytes 786432 | tf_op jit(solution)/shard_map/slice | solution.py:127
  8.7 10.1 %collective-permute-start.2 = (bf16[32,3,8,128]{3,0,2,1:T(8,128)(2,1)S(1)}, bf16[32,3,8,128]{3,0,2,1:T(8,128)(2,1)S(1)}, u32[]{:S(2)}, u32[]{:S(2)}) collective-permute-start(bf16[32,3,8,128]{3,0,2,1:T(8,128)(2,1)S(1)} %bitcast_multiply_fusion), channel_id=1, source_target_pairs={{16,0},{32,16},{48,32},{64,48},{80,64},{96,80},{112,96},{128,112},... | collective-permute-start | bytes 589832 | tf_op jit(solution)/shard_map/ppermute | solution.py:12
  18.7 5.6 %shard_map.37 = (bf16[3,16,32,1024]{3,2,1,0:T(8,128)(2,1)}, bf16[2,3,16,32,128]{4,3,2,1,0:T(8,128)(2,1)}) custom-call(s32[1]{0:T(128)} %copy.36.depth_ref, bf16[32,3,16,8,128]{4,3,2,1,0:T(8,128)(2,1)} %defl_ref.1), custom_call_target="tpu_custom_call" | custom-call | bytes 7864320 | tf_op jit(solution)/shard_map/pallas_call | solution.py:82
  24.3 0.0 copy-start
  24.3 1.1 %slice_bitcast_fusion = bf16[3,16,32,128]{3,2,1,0:T(8,128)(2,1)S(1)} fusion(bf16[2,3,16,32,128]{4,3,2,1,0:T(8,128)(2,1)} %get-tuple-element.8), kind=kLoop, calls=%fused_computation.19 | loop fusion | bytes 786432 | tf_op jit(solution)/shard_map/squeeze | solution.py:124
  25.4 2.4 %collective-permute-start.3 = (bf16[3,16,32,128]{3,2,1,0:T(8,128)(2,1)S(1)}, bf16[3,16,32,128]{3,2,1,0:T(8,128)(2,1)S(1)}, u32[]{:S(2)}, u32[]{:S(2)}) collective-permute-start(bf16[3,16,32,128]{3,2,1,0:T(8,128)(2,1)S(1)} %slice_bitcast_fusion), channel_id=1, source_target_pairs={{1,0},{2,1},{3,2},{4,3},{5,4},{6,5},{7,6},{8,7},{9,8},{10,9},{11,1... | collective-permute-start | bytes 1179656 | tf_op jit(solution)/shard_map/ppermute | solution.py:12
  27.8 8.9 %shard_map.38 = f32[32,32]{1,0:T(8,128)} custom-call(bf16[3,16,32,1024]{3,2,1,0:T(8,128)(2,1)} %get-tuple-element.7.live_ref, bf16[4,16,8,128]{3,2,1,0:T(8,128)(2,1)} %coeff_ref.1), custom_call_target="tpu_custom_call" | custom-call | flops 402653184 | bytes 3276800 | tf_op jit(solution)/shard_map/pallas_call | solution.py:96
  36.7 0.0 collective-permute-done
  36.7 0.0 collective-permute-done.1
  36.7 0.0 copy-done
  36.7 0.2 convolution_bitcast_fusion.1
  37.0 0.9 %fusion.3 = f32[32,32]{1,0:T(8,128)S(1)} fusion(f32[32,32]{1,0:T(8,128)S(1)} %convolution_bitcast_fusion.1, f32[32,32]{1,0:T(8,128)} %shard_map.38, f32[8,128]{1,0:T(8,128)S(1)} %convert_element_type.53, bf16[32,3,1,8,128]{4,3,2,1,0:T(8,128)(2,1)S(1)} %get-tuple-element.12, bf16[128]{0:T(256)(128)(2,1)S(1)} %compare_convert_fusion), kind=kOutput, calls=%fused_computation.7 | convolution fusion | flops 6785024 | bytes 213248 | tf_op jit(solution)/shard_map/dot_general | solution.py:17
  37.9 0.0 collective-permute-done.2
  37.9 0.2 fusion.1
  38.1 0.0 collective-permute-done.3
  38.1 0.2 fusion
  38.4 0.1 maximum_multiply_fusion
  38.5 21.0 %all_to_all.5 = f32[1,16,32,96]{3,2,0,1:T(8,128)S(1)} all-to-all(f32[1,16,32,96]{3,2,0,1:T(8,128)S(1)} %broadcast_in_dim.2), channel_id=1, replica_groups=mesh['sub'=32,'grp'=16] {'grp'}, dimensions={1} | all-to-all | bytes 393216 | tf_op jit(solution)/shard_map/all_to_all | solution.py:135
  59.5 0.7 %copy.37 = f32[1,16,32,96]{3,2,1,0:T(8,128)} copy(f32[1,16,32,96]{3,2,1,0:T(8,128)S(1)} %bitcast.63) | data formatting | bytes 393216
  (6 shorter events, 0.1 us)
Async XLA Ops:
  0.8 35.9 %collective-permute-start.1 = (bf16[16,128]{1,0:T(8,128)(2,1)S(1)}, bf16[16,128]{1,0:T(8,128)(2,1)S(1)}, u32[]{:S(2)}, u32[]{:S(2)}) collective-permute-start(bf16[16,128]{1,0:T(8,128)(2,1)S(1)} %get-tuple-element.10), channel_id=1, source_target_pairs={{0,1},{1,2},{2,3},{3,4},{4,5},{5,6},{6,7},{7,8},{8,9},{9,10},{10,1... | collective-permute-start | bytes 12296 | tf_op jit(solution)/shard_map/ppermute | solution.py:12
  5.0 31.7 %collective-permute-start = (bf16[8,128]{1,0:T(8,128)(2,1)S(1)}, bf16[8,128]{1,0:T(8,128)(2,1)S(1)}, u32[]{:S(2)}, u32[]{:S(2)}) collective-permute-start(bf16[8,128]{1,0:T(8,128)(2,1)S(1)} %get-tuple-element.13), channel_id=1, source_target_pairs={{0,16},{16,32},{32,48},{48,64},{64,80},{80,96},{96,112},{112,128},... | collective-permute-start | bytes 6152 | tf_op jit(solution)/shard_map/ppermute | solution.py:12
  8.7 29.3 %collective-permute-start.2 = (bf16[32,3,8,128]{3,0,2,1:T(8,128)(2,1)S(1)}, bf16[32,3,8,128]{3,0,2,1:T(8,128)(2,1)S(1)}, u32[]{:S(2)}, u32[]{:S(2)}) collective-permute-start(bf16[32,3,8,128]{3,0,2,1:T(8,128)(2,1)S(1)} %bitcast_multiply_fusion), channel_id=1, source_target_pairs={{16,0},{32,16},{48,32},{64,48},{80,64},{96,80},{112,96},{128,112},... | collective-permute-start | bytes 589832 | tf_op jit(solution)/shard_map/ppermute | solution.py:12
  24.3 12.4 %copy-start = (bf16[2,3,16,32,128]{4,3,2,1,0:T(8,128)(2,1)S(1)}, bf16[2,3,16,32,128]{4,3,2,1,0:T(8,128)(2,1)}, u32[]{:S(2)}) copy-start(bf16[2,3,16,32,128]{4,3,2,1,0:T(8,128)(2,1)} %get-tuple-element.8) | copy-start | bytes 2359300
  25.4 12.7 %collective-permute-start.3 = (bf16[3,16,32,128]{3,2,1,0:T(8,128)(2,1)S(1)}, bf16[3,16,32,128]{3,2,1,0:T(8,128)(2,1)S(1)}, u32[]{:S(2)}, u32[]{:S(2)}) collective-permute-start(bf16[3,16,32,128]{3,2,1,0:T(8,128)(2,1)S(1)} %slice_bitcast_fusion), channel_id=1, source_target_pairs={{1,0},{2,1},{3,2},{4,3},{5,4},{6,5},{7,6},{8,7},{9,8},{10,9},{11,1... | collective-permute-start | bytes 1179656 | tf_op jit(solution)/shard_map/ppermute | solution.py:12

commit v9 on v8

--- a/solution.py
+++ b/solution.py
@@ -40,7 +40,7 @@
             edge_ref[1, comp, row] = turned[cols - 1]
         return carry
 
-    lax.fori_loop(0, rows, body, 0)
+    lax.fori_loop(0, rows, body, 0, unroll=4)
 
 
 def local_kernel(live_ref, coeff_ref, out_ref):
@@ -74,7 +74,7 @@
             left, right, (((1,), (1,)), ((), ())), preferred_element_type=jnp.float32
         )
 
-    out_ref[...] = lax.fori_loop(0, rows, body, jnp.zeros((count, count), jnp.float32))
+    out_ref[...] = lax.fori_loop(0, rows, body, jnp.zeros((count, count), jnp.float32), unroll=8)
 
 
 def turned_field(deflation, depths):

time: 60.6 us -> 57.7 us (0.952)
  Pallas kernels: 14.5 us -> 11.6 us
    pallas_call x1, Pallas kernels: 8.9 us -> 6.11 us  [local_terms(): pl.pallas_call(local_kernel, out_shape=jax.ShapeDtypeStruct((count, count...]
  transfers between devices with their start and end apart: 4 -> 4, of which waited for: 0 -> 0; matrix products, arithmetic and copies ran while one was open for 7% -> 7% of each run, Pallas kernels for 24% -> 20%
where the time goes in v9:
time: 57.7 us; the launch traced here: 57.3 us
  blocking collectives  21 us (36%)
  starting transfers between devices  17.8 us (31%)
  Pallas kernels  11.6 us (20%)
  local copies, waits for them, and re-layouts  3.67 us (6%)
  matrix products  1.6 us (3%)
  other arithmetic  0.82 us (1%)
  between operations  0.77 us (1%)
    all_to_all x1, blocking collectives, shards(): return lax.all_to_all(copies, 'grp', 1, 1, tiled=True)  21 us
    ppermute x4, starting transfers between devices, from_behind(): return lax.ppermute(x, axis, pairs)  17.8 us
    pallas_call x1, Pallas kernels, local_terms(): pl.pallas_call(local_kernel, out_shape=jax.ShapeDtypeStruct((count, count...  6.11 us
    pallas_call x1, Pallas kernels, turned_field(): pl.pallas_call(turn_kernel, out_shape=(jax.ShapeDtypeStruct((comps, rows,...  5.5 us
  transfers between devices with their start and end apart: 4, of which 0 were waited for; matrix products, arithmetic and copies ran while one was open for 7% of the time, Pallas kernels for 20%

profile of v9, /device:TPU:10, one launch (start us, length us, event | category | flops | bytes accessed | tf_op | source)
XLA Modules:
  0.0 57.3 jit_solution(16191680657047213115)
XLA Ops:
  0.0 0.8 %slice.21 = bf16[1,16,1,128]{3,2,1,0:T(2,128)(2,1)S(1)} slice(bf16[4,16,8,128]{3,2,1,0:T(8,128)(2,1)} %coeff_ref.1), slice={[2:3], [0:16], [7:8], [0:128]} | slice | bytes 8192 | tf_op jit(solution)/shard_map/slice | solution.py:119
  0.8 3.5 %collective-permute-start.1 = (bf16[16,128]{1,0:T(8,128)(2,1)S(1)}, bf16[16,128]{1,0:T(8,128)(2,1)S(1)}, u32[]{:S(2)}, u32[]{:S(2)}) collective-permute-start(bf16[16,128]{1,0:T(8,128)(2,1)S(1)} %get-tuple-element.10), channel_id=1, source_target_pairs={{0,1},{1,2},{2,3},{3,4},{4,5},{5,6},{6,7},{7,8},{8,9},{9,10},{10,1... | collective-permute-start | bytes 12296 | tf_op jit(solution)/shard_map/ppermute | solution.py:12
  4.3 0.7 %slice_bitcast_fusion.1 = (bf16[8,128]{1,0:T(8,128)(2,1)S(1)}, f32[8,128]{1,0:T(8,128)S(1)}) fusion(bf16[4,16,8,128]{3,2,1,0:T(8,128)(2,1)} %coeff_ref.1), kind=kLoop, calls=%fused_computation.33 | loop fusion | flops 1024 | bytes 8192 | tf_op jit(solution)/shard_map/squeeze | solution.py:118
  5.0 1.9 %collective-permute-start = (bf16[8,128]{1,0:T(8,128)(2,1)S(1)}, bf16[8,128]{1,0:T(8,128)(2,1)S(1)}, u32[]{:S(2)}, u32[]{:S(2)}) collective-permute-start(bf16[8,128]{1,0:T(8,128)(2,1)S(1)} %get-tuple-element.13), channel_id=1, source_target_pairs={{0,16},{16,32},{32,48},{48,64},{64,80},{80,96},{96,112},{112,128},... | collective-permute-start | bytes 6152 | tf_op jit(solution)/shard_map/ppermute | solution.py:12
  7.5 1.1 %fusion.26 = (bf16[32,3,1,8,128]{4,3,2,1,0:T(8,128)(2,1)S(1)}, bf16[32,3,1,8,128]{4,3,2,1,0:T(8,128)(2,1)S(1)}) fusion(bf16[32,3,16,8,128]{4,3,2,1,0:T(8,128)(2,1)} %defl_ref.1), kind=kLoop, calls=%fused_computation.37 | loop fusion | bytes 786432 | tf_op jit(solution)/shard_map/slice | solution.py:127
  8.7 10.1 %collective-permute-start.2 = (bf16[32,3,8,128]{3,0,2,1:T(8,128)(2,1)S(1)}, bf16[32,3,8,128]{3,0,2,1:T(8,128)(2,1)S(1)}, u32[]{:S(2)}, u32[]{:S(2)}) collective-permute-start(bf16[32,3,8,128]{3,0,2,1:T(8,128)(2,1)S(1)} %bitcast_multiply_fusion), channel_id=1, source_target_pairs={{16,0},{32,16},{48,32},{64,48},{80,64},{96,80},{112,96},{128,112},... | collective-permute-start | bytes 589832 | tf_op jit(solution)/shard_map/ppermute | solution.py:12
  18.7 5.5 %shard_map.37 = (bf16[3,16,32,1024]{3,2,1,0:T(8,128)(2,1)}, bf16[2,3,16,32,128]{4,3,2,1,0:T(8,128)(2,1)}) custom-call(s32[1]{0:T(128)} %copy.36.depth_ref, bf16[32,3,16,8,128]{4,3,2,1,0:T(8,128)(2,1)} %defl_ref.1), custom_call_target="tpu_custom_call" | custom-call | bytes 7864320 | tf_op jit(solution)/shard_map/pallas_call | solution.py:82
  24.2 0.0 copy-start
  24.2 1.1 %slice_bitcast_fusion = bf16[3,16,32,128]{3,2,1,0:T(8,128)(2,1)S(1)} fusion(bf16[2,3,16,32,128]{4,3,2,1,0:T(8,128)(2,1)} %get-tuple-element.8), kind=kLoop, calls=%fused_computation.19 | loop fusion | bytes 786432 | tf_op jit(solution)/shard_map/squeeze | solution.py:124
  25.3 2.4 %collective-permute-start.3 = (bf16[3,16,32,128]{3,2,1,0:T(8,128)(2,1)S(1)}, bf16[3,16,32,128]{3,2,1,0:T(8,128)(2,1)S(1)}, u32[]{:S(2)}, u32[]{:S(2)}) collective-permute-start(bf16[3,16,32,128]{3,2,1,0:T(8,128)(2,1)S(1)} %slice_bitcast_fusion), channel_id=1, source_target_pairs={{1,0},{2,1},{3,2},{4,3},{5,4},{6,5},{7,6},{8,7},{9,8},{10,9},{11,1... | collective-permute-start | bytes 1179656 | tf_op jit(solution)/shard_map/ppermute | solution.py:12
  27.7 6.1 %shard_map.38 = f32[32,32]{1,0:T(8,128)} custom-call(bf16[3,16,32,1024]{3,2,1,0:T(8,128)(2,1)} %get-tuple-element.7.live_ref, bf16[4,16,8,128]{3,2,1,0:T(8,128)(2,1)} %coeff_ref.1), custom_call_target="tpu_custom_call" | custom-call | flops 402653184 | bytes 3276800 | tf_op jit(solution)/shard_map/pallas_call | solution.py:96
  33.8 0.0 collective-permute-done
  33.8 0.0 collective-permute-done.1
  33.8 0.0 copy-done
  33.8 0.2 convolution_bitcast_fusion.1
  34.1 0.9 %fusion.3 = f32[32,32]{1,0:T(8,128)S(1)} fusion(f32[32,32]{1,0:T(8,128)S(1)} %convolution_bitcast_fusion.1, f32[32,32]{1,0:T(8,128)} %shard_map.38, f32[8,128]{1,0:T(8,128)S(1)} %convert_element_type.53, bf16[32,3,1,8,128]{4,3,2,1,0:T(8,128)(2,1)S(1)} %get-tuple-element.12, bf16[128]{0:T(256)(128)(2,1)S(1)} %compare_convert_fusion), kind=kOutput, calls=%fused_computation.7 | convolution fusion | flops 6785024 | bytes 213248 | tf_op jit(solution)/shard_map/dot_general | solution.py:17
  35.0 0.0 collective-permute-done.2
  35.0 0.2 fusion.1
  35.2 0.0 collective-permute-done.3
  35.2 0.2 fusion
  35.5 0.1 maximum_multiply_fusion
  35.6 21.0 %all_to_all.5 = f32[1,16,32,96]{3,2,0,1:T(8,128)S(1)} all-to-all(f32[1,16,32,96]{3,2,0,1:T(8,128)S(1)} %broadcast_in_dim.2), channel_id=1, replica_groups=mesh['sub'=32,'grp'=16] {'grp'}, dimensions={1} | all-to-all | bytes 393216 | tf_op jit(solution)/shard_map/all_to_all | solution.py:135
  56.6 0.7 %copy.37 = f32[1,16,32,96]{3,2,1,0:T(8,128)} copy(f32[1,16,32,96]{3,2,1,0:T(8,128)S(1)} %bitcast.63) | data formatting | bytes 393216
  (6 shorter events, 0.1 us)
Async XLA Ops:
  0.8 33.0 %collective-permute-start.1 = (bf16[16,128]{1,0:T(8,128)(2,1)S(1)}, bf16[16,128]{1,0:T(8,128)(2,1)S(1)}, u32[]{:S(2)}, u32[]{:S(2)}) collective-permute-start(bf16[16,128]{1,0:T(8,128)(2,1)S(1)} %get-tuple-element.10), channel_id=1, source_target_pairs={{0,1},{1,2},{2,3},{3,4},{4,5},{5,6},{6,7},{7,8},{8,9},{9,10},{10,1... | collective-permute-start | bytes 12296 | tf_op jit(solution)/shard_map/ppermute | solution.py:12
  5.0 28.8 %collective-permute-start = (bf16[8,128]{1,0:T(8,128)(2,1)S(1)}, bf16[8,128]{1,0:T(8,128)(2,1)S(1)}, u32[]{:S(2)}, u32[]{:S(2)}) collective-permute-start(bf16[8,128]{1,0:T(8,128)(2,1)S(1)} %get-tuple-element.13), channel_id=1, source_target_pairs={{0,16},{16,32},{32,48},{48,64},{64,80},{80,96},{96,112},{112,128},... | collective-permute-start | bytes 6152 | tf_op jit(solution)/shard_map/ppermute | solution.py:12
  8.7 26.4 %collective-permute-start.2 = (bf16[32,3,8,128]{3,0,2,1:T(8,128)(2,1)S(1)}, bf16[32,3,8,128]{3,0,2,1:T(8,128)(2,1)S(1)}, u32[]{:S(2)}, u32[]{:S(2)}) collective-permute-start(bf16[32,3,8,128]{3,0,2,1:T(8,128)(2,1)S(1)} %bitcast_multiply_fusion), channel_id=1, source_target_pairs={{16,0},{32,16},{48,32},{64,48},{80,64},{96,80},{112,96},{128,112},... | collective-permute-start | bytes 589832 | tf_op jit(solution)/shard_map/ppermute | solution.py:12
  24.2 9.6 %copy-start = (bf16[2,3,16,32,128]{4,3,2,1,0:T(8,128)(2,1)S(1)}, bf16[2,3,16,32,128]{4,3,2,1,0:T(8,128)(2,1)}, u32[]{:S(2)}) copy-start(bf16[2,3,16,32,128]{4,3,2,1,0:T(8,128)(2,1)} %get-tuple-element.8) | copy-start | bytes 2359300
  25.3 9.9 %collective-permute-start.3 = (bf16[3,16,32,128]{3,2,1,0:T(8,128)(2,1)S(1)}, bf16[3,16,32,128]{3,2,1,0:T(8,128)(2,1)S(1)}, u32[]{:S(2)}, u32[]{:S(2)}) collective-permute-start(bf16[3,16,32,128]{3,2,1,0:T(8,128)(2,1)S(1)} %slice_bitcast_fusion), channel_id=1, source_target_pairs={{1,0},{2,1},{3,2},{4,3},{5,4},{6,5},{7,6},{8,7},{9,8},{10,9},{11,1... | collective-permute-start | bytes 1179656 | tf_op jit(solution)/shard_map/ppermute | solution.py:12

commit v10 on v9

--- a/solution.py
+++ b/solution.py
@@ -25,7 +25,7 @@
     return (weight.astype(jnp.float32) * values.astype(jnp.float32)).astype(jnp.bfloat16)
 
 
-def turn_kernel(depth_ref, defl_ref, live_ref, edge_ref):
+def turn_kernel(depth_ref, defl_ref, live_ref, low_ref, high_ref, first_ref):
     count, comps, rows, cols, depth = defl_ref.shape
     lane = lax.broadcasted_iota(jnp.int32, (count, cols, depth), 2)
     live_mask = (lane < depth_ref[0]).astype(jnp.bfloat16)
@@ -36,8 +36,14 @@
             turned = pltpu.einshape("kyz->ykz", tiles).astype(jnp.bfloat16)
             for col in range(cols):
                 live_ref[comp, row, :, pl.ds(col * depth, depth)] = turned[col]
-            edge_ref[0, comp, row] = turned[0]
-            edge_ref[1, comp, row] = turned[cols - 1]
+            low_ref[comp, row] = turned[0]
+            high_ref[comp, row] = turned[cols - 1]
+
+            @pl.when(row == 0)
+            def _():
+                for col in range(cols):
+                    first_ref[comp, :, pl.ds(col * depth, depth)] = turned[col]
+
         return carry
 
     lax.fori_loop(0, rows, body, 0, unroll=4)
@@ -83,10 +89,12 @@
         turn_kernel,
         out_shape=(
             jax.ShapeDtypeStruct((comps, rows, count, cols * depth), jnp.bfloat16),
-            jax.ShapeDtypeStruct((2, comps, rows, count, depth), jnp.bfloat16),
+            jax.ShapeDtypeStruct((comps, rows, count, depth), jnp.bfloat16),
+            jax.ShapeDtypeStruct((comps, rows, count, depth), jnp.bfloat16),
+            jax.ShapeDtypeStruct((comps, count, cols * depth), jnp.bfloat16),
         ),
         in_specs=[pl.BlockSpec(memory_space=pltpu.SMEM), pl.BlockSpec(memory_space=pltpu.VMEM)],
-        out_specs=(pl.BlockSpec(memory_space=pltpu.VMEM), pl.BlockSpec(memory_space=pltpu.VMEM)),
+        out_specs=(pl.BlockSpec(memory_space=pltpu.VMEM),) * 4,
         cost_estimate=pl.CostEstimate(flops=0, bytes_accessed=deflation.size * 5, transcendentals=0),
     )(depths, deflation)
 
@@ -110,24 +118,28 @@
     return jnp.einsum("cxkz,cxlz->kl", left_side, right_side, preferred_element_type=jnp.float32)
 
 
+def layer_gram(left_side, right_side):
+    return jnp.einsum("ckj,clj->kl", left_side, right_side, preferred_element_type=jnp.float32)
+
+
 def shards(deflation, stiffness, depths):
     cell_count = deflation.shape[2] * deflation.shape[3] * deflation.shape[4]
     normalizer = 1.0 / (24.0 * cell_count)
-    live_mask = (lax.iota(jnp.int32, deflation.shape[4]) < depths[0]).astype(jnp.bfloat16)
-    bottom_x = deflation[:, :, 0] * live_mask
-    weight_top_x = stiffness[1, -1]
+    live_t, bottom_y, top_y, bottom_x = turned_field(deflation, depths)
+    weight_top_x = stiffness[1, -1].reshape(-1)
     weight_top_y = stiffness[2, :, -1]
+    live_t, bottom_y, bottom_x, weight_top_x, weight_top_y = lax.optimization_barrier(
+        (live_t, bottom_y, bottom_x, weight_top_x, weight_top_y)
+    )
+    next_y = from_behind(bottom_y, "grp", -1)
     next_x = from_behind(bottom_x, "sub", -1)
     weight_low_x = from_behind(weight_top_x, "sub", 1)
     weight_low_y = from_behind(weight_top_y, "grp", 1)
-    live_t, edges = turned_field(deflation, depths)
-    bottom_y, top_y = edges[0], edges[1]
-    next_y = from_behind(bottom_y, "grp", -1)
     diagonal_block = local_terms(live_t, stiffness)
-    top_x = deflation[:, :, -1] * live_mask
-    coupling_x = -gram_of(weighted(weight_top_x, top_x), next_x)
+    top_x = live_t[:, -1]
+    coupling_x = -layer_gram(weighted(weight_top_x, top_x), next_x)
     coupling_y = -face_gram(weighted(weight_top_y[None, :, None], top_y), next_y)
-    diagonal_block = diagonal_block + gram_of(bottom_x, weighted(weight_low_x, bottom_x))
+    diagonal_block = diagonal_block + layer_gram(bottom_x, weighted(weight_low_x, bottom_x))
     diagonal_block = diagonal_block + face_gram(bottom_y, weighted(weight_low_y[None, :, None], bottom_y))
     row_block = normalizer * jnp.concatenate([diagonal_block, coupling_x, coupling_y], axis=1)
     groups = lax.axis_size("grp")

time: 57.7 us -> 57 us (0.988)
  local copies, waits for them, and re-layouts: 3.67 us -> 2.2 us
  matrix products: 1.6 us -> 2.53 us
  other arithmetic: 0.82 us -> 0.1 us
    squeeze x1 -> x0, local copies, waits for them, and re-layouts: 1.09 us -> none  [shards(): bottom_y, top_y = (edges[0], edges[1])]
    slice x1 -> x0, local copies, waits for them, and re-layouts: 1.07 us -> none  [shards(): top_x = deflation[:, :, -1] * live_mask]
    dot_general x2, matrix products: 1.11 us -> 2.03 us  [layer_gram(): jnp.einsum('ckj,clj->kl', left_side, right_side, preferred_element_type=j...]
    squeeze x1 -> x0, other arithmetic: 0.69 us -> none  [shards(): weight_top_x = stiffness[1, -1]]
    another operation x0 -> x1, local copies, waits for them, and re-layouts: none -> 0.69 us  [shards(): weight_top_x = stiffness[1, -1].reshape(-1)]
  transfers between devices with their start and end apart: 4 -> 4, of which waited for: 0 -> 0; matrix products, arithmetic and copies ran while one was open for 7% -> 4% of each run, Pallas kernels for 20% -> 11%
where the time goes in v10:
time: 57 us; the launch traced here: 56.6 us
  blocking collectives  21 us (37%)
  starting transfers between devices  18 us (32%)
  Pallas kernels  12 us (21%)
  matrix products  2.53 us (4%)
  local copies, waits for them, and re-layouts  2.2 us (4%)
  between operations  0.77 us (1%)
    all_to_all x1, blocking collectives, shards(): return lax.all_to_all(copies, 'grp', 1, 1, tiled=True)  21 us
    ppermute x4, starting transfers between devices, from_behind(): return lax.ppermute(x, axis, pairs)  18 us
    pallas_call x1, Pallas kernels, local_terms(): pl.pallas_call(local_kernel, out_shape=jax.ShapeDtypeStruct((count, count...  6.1 us
    pallas_call x1, Pallas kernels, turned_field(): pl.pallas_call(turn_kernel, out_shape=(jax.ShapeDtypeStruct((comps, rows,...  5.9 us
    dot_general x2, matrix products, layer_gram(): jnp.einsum('ckj,clj->kl', left_side, right_side, preferred_element_type=j...  2.03 us
  transfers between devices with their start and end apart: 4, of which 0 were waited for; matrix products, arithmetic and copies ran while one was open for 4% of the time, Pallas kernels for 11%

profile of v10, /device:TPU:10, one launch (start us, length us, event | category | flops | bytes accessed | tf_op | source)
XLA Modules:
  0.0 56.6 jit_solution(7526489913246405876)
XLA Ops:
  0.0 0.8 %slice.10 = bf16[1,16,1,128]{3,2,1,0:T(2,128)(2,1)S(1)} slice(bf16[4,16,8,128]{3,2,1,0:T(8,128)(2,1)} %coeff_ref.1), slice={[2:3], [0:16], [7:8], [0:128]} | slice | bytes 8192 | tf_op jit(solution)/shard_map/slice | solution.py:130
  0.8 0.7 %slice_bitcast_fusion = bf16[1024]{0:T(1024)(128)(2,1)S(1)} fusion(bf16[4,16,8,128]{3,2,1,0:T(8,128)(2,1)} %coeff_ref.1), kind=kLoop, calls=%fused_computation.21 | loop fusion | bytes 4096 | tf_op jit(solution)/shard_map/reshape;squeeze | solution.py:129
  2.1 5.9 %shard_map.37 = (bf16[3,16,32,1024]{3,2,1,0:T(8,128)(2,1)}, bf16[3,16,32,128]{3,2,1,0:T(8,128)(2,1)}, bf16[3,16,32,128]{3,2,1,0:T(8,128)(2,1)}, bf16[3,32,1024]{2,1,0:T(8,128)(2,1)}) custom-call(s32[1]{0:T(128)S(6)} %copy.13.depth_ref, bf16[32,3,16,8,128]{4,3,2,1,0:T(8,128)(2,1)} %defl_ref.1), custom_call_target="tpu_custom_call" | custom-call | bytes 7864320 | tf_op jit(solution)/shard_map/pallas_call | solution.py:88
  8.0 0.0 copy-start.2
  8.0 0.0 copy-start
  8.0 0.0 copy-start.1
  8.0 3.6 %collective-permute-start.1 = (bf16[16,128]{1,0:T(8,128)(2,1)S(1)}, bf16[16,128]{1,0:T(8,128)(2,1)S(1)}, u32[]{:S(2)}, u32[]{:S(2)}) collective-permute-start(bf16[16,128]{1,0:T(8,128)(2,1)S(1)} %bitcast.37), channel_id=1, source_target_pairs={{0,1},{1,2},{2,3},{3,4},{4,5},{5,6},{6,7},{7,8},{8,9},{9,10},{10,1... | collective-permute-start | bytes 12296 | tf_op jit(solution)/shard_map/ppermute | solution.py:12
  11.7 1.9 %collective-permute-start = (bf16[1024]{0:T(1024)(128)(2,1)S(1)}, bf16[1024]{0:T(1024)(128)(2,1)S(1)}, u32[]{:S(2)}, u32[]{:S(2)}) collective-permute-start(bf16[1024]{0:T(1024)(128)(2,1)S(1)} %slice_bitcast_fusion), channel_id=1, source_target_pairs={{0,16},{16,32},{32,48},{48,64},{64,80},{80,96},{96,112},{112,128},... | collective-permute-start | bytes 6152 | tf_op jit(solution)/shard_map/ppermute | solution.py:12
  13.6 10.1 %collective-permute-start.2 = (bf16[3,32,1024]{2,1,0:T(8,128)(2,1)}, bf16[3,32,1024]{2,1,0:T(8,128)(2,1)S(1)}, u32[]{:S(2)}, u32[]{:S(2)}) collective-permute-start(bf16[3,32,1024]{2,1,0:T(8,128)(2,1)} %get-tuple-element.18), channel_id=1, source_target_pairs={{16,0},{32,16},{48,32},{64,48},{80,64},{96,80},{112,96},{128,112},... | collective-permute-start | bytes 589832 | tf_op jit(solution)/shard_map/ppermute | solution.py:12
  23.7 2.4 %collective-permute-start.3 = (bf16[3,16,32,128]{3,2,1,0:T(8,128)(2,1)}, bf16[3,16,32,128]{3,2,1,0:T(8,128)(2,1)S(1)}, u32[]{:S(2)}, u32[]{:S(2)}) collective-permute-start(bf16[3,16,32,128]{3,2,1,0:T(8,128)(2,1)} %get-tuple-element.20), channel_id=1, source_target_pairs={{1,0},{2,1},{3,2},{4,3},{5,4},{6,5},{7,6},{8,7},{9,8},{10,9},{11,1... | collective-permute-start | bytes 1179656 | tf_op jit(solution)/shard_map/ppermute | solution.py:12
  26.0 6.1 %shard_map.38 = f32[32,32]{1,0:T(8,128)} custom-call(bf16[3,16,32,1024]{3,2,1,0:T(8,128)(2,1)} %get-tuple-element.17.live_ref, bf16[4,16,8,128]{3,2,1,0:T(8,128)(2,1)} %coeff_ref.1), custom_call_target="tpu_custom_call" | custom-call | flops 402653184 | bytes 3276800 | tf_op jit(solution)/shard_map/pallas_call | solution.py:104
  32.1 0.0 collective-permute-done
  32.1 0.0 collective-permute-done.1
  32.2 0.0 copy-done.2
  32.2 0.2 convolution_bitcast_fusion.1
  32.4 0.0 copy-done
  32.4 0.9 %fusion.3 = f32[32,32]{1,0:T(8,128)S(1)} fusion(f32[32,32]{1,0:T(8,128)S(1)} %convolution_bitcast_fusion.1, f32[32,32]{1,0:T(8,128)} %shard_map.38, bf16[3,32,1024]{2,1,0:T(8,128)(2,1)S(1)} %copy-done, f32[1024]{0:T(1024)S(1)} %convert_element_type.41), kind=kOutput, calls=%fused_computation.7 | convolution fusion | flops 6588416 | bytes 212992 | tf_op jit(solution)/shard_map/ckj,clj->kl/dot_general | solution.py:122
  33.4 0.0 collective-permute-done.2
  33.4 1.1 %fusion.1 = f32[32,32]{1,0:T(8,128)S(1)} fusion(bf16[3,32,1024]{2,1,0:T(8,128)(2,1)S(1)} %collective-permute-done.2, bf16[3,16,32,1024]{3,2,1,0:T(8,128)(2,1)} %get-tuple-element.17.live_ref, f32[1024]{0:T(1024)S(1)} %convert_element_type.47), kind=kOutput, calls=%fused_computation.4 | convolution fusion | flops 6587392 | bytes 401408 | tf_op jit(solution)/shard_map/ckj,clj->kl/dot_general | solution.py:122
  34.5 0.0 collective-permute-done.3
  34.5 0.0 copy-done.1
  34.5 0.2 fusion
  34.8 0.1 maximum_multiply_fusion
  34.9 21.0 %all_to_all.5 = f32[1,16,32,96]{3,2,0,1:T(8,128)S(1)} all-to-all(f32[1,16,32,96]{3,2,0,1:T(8,128)S(1)} %broadcast_in_dim.2), channel_id=1, replica_groups=mesh['sub'=32,'grp'=16] {'grp'}, dimensions={1} | all-to-all | bytes 393216 | tf_op jit(solution)/shard_map/all_to_all | solution.py:147
  55.9 0.7 %copy.14 = f32[1,16,32,96]{3,2,1,0:T(8,128)} copy(f32[1,16,32,96]{3,2,1,0:T(8,128)S(1)} %bitcast.36) | data formatting | bytes 393216
  (6 shorter events, 0.0 us)
Async XLA Ops:
  8.0 24.1 %copy-start.2 = (bf16[3,16,32,128]{3,2,1,0:T(8,128)(2,1)S(1)}, bf16[3,16,32,128]{3,2,1,0:T(8,128)(2,1)}, u32[]{:S(2)}) copy-start(bf16[3,16,32,128]{3,2,1,0:T(8,128)(2,1)} %get-tuple-element.20) | copy-start | bytes 1179652
  8.0 24.4 %copy-start = (bf16[3,32,1024]{2,1,0:T(8,128)(2,1)S(1)}, bf16[3,32,1024]{2,1,0:T(8,128)(2,1)}, u32[]{:S(2)}) copy-start(bf16[3,32,1024]{2,1,0:T(8,128)(2,1)} %get-tuple-element.18) | copy-start | bytes 589828
  8.0 26.5 %copy-start.1 = (bf16[3,16,32,128]{3,2,1,0:T(8,128)(2,1)S(1)}, bf16[3,16,32,128]{3,2,1,0:T(8,128)(2,1)}, u32[]{:S(2)}) copy-start(bf16[3,16,32,128]{3,2,1,0:T(8,128)(2,1)} %get-tuple-element.22) | copy-start | bytes 1179652
  8.0 24.1 %collective-permute-start.1 = (bf16[16,128]{1,0:T(8,128)(2,1)S(1)}, bf16[16,128]{1,0:T(8,128)(2,1)S(1)}, u32[]{:S(2)}, u32[]{:S(2)}) collective-permute-start(bf16[16,128]{1,0:T(8,128)(2,1)S(1)} %bitcast.37), channel_id=1, source_target_pairs={{0,1},{1,2},{2,3},{3,4},{4,5},{5,6},{6,7},{7,8},{8,9},{9,10},{10,1... | collective-permute-start | bytes 12296 | tf_op jit(solution)/shard_map/ppermute | solution.py:12
  11.7 20.5 %collective-permute-start = (bf16[1024]{0:T(1024)(128)(2,1)S(1)}, bf16[1024]{0:T(1024)(128)(2,1)S(1)}, u32[]{:S(2)}, u32[]{:S(2)}) collective-permute-start(bf16[1024]{0:T(1024)(128)(2,1)S(1)} %slice_bitcast_fusion), channel_id=1, source_target_pairs={{0,16},{16,32},{32,48},{48,64},{64,80},{80,96},{96,112},{112,128},... | collective-permute-start | bytes 6152 | tf_op jit(solution)/shard_map/ppermute | solution.py:12
  13.6 19.8 %collective-permute-start.2 = (bf16[3,32,1024]{2,1,0:T(8,128)(2,1)}, bf16[3,32,1024]{2,1,0:T(8,128)(2,1)S(1)}, u32[]{:S(2)}, u32[]{:S(2)}) collective-permute-start(bf16[3,32,1024]{2,1,0:T(8,128)(2,1)} %get-tuple-element.18), channel_id=1, source_target_pairs={{16,0},{32,16},{48,32},{64,48},{80,64},{96,80},{112,96},{128,112},... | collective-permute-start | bytes 589832 | tf_op jit(solution)/shard_map/ppermute | solution.py:12
  23.7 10.8 %collective-permute-start.3 = (bf16[3,16,32,128]{3,2,1,0:T(8,128)(2,1)}, bf16[3,16,32,128]{3,2,1,0:T(8,128)(2,1)S(1)}, u32[]{:S(2)}, u32[]{:S(2)}) collective-permute-start(bf16[3,16,32,128]{3,2,1,0:T(8,128)(2,1)} %get-tuple-element.20), channel_id=1, source_target_pairs={{1,0},{2,1},{3,2},{4,3},{5,4},{6,5},{7,6},{8,7},{9,8},{10,9},{11,1... | collective-permute-start | bytes 1179656 | tf_op jit(solution)/shard_map/ppermute | solution.py:12

commit v11 on v10

--- a/solution.py
+++ b/solution.py
@@ -128,9 +128,7 @@
     live_t, bottom_y, top_y, bottom_x = turned_field(deflation, depths)
     weight_top_x = stiffness[1, -1].reshape(-1)
     weight_top_y = stiffness[2, :, -1]
-    live_t, bottom_y, bottom_x, weight_top_x, weight_top_y = lax.optimization_barrier(
-        (live_t, bottom_y, bottom_x, weight_top_x, weight_top_y)
-    )
+    live_t, bottom_y, bottom_x = lax.optimization_barrier((live_t, bottom_y, bottom_x))
     next_y = from_behind(bottom_y, "grp", -1)
     next_x = from_behind(bottom_x, "sub", -1)
     weight_low_x = from_behind(weight_top_x, "sub", 1)
@@ -138,9 +136,9 @@
     diagonal_block = local_terms(live_t, stiffness)
     top_x = live_t[:, -1]
     coupling_x = -layer_gram(weighted(weight_top_x, top_x), next_x)
-    coupling_y = -face_gram(weighted(weight_top_y[None, :, None], top_y), next_y)
     diagonal_block = diagonal_block + layer_gram(bottom_x, weighted(weight_low_x, bottom_x))
     diagonal_block = diagonal_block + face_gram(bottom_y, weighted(weight_low_y[None, :, None], bottom_y))
+    coupling_y = -face_gram(weighted(weight_top_y[None, :, None], top_y), next_y)
     row_block = normalizer * jnp.concatenate([diagonal_block, coupling_x, coupling_y], axis=1)
     groups = lax.axis_size("grp")
     copies = jnp.broadcast_to(row_block[None, None], (1, groups) + row_block.shape)

time: 57 us -> 57 us (level)
  local copies, waits for them, and re-layouts: 2.2 us -> 1.52 us
  other arithmetic: 0.1 us -> 0.78 us
    another operation x1 -> x0, local copies, waits for them, and re-layouts: 0.69 us -> none  [shards(): weight_top_x = stiffness[1, -1].reshape(-1)]
    another operation x0 -> x1, other arithmetic: none -> 0.68 us  [shards(): weight_top_x = stiffness[1, -1].reshape(-1)]
  transfers between devices with their start and end apart: 4 -> 4, of which waited for: 0 -> 0; matrix products, arithmetic and copies ran while one was open for 4% -> 5% of each run, Pallas kernels for 11% -> 21%
where the time goes in v11:
time: 57 us; the launch traced here: 56.5 us
  blocking collectives  21 us (37%)
  starting transfers between devices  18 us (32%)
  Pallas kernels  12 us (21%)
  matrix products  2.53 us (4%)
  local copies, waits for them, and re-layouts  1.52 us (3%)
  other arithmetic  0.78 us (1%)
  between operations  0.75 us (1%)
    all_to_all x1, blocking collectives, shards(): return lax.all_to_all(copies, 'grp', 1, 1, tiled=True)  21 us
    ppermute x4, starting transfers between devices, from_behind(): return lax.ppermute(x, axis, pairs)  18 us
    pallas_call x1, Pallas kernels, local_terms(): pl.pallas_call(local_kernel, out_shape=jax.ShapeDtypeStruct((count, count...  6.1 us
    pallas_call x1, Pallas kernels, turned_field(): pl.pallas_call(turn_kernel, out_shape=(jax.ShapeDtypeStruct((comps, rows,...  5.9 us
    dot_general x2, matrix products, layer_gram(): jnp.einsum('ckj,clj->kl', left_side, right_side, preferred_element_type=j...  2.04 us
  transfers between devices with their start and end apart: 4, of which 0 were waited for; matrix products, arithmetic and copies ran while one was open for 5% of the time, Pallas kernels for 21%

profile of v11, /device:TPU:10, one launch (start us, length us, event | category | flops | bytes accessed | tf_op | source)
XLA Modules:
  0.0 56.5 jit_solution(11470379784938229746)
XLA Ops:
  0.0 0.7 %slice_bitcast_fusion = (bf16[1024]{0:T(1024)(128)(2,1)S(1)}, f32[1024]{0:T(1024)S(1)}) fusion(bf16[4,16,8,128]{3,2,1,0:T(8,128)(2,1)} %coeff_ref.1), kind=kLoop, calls=%fused_computation.21 | loop fusion | flops 1024 | bytes 8192 | tf_op jit(solution)/shard_map/reshape;squeeze | solution.py:129
  0.7 1.9 %collective-permute-start = (bf16[1024]{0:T(1024)(128)(2,1)S(1)}, bf16[1024]{0:T(1024)(128)(2,1)S(1)}, u32[]{:S(2)}, u32[]{:S(2)}) collective-permute-start(bf16[1024]{0:T(1024)(128)(2,1)S(1)} %get-tuple-element.21), channel_id=1, source_target_pairs={{0,16},{16,32},{32,48},{48,64},{64,80},{80,96},{96,112},{112,128},... | collective-permute-start | bytes 6152 | tf_op jit(solution)/shard_map/ppermute | solution.py:12
  2.6 0.8 %slice.10 = bf16[1,16,1,128]{3,2,1,0:T(2,128)(2,1)S(1)} slice(bf16[4,16,8,128]{3,2,1,0:T(8,128)(2,1)} %coeff_ref.1), slice={[2:3], [0:16], [7:8], [0:128]} | slice | bytes 8192 | tf_op jit(solution)/shard_map/slice | solution.py:130
  3.4 3.5 %collective-permute-start.1 = (bf16[16,128]{1,0:T(8,128)(2,1)S(1)}, bf16[16,128]{1,0:T(8,128)(2,1)S(1)}, u32[]{:S(2)}, u32[]{:S(2)}) collective-permute-start(bf16[16,128]{1,0:T(8,128)(2,1)S(1)} %get-tuple-element.20), channel_id=1, source_target_pairs={{0,1},{1,2},{2,3},{3,4},{4,5},{5,6},{6,7},{7,8},{8,9},{9,10},{10,1... | collective-permute-start | bytes 12296 | tf_op jit(solution)/shard_map/ppermute | solution.py:12
  7.5 5.9 %shard_map.37 = (bf16[3,16,32,1024]{3,2,1,0:T(8,128)(2,1)}, bf16[3,16,32,128]{3,2,1,0:T(8,128)(2,1)}, bf16[3,16,32,128]{3,2,1,0:T(8,128)(2,1)}, bf16[3,32,1024]{2,1,0:T(8,128)(2,1)}) custom-call(s32[1]{0:T(128)S(6)} %copy.13.depth_ref, bf16[32,3,16,8,128]{4,3,2,1,0:T(8,128)(2,1)} %defl_ref.1), custom_call_target="tpu_custom_call" | custom-call | bytes 7864320 | tf_op jit(solution)/shard_map/pallas_call | solution.py:88
  13.4 0.0 copy-start.2
  13.4 0.0 copy-start
  13.4 0.0 copy-start.1
  13.4 10.2 %collective-permute-start.2 = (bf16[3,32,1024]{2,1,0:T(8,128)(2,1)}, bf16[3,32,1024]{2,1,0:T(8,128)(2,1)S(1)}, u32[]{:S(2)}, u32[]{:S(2)}) collective-permute-start(bf16[3,32,1024]{2,1,0:T(8,128)(2,1)} %get-tuple-element.16), channel_id=1, source_target_pairs={{16,0},{32,16},{48,32},{64,48},{80,64},{96,80},{112,96},{128,112},... | collective-permute-start | bytes 589832 | tf_op jit(solution)/shard_map/ppermute | solution.py:12
  23.7 2.4 %collective-permute-start.3 = (bf16[3,16,32,128]{3,2,1,0:T(8,128)(2,1)}, bf16[3,16,32,128]{3,2,1,0:T(8,128)(2,1)S(1)}, u32[]{:S(2)}, u32[]{:S(2)}) collective-permute-start(bf16[3,16,32,128]{3,2,1,0:T(8,128)(2,1)} %get-tuple-element.17), channel_id=1, source_target_pairs={{1,0},{2,1},{3,2},{4,3},{5,4},{6,5},{7,6},{8,7},{9,8},{10,9},{11,1... | collective-permute-start | bytes 1179656 | tf_op jit(solution)/shard_map/ppermute | solution.py:12
  26.0 6.1 %shard_map.38 = f32[32,32]{1,0:T(8,128)} custom-call(bf16[3,16,32,1024]{3,2,1,0:T(8,128)(2,1)} %get-tuple-element.15.live_ref, bf16[4,16,8,128]{3,2,1,0:T(8,128)(2,1)} %coeff_ref.1), custom_call_target="tpu_custom_call" | custom-call | flops 402653184 | bytes 3276800 | tf_op jit(solution)/shard_map/pallas_call | solution.py:104
  32.1 0.0 collective-permute-done
  32.1 0.0 collective-permute-done.1
  32.1 0.0 copy-done.2
  32.1 0.2 convolution_bitcast_fusion.1
  32.4 0.0 copy-done
  32.4 0.9 %fusion.3 = f32[32,32]{1,0:T(8,128)S(1)} fusion(f32[32,32]{1,0:T(8,128)S(1)} %convolution_bitcast_fusion.1, f32[32,32]{1,0:T(8,128)} %shard_map.38, bf16[3,32,1024]{2,1,0:T(8,128)(2,1)S(1)} %copy-done, f32[1024]{0:T(1024)S(1)} %convert_element_type.42), kind=kOutput, calls=%fused_computation.7 | convolution fusion | flops 6588416 | bytes 212992 | tf_op jit(solution)/shard_map/ckj,clj->kl/dot_general | solution.py:122
  33.3 0.0 collective-permute-done.2
  33.3 1.1 %fusion.1 = f32[32,32]{1,0:T(8,128)S(1)} fusion(bf16[3,32,1024]{2,1,0:T(8,128)(2,1)S(1)} %collective-permute-done.2, bf16[3,16,32,1024]{3,2,1,0:T(8,128)(2,1)} %get-tuple-element.15.live_ref, f32[1024]{0:T(1024)S(1)} %get-tuple-element.22), kind=kOutput, calls=%fused_computation.4 | convolution fusion | flops 6587392 | bytes 401408 | tf_op jit(solution)/shard_map/ckj,clj->kl/dot_general | solution.py:122
  34.5 0.0 collective-permute-done.3
  34.5 0.0 copy-done.1
  34.5 0.2 fusion
  34.7 0.1 maximum_multiply_fusion
  34.9 21.0 %all_to_all.5 = f32[1,16,32,96]{3,2,0,1:T(8,128)S(1)} all-to-all(f32[1,16,32,96]{3,2,0,1:T(8,128)S(1)} %broadcast_in_dim.2), channel_id=1, replica_groups=mesh['sub'=32,'grp'=16] {'grp'}, dimensions={1} | all-to-all | bytes 393216 | tf_op jit(solution)/shard_map/all_to_all | solution.py:145
  55.8 0.7 %copy.14 = f32[1,16,32,96]{3,2,1,0:T(8,128)} copy(f32[1,16,32,96]{3,2,1,0:T(8,128)S(1)} %bitcast.38) | data formatting | bytes 393216
  (4 shorter events, 0.0 us)
Async XLA Ops:
  0.7 31.4 %collective-permute-start = (bf16[1024]{0:T(1024)(128)(2,1)S(1)}, bf16[1024]{0:T(1024)(128)(2,1)S(1)}, u32[]{:S(2)}, u32[]{:S(2)}) collective-permute-start(bf16[1024]{0:T(1024)(128)(2,1)S(1)} %get-tuple-element.21), channel_id=1, source_target_pairs={{0,16},{16,32},{32,48},{48,64},{64,80},{80,96},{96,112},{112,128},... | collective-permute-start | bytes 6152 | tf_op jit(solution)/shard_map/ppermute | solution.py:12
  3.4 28.7 %collective-permute-start.1 = (bf16[16,128]{1,0:T(8,128)(2,1)S(1)}, bf16[16,128]{1,0:T(8,128)(2,1)S(1)}, u32[]{:S(2)}, u32[]{:S(2)}) collective-permute-start(bf16[16,128]{1,0:T(8,128)(2,1)S(1)} %get-tuple-element.20), channel_id=1, source_target_pairs={{0,1},{1,2},{2,3},{3,4},{4,5},{5,6},{6,7},{7,8},{8,9},{9,10},{10,1... | collective-permute-start | bytes 12296 | tf_op jit(solution)/shard_map/ppermute | solution.py:12
  13.4 18.7 %copy-start.2 = (bf16[3,16,32,128]{3,2,1,0:T(8,128)(2,1)S(1)}, bf16[3,16,32,128]{3,2,1,0:T(8,128)(2,1)}, u32[]{:S(2)}) copy-start(bf16[3,16,32,128]{3,2,1,0:T(8,128)(2,1)} %get-tuple-element.17) | copy-start | bytes 1179652
  13.4 19.0 %copy-start = (bf16[3,32,1024]{2,1,0:T(8,128)(2,1)S(1)}, bf16[3,32,1024]{2,1,0:T(8,128)(2,1)}, u32[]{:S(2)}) copy-start(bf16[3,32,1024]{2,1,0:T(8,128)(2,1)} %get-tuple-element.16) | copy-start | bytes 589828
  13.4 21.0 %copy-start.1 = (bf16[3,16,32,128]{3,2,1,0:T(8,128)(2,1)S(1)}, bf16[3,16,32,128]{3,2,1,0:T(8,128)(2,1)}, u32[]{:S(2)}) copy-start(bf16[3,16,32,128]{3,2,1,0:T(8,128)(2,1)} %get-tuple-element.18) | copy-start | bytes 1179652
  13.4 19.9 %collective-permute-start.2 = (bf16[3,32,1024]{2,1,0:T(8,128)(2,1)}, bf16[3,32,1024]{2,1,0:T(8,128)(2,1)S(1)}, u32[]{:S(2)}, u32[]{:S(2)}) collective-permute-start(bf16[3,32,1024]{2,1,0:T(8,128)(2,1)} %get-tuple-element.16), channel_id=1, source_target_pairs={{16,0},{32,16},{48,32},{64,48},{80,64},{96,80},{112,96},{128,112},... | collective-permute-start | bytes 589832 | tf_op jit(solution)/shard_map/ppermute | solution.py:12
  23.7 10.8 %collective-permute-start.3 = (bf16[3,16,32,128]{3,2,1,0:T(8,128)(2,1)}, bf16[3,16,32,128]{3,2,1,0:T(8,128)(2,1)S(1)}, u32[]{:S(2)}, u32[]{:S(2)}) collective-permute-start(bf16[3,16,32,128]{3,2,1,0:T(8,128)(2,1)} %get-tuple-element.17), channel_id=1, source_target_pairs={{1,0},{2,1},{3,2},{4,3},{5,4},{6,5},{7,6},{8,7},{9,8},{10,9},{11,1... | collective-permute-start | bytes 1179656 | tf_op jit(solution)/shard_map/ppermute | solution.py:12

commit v12 on v10

--- a/solution.py
+++ b/solution.py
@@ -143,8 +143,10 @@
     diagonal_block = diagonal_block + face_gram(bottom_y, weighted(weight_low_y[None, :, None], bottom_y))
     row_block = normalizer * jnp.concatenate([diagonal_block, coupling_x, coupling_y], axis=1)
     groups = lax.axis_size("grp")
-    copies = jnp.broadcast_to(row_block[None, None], (1, groups) + row_block.shape)
-    return lax.all_to_all(copies, "grp", 1, 1, tiled=True)
+    dense = row_block.reshape(-1, 128)
+    copies = jnp.broadcast_to(dense[None, None], (1, groups) + dense.shape)
+    gathered = lax.all_to_all(copies, "grp", 1, 1, tiled=True)
+    return gathered.reshape((1, groups) + row_block.shape)
 
 
 def solution(mesh):

time: 57 us -> 56.7 us (level)
    reshape x0 -> x1, local copies, waits for them, and re-layouts: none -> 0.82 us  [shards(): return gathered.reshape((1, groups) + row_block.shape)]
    unnamed x8 -> x7, local copies, waits for them, and re-layouts: 0.72 us -> 0.01 us
where the time goes in v12:
time: 56.7 us; the launch traced here: 56.2 us
  blocking collectives  20.5 us (36%)
  starting transfers between devices  18 us (32%)
  Pallas kernels  12 us (21%)
  matrix products  2.53 us (4%)
  local copies, waits for them, and re-layouts  2.39 us (4%)
  between operations  0.77 us (1%)
    all_to_all x1, blocking collectives, shards(): gathered = lax.all_to_all(copies, 'grp', 1, 1, tiled=True)  20.5 us
    ppermute x4, starting transfers between devices, from_behind(): return lax.ppermute(x, axis, pairs)  18 us
    pallas_call x1, Pallas kernels, local_terms(): pl.pallas_call(local_kernel, out_shape=jax.ShapeDtypeStruct((count, count...  6.1 us
    pallas_call x1, Pallas kernels, turned_field(): pl.pallas_call(turn_kernel, out_shape=(jax.ShapeDtypeStruct((comps, rows,...  5.9 us
    dot_general x2, matrix products, layer_gram(): jnp.einsum('ckj,clj->kl', left_side, right_side, preferred_element_type=j...  2.03 us
  transfers between devices with their start and end apart: 4, of which 0 were waited for; matrix products, arithmetic and copies ran while one was open for 4% of the time, Pallas kernels for 11%

profile of v12, /device:TPU:10, one launch (start us, length us, event | category | flops | bytes accessed | tf_op | source)
XLA Modules:
  0.0 56.2 jit_solution(10087525211278407826)
XLA Ops:
  0.0 0.8 %slice.10 = bf16[1,16,1,128]{3,2,1,0:T(2,128)(2,1)S(1)} slice(bf16[4,16,8,128]{3,2,1,0:T(8,128)(2,1)} %coeff_ref.1), slice={[2:3], [0:16], [7:8], [0:128]} | slice | bytes 8192 | tf_op jit(solution)/shard_map/slice | solution.py:130
  0.8 0.7 %slice_bitcast_fusion = bf16[1024]{0:T(1024)(128)(2,1)S(1)} fusion(bf16[4,16,8,128]{3,2,1,0:T(8,128)(2,1)} %coeff_ref.1), kind=kLoop, calls=%fused_computation.21 | loop fusion | bytes 4096 | tf_op jit(solution)/shard_map/reshape;squeeze | solution.py:129
  2.1 5.9 %shard_map.37 = (bf16[3,16,32,1024]{3,2,1,0:T(8,128)(2,1)}, bf16[3,16,32,128]{3,2,1,0:T(8,128)(2,1)}, bf16[3,16,32,128]{3,2,1,0:T(8,128)(2,1)}, bf16[3,32,1024]{2,1,0:T(8,128)(2,1)}) custom-call(s32[1]{0:T(128)S(6)} %copy.11.depth_ref, bf16[32,3,16,8,128]{4,3,2,1,0:T(8,128)(2,1)} %defl_ref.1), custom_call_target="tpu_custom_call" | custom-call | bytes 7864320 | tf_op jit(solution)/shard_map/pallas_call | solution.py:88
  8.0 0.0 copy-start.2
  8.0 0.0 copy-start
  8.0 0.0 copy-start.1
  8.0 3.6 %collective-permute-start.1 = (bf16[16,128]{1,0:T(8,128)(2,1)S(1)}, bf16[16,128]{1,0:T(8,128)(2,1)S(1)}, u32[]{:S(2)}, u32[]{:S(2)}) collective-permute-start(bf16[16,128]{1,0:T(8,128)(2,1)S(1)} %bitcast.39), channel_id=1, source_target_pairs={{0,1},{1,2},{2,3},{3,4},{4,5},{5,6},{6,7},{7,8},{8,9},{9,10},{10,1... | collective-permute-start | bytes 12296 | tf_op jit(solution)/shard_map/ppermute | solution.py:12
  11.7 1.9 %collective-permute-start = (bf16[1024]{0:T(1024)(128)(2,1)S(1)}, bf16[1024]{0:T(1024)(128)(2,1)S(1)}, u32[]{:S(2)}, u32[]{:S(2)}) collective-permute-start(bf16[1024]{0:T(1024)(128)(2,1)S(1)} %slice_bitcast_fusion), channel_id=1, source_target_pairs={{0,16},{16,32},{32,48},{48,64},{64,80},{80,96},{96,112},{112,128},... | collective-permute-start | bytes 6152 | tf_op jit(solution)/shard_map/ppermute | solution.py:12
  13.6 10.1 %collective-permute-start.2 = (bf16[3,32,1024]{2,1,0:T(8,128)(2,1)}, bf16[3,32,1024]{2,1,0:T(8,128)(2,1)S(1)}, u32[]{:S(2)}, u32[]{:S(2)}) collective-permute-start(bf16[3,32,1024]{2,1,0:T(8,128)(2,1)} %get-tuple-element.18), channel_id=1, source_target_pairs={{16,0},{32,16},{48,32},{64,48},{80,64},{96,80},{112,96},{128,112},... | collective-permute-start | bytes 589832 | tf_op jit(solution)/shard_map/ppermute | solution.py:12
  23.7 2.4 %collective-permute-start.3 = (bf16[3,16,32,128]{3,2,1,0:T(8,128)(2,1)}, bf16[3,16,32,128]{3,2,1,0:T(8,128)(2,1)S(1)}, u32[]{:S(2)}, u32[]{:S(2)}) collective-permute-start(bf16[3,16,32,128]{3,2,1,0:T(8,128)(2,1)} %get-tuple-element.20), channel_id=1, source_target_pairs={{1,0},{2,1},{3,2},{4,3},{5,4},{6,5},{7,6},{8,7},{9,8},{10,9},{11,1... | collective-permute-start | bytes 1179656 | tf_op jit(solution)/shard_map/ppermute | solution.py:12
  26.0 6.1 %shard_map.38 = f32[32,32]{1,0:T(8,128)} custom-call(bf16[3,16,32,1024]{3,2,1,0:T(8,128)(2,1)} %get-tuple-element.17.live_ref, bf16[4,16,8,128]{3,2,1,0:T(8,128)(2,1)} %coeff_ref.1), custom_call_target="tpu_custom_call" | custom-call | flops 402653184 | bytes 3276800 | tf_op jit(solution)/shard_map/pallas_call | solution.py:104
  32.1 0.0 collective-permute-done
  32.1 0.0 collective-permute-done.1
  32.2 0.0 copy-done.2
  32.2 0.2 convolution_bitcast_fusion.1
  32.4 0.0 copy-done
  32.4 0.9 %fusion.3 = f32[32,32]{1,0:T(8,128)S(1)} fusion(f32[32,32]{1,0:T(8,128)S(1)} %convolution_bitcast_fusion.1, f32[32,32]{1,0:T(8,128)} %shard_map.38, bf16[3,32,1024]{2,1,0:T(8,128)(2,1)S(1)} %copy-done, f32[1024]{0:T(1024)S(1)} %convert_element_type.41), kind=kOutput, calls=%fused_computation.7 | convolution fusion | flops 6588416 | bytes 212992 | tf_op jit(solution)/shard_map/ckj,clj->kl/dot_general | solution.py:122
  33.4 0.0 collective-permute-done.2
  33.4 1.1 %fusion.1 = f32[32,32]{1,0:T(8,128)S(1)} fusion(bf16[3,32,1024]{2,1,0:T(8,128)(2,1)S(1)} %collective-permute-done.2, bf16[3,16,32,1024]{3,2,1,0:T(8,128)(2,1)} %get-tuple-element.17.live_ref, f32[1024]{0:T(1024)S(1)} %convert_element_type.47), kind=kOutput, calls=%fused_computation.4 | convolution fusion | flops 6587392 | bytes 401408 | tf_op jit(solution)/shard_map/ckj,clj->kl/dot_general | solution.py:122
  34.5 0.0 collective-permute-done.3
  34.5 0.0 copy-done.1
  34.5 0.2 fusion
  34.8 0.1 maximum_multiply_fusion
  34.8 0.1 mul.55
  35.0 20.5 %all_to_all.5 = f32[1,16,24,128]{3,2,0,1:T(8,128)S(1)} all-to-all(f32[1,16,24,128]{3,2,0,1:T(8,128)S(1)} %broadcast_in_dim.2), channel_id=1, replica_groups=mesh['sub'=32,'grp'=16] {'grp'}, dimensions={1} | all-to-all | bytes 393216 | tf_op jit(solution)/shard_map/all_to_all | solution.py:148
  55.4 0.8 %reshape.20 = f32[1,16,32,96]{3,2,1,0:T(8,128)} reshape(f32[1,16,24,128]{3,2,0,1:T(8,128)S(1)} %all_to_all.5) | data formatting | bytes 393216 | tf_op jit(solution)/shard_map/reshape | solution.py:149
  (6 shorter events, 0.0 us)
Async XLA Ops:
  8.0 24.1 %copy-start.2 = (bf16[3,16,32,128]{3,2,1,0:T(8,128)(2,1)S(1)}, bf16[3,16,32,128]{3,2,1,0:T(8,128)(2,1)}, u32[]{:S(2)}) copy-start(bf16[3,16,32,128]{3,2,1,0:T(8,128)(2,1)} %get-tuple-element.20) | copy-start | bytes 1179652
  8.0 24.4 %copy-start = (bf16[3,32,1024]{2,1,0:T(8,128)(2,1)S(1)}, bf16[3,32,1024]{2,1,0:T(8,128)(2,1)}, u32[]{:S(2)}) copy-start(bf16[3,32,1024]{2,1,0:T(8,128)(2,1)} %get-tuple-element.18) | copy-start | bytes 589828
  8.0 26.5 %copy-start.1 = (bf16[3,16,32,128]{3,2,1,0:T(8,128)(2,1)S(1)}, bf16[3,16,32,128]{3,2,1,0:T(8,128)(2,1)}, u32[]{:S(2)}) copy-start(bf16[3,16,32,128]{3,2,1,0:T(8,128)(2,1)} %get-tuple-element.22) | copy-start | bytes 1179652
  8.0 24.1 %collective-permute-start.1 = (bf16[16,128]{1,0:T(8,128)(2,1)S(1)}, bf16[16,128]{1,0:T(8,128)(2,1)S(1)}, u32[]{:S(2)}, u32[]{:S(2)}) collective-permute-start(bf16[16,128]{1,0:T(8,128)(2,1)S(1)} %bitcast.39), channel_id=1, source_target_pairs={{0,1},{1,2},{2,3},{3,4},{4,5},{5,6},{6,7},{7,8},{8,9},{9,10},{10,1... | collective-permute-start | bytes 12296 | tf_op jit(solution)/shard_map/ppermute | solution.py:12
  11.7 20.5 %collective-permute-start = (bf16[1024]{0:T(1024)(128)(2,1)S(1)}, bf16[1024]{0:T(1024)(128)(2,1)S(1)}, u32[]{:S(2)}, u32[]{:S(2)}) collective-permute-start(bf16[1024]{0:T(1024)(128)(2,1)S(1)} %slice_bitcast_fusion), channel_id=1, source_target_pairs={{0,16},{16,32},{32,48},{48,64},{64,80},{80,96},{96,112},{112,128},... | collective-permute-start | bytes 6152 | tf_op jit(solution)/shard_map/ppermute | solution.py:12
  13.6 19.8 %collective-permute-start.2 = (bf16[3,32,1024]{2,1,0:T(8,128)(2,1)}, bf16[3,32,1024]{2,1,0:T(8,128)(2,1)S(1)}, u32[]{:S(2)}, u32[]{:S(2)}) collective-permute-start(bf16[3,32,1024]{2,1,0:T(8,128)(2,1)} %get-tuple-element.18), channel_id=1, source_target_pairs={{16,0},{32,16},{48,32},{64,48},{80,64},{96,80},{112,96},{128,112},... | collective-permute-start | bytes 589832 | tf_op jit(solution)/shard_map/ppermute | solution.py:12
  23.7 10.8 %collective-permute-start.3 = (bf16[3,16,32,128]{3,2,1,0:T(8,128)(2,1)}, bf16[3,16,32,128]{3,2,1,0:T(8,128)(2,1)S(1)}, u32[]{:S(2)}, u32[]{:S(2)}) collective-permute-start(bf16[3,16,32,128]{3,2,1,0:T(8,128)(2,1)} %get-tuple-element.20), channel_id=1, source_target_pairs={{1,0},{2,1},{3,2},{4,3},{5,4},{6,5},{7,6},{8,7},{9,8},{10,9},{11,1... | collective-permute-start | bytes 1179656 | tf_op jit(solution)/shard_map/ppermute | solution.py:12

commit v13 on v7

--- a/solution.py
+++ b/solution.py
@@ -64,7 +64,7 @@
             left, right, (((1,), (1,)), ((), ())), preferred_element_type=jnp.float32
         )
 
-    out_ref[...] = lax.fori_loop(0, rows, body, jnp.zeros((count, count), jnp.float32))
+    out_ref[...] = lax.fori_loop(0, rows, body, jnp.zeros((count, count), jnp.float32), unroll=8)
 
 
 def local_terms(deflation, coefficients, depths):
@@ -103,8 +103,10 @@
     diagonal_block = diagonal_block + gram_of(bottom_y, weighted(weight_low_y, bottom_y))
     row_block = normalizer * jnp.concatenate([diagonal_block, coupling_x, coupling_y], axis=1)
     groups = lax.axis_size("grp")
-    copies = jnp.broadcast_to(row_block[None, None], (1, groups) + row_block.shape)
-    return lax.all_to_all(copies, "grp", 1, 1, tiled=True)
+    dense = row_block.reshape(-1, 128)
+    copies = jnp.broadcast_to(dense[None, None], (1, groups) + dense.shape)
+    gathered = lax.all_to_all(copies, "grp", 1, 1, tiled=True)
+    return gathered.reshape((1, groups) + row_block.shape)
 
 
 def solution(mesh):

time: 60.3 us -> 57.5 us (0.954)
  Pallas kernels: 10.6 us -> 8.1 us
    pallas_call x1, Pallas kernels: 10.6 us -> 8.1 us  [local_terms(): pl.pallas_call(local_kernel, out_shape=jax.ShapeDtypeStruct((count, count...]
    reshape x0 -> x1, local copies, waits for them, and re-layouts: none -> 0.82 us  [shards(): return gathered.reshape((1, groups) + row_block.shape)]
    unnamed x1 -> x0, local copies, waits for them, and re-layouts: 0.7 us -> none
  transfers between devices with their start and end apart: 4 -> 4, of which waited for: 0 -> 0; matrix products, arithmetic and copies ran while one was open for 13% -> 14% of each run, Pallas kernels for 18% -> 14%
where the time goes in v13:
time: 57.5 us; the launch traced here: 57.2 us
  blocking collectives  20.5 us (36%)
  starting transfers between devices  17.8 us (31%)
  Pallas kernels  8.1 us (14%)
  local copies, waits for them, and re-layouts  7.12 us (12%)
  matrix products  1.81 us (3%)
  other arithmetic  1.04 us (2%)
  between operations  0.78 us (1%)
    all_to_all x1, blocking collectives, shards(): gathered = lax.all_to_all(copies, 'grp', 1, 1, tiled=True)  20.5 us
    ppermute x4, starting transfers between devices, from_behind(): return lax.ppermute(x, axis, pairs)  17.8 us
    pallas_call x1, Pallas kernels, local_terms(): pl.pallas_call(local_kernel, out_shape=jax.ShapeDtypeStruct((count, count...  8.1 us
    slice x1, local copies, waits for them, and re-layouts, shards(): top_y = deflation[:, :, :, -1] * live_mask  4.35 us
    dot_general x4, matrix products, gram_of(): jnp.dot(left_side.reshape(count, -1), right_side.reshape(count, -1).T, pr...  1.81 us
  transfers between devices with their start and end apart: 4, of which 0 were waited for; matrix products, arithmetic and copies ran while one was open for 14% of the time, Pallas kernels for 14%

profile of v13, /device:TPU:10, one launch (start us, length us, event | category | flops | bytes accessed | tf_op | source)
XLA Modules:
  0.0 57.2 jit_solution(10373007773423807209)
XLA Ops:
  0.0 0.7 %slice_bitcast_fusion = (bf16[8,128]{1,0:T(8,128)(2,1)S(1)}, f32[8,128]{1,0:T(8,128)S(1)}) fusion(bf16[4,16,8,128]{3,2,1,0:T(8,128)(2,1)} %coeff_ref.1), kind=kLoop, calls=%fused_computation.36 | loop fusion | flops 1024 | bytes 8192 | tf_op jit(solution)/shard_map/squeeze | solution.py:91
  0.7 1.9 %collective-permute-start = (bf16[8,128]{1,0:T(8,128)(2,1)S(1)}, bf16[8,128]{1,0:T(8,128)(2,1)S(1)}, u32[]{:S(2)}, u32[]{:S(2)}) collective-permute-start(bf16[8,128]{1,0:T(8,128)(2,1)S(1)} %get-tuple-element.11), channel_id=1, source_target_pairs={{0,16},{16,32},{32,48},{48,64},{64,80},{80,96},{96,112},{112,128},... | collective-permute-start | bytes 6152 | tf_op jit(solution)/shard_map/ppermute | solution.py:12
  2.6 0.8 %slice.21 = bf16[1,16,1,128]{3,2,1,0:T(2,128)(2,1)S(1)} slice(bf16[4,16,8,128]{3,2,1,0:T(8,128)(2,1)} %coeff_ref.1), slice={[2:3], [0:16], [7:8], [0:128]} | slice | bytes 8192 | tf_op jit(solution)/shard_map/slice | solution.py:92
  3.4 3.5 %collective-permute-start.1 = (bf16[16,128]{1,0:T(8,128)(2,1)S(1)}, bf16[16,128]{1,0:T(8,128)(2,1)S(1)}, u32[]{:S(2)}, u32[]{:S(2)}) collective-permute-start(bf16[16,128]{1,0:T(8,128)(2,1)S(1)} %get-tuple-element.6), channel_id=1, source_target_pairs={{0,1},{1,2},{2,3},{3,4},{4,5},{5,6},{6,7},{7,8},{8,9},{9,10},{10,1... | collective-permute-start | bytes 12296 | tf_op jit(solution)/shard_map/ppermute | solution.py:12
  7.5 1.1 %fusion.28 = (bf16[32,3,1,8,128]{4,3,2,1,0:T(8,128)(2,1)S(1)}, bf16[32,3,1,8,128]{4,3,2,1,0:T(8,128)(2,1)S(1)}) fusion(bf16[32,3,16,8,128]{4,3,2,1,0:T(8,128)(2,1)} %defl_ref.1), kind=kLoop, calls=%fused_computation.40 | loop fusion | bytes 786432 | tf_op jit(solution)/shard_map/slice | solution.py:98
  8.7 10.1 %collective-permute-start.2 = (bf16[32,3,8,128]{3,0,2,1:T(8,128)(2,1)S(1)}, bf16[32,3,8,128]{3,0,2,1:T(8,128)(2,1)S(1)}, u32[]{:S(2)}, u32[]{:S(2)}) collective-permute-start(bf16[32,3,8,128]{3,0,2,1:T(8,128)(2,1)S(1)} %bitcast_multiply_fusion.1), channel_id=1, source_target_pairs={{16,0},{32,16},{48,32},{64,48},{80,64},{96,80},{112,96},{128,112},... | collective-permute-start | bytes 589832 | tf_op jit(solution)/shard_map/ppermute | solution.py:12
  18.7 4.4 %fusion.29 = (bf16[32,3,16,1,128]{4,3,2,1,0:T(2,128)(2,1)S(1)}, bf16[32,3,16,1,128]{4,3,2,1,0:T(2,128)(2,1)S(1)}) fusion(bf16[32,3,16,8,128]{4,3,2,1,0:T(8,128)(2,1)} %defl_ref.1), kind=kLoop, calls=%fused_computation.41 | loop fusion | bytes 1572864 | tf_op jit(solution)/shard_map/slice | solution.py:99
  23.1 0.2 bitcast_multiply_fusion
  23.3 2.4 %collective-permute-start.3 = (bf16[32,3,16,128]{3,0,2,1:T(8,128)(2,1)S(1)}, bf16[32,3,16,128]{3,0,2,1:T(8,128)(2,1)S(1)}, u32[]{:S(2)}, u32[]{:S(2)}) collective-permute-start(bf16[32,3,16,128]{3,0,2,1:T(8,128)(2,1)S(1)} %bitcast_multiply_fusion), channel_id=1, source_target_pairs={{1,0},{2,1},{3,2},{4,3},{5,4},{6,5},{7,6},{8,7},{9,8},{10,9},{11,1... | collective-permute-start | bytes 1179656 | tf_op jit(solution)/shard_map/ppermute | solution.py:12
  25.7 8.1 %shard_map.37 = f32[32,32]{1,0:T(8,128)} custom-call(s32[1]{0:T(128)} %copy.55.depth_ref, bf16[32,3,16,8,128]{4,3,2,1,0:T(8,128)(2,1)} %defl_ref.1, bf16[4,16,8,128]{3,2,1,0:T(8,128)(2,1)} %coeff_ref.1), custom_call_target="tpu_custom_call" | custom-call | flops 402653184 | bytes 3276800 | tf_op jit(solution)/shard_map/pallas_call | solution.py:72
  33.8 0.0 collective-permute-done
  33.8 0.0 collective-permute-done.1
  33.8 0.4 convolution_bitcast_fusion.1
  34.2 0.9 %fusion.3 = f32[32,32]{1,0:T(8,128)S(1)} fusion(f32[32,32]{1,0:T(8,128)S(1)} %convolution_bitcast_fusion.1, f32[32,32]{1,0:T(8,128)} %shard_map.37, f32[8,128]{1,0:T(8,128)S(1)} %convert_element_type.55, bf16[32,3,1,8,128]{4,3,2,1,0:T(8,128)(2,1)S(1)} %get-tuple-element.8, bf16[128]{0:T(256)(128)(2,1)S(1)} %compare_convert_fusion), kind=kOutput, calls=%fused_computation.7 | convolution fusion | flops 6785024 | bytes 213248 | tf_op jit(solution)/shard_map/dot_general | solution.py:17
  35.1 0.0 collective-permute-done.2
  35.1 0.2 fusion.1
  35.3 0.0 collective-permute-done.3
  35.3 0.4 fusion
  35.7 0.1 maximum_multiply_fusion
  35.8 0.1 mul.117
  35.9 20.5 %all_to_all.5 = f32[1,16,24,128]{3,2,0,1:T(8,128)S(1)} all-to-all(f32[1,16,24,128]{3,2,0,1:T(8,128)S(1)} %broadcast_in_dim.2), channel_id=1, replica_groups=mesh['sub'=32,'grp'=16] {'grp'}, dimensions={1} | all-to-all | bytes 393216 | tf_op jit(solution)/shard_map/all_to_all | solution.py:108
  56.3 0.8 %reshape.36 = f32[1,16,32,96]{3,2,1,0:T(8,128)} reshape(f32[1,16,24,128]{3,2,0,1:T(8,128)S(1)} %all_to_all.5) | data formatting | bytes 393216 | tf_op jit(solution)/shard_map/reshape | solution.py:109
  (6 shorter events, 0.1 us)
Async XLA Ops:
  0.7 33.1 %collective-permute-start = (bf16[8,128]{1,0:T(8,128)(2,1)S(1)}, bf16[8,128]{1,0:T(8,128)(2,1)S(1)}, u32[]{:S(2)}, u32[]{:S(2)}) collective-permute-start(bf16[8,128]{1,0:T(8,128)(2,1)S(1)} %get-tuple-element.11), channel_id=1, source_target_pairs={{0,16},{16,32},{32,48},{48,64},{64,80},{80,96},{96,112},{112,128},... | collective-permute-start | bytes 6152 | tf_op jit(solution)/shard_map/ppermute | solution.py:12
  3.4 30.4 %collective-permute-start.1 = (bf16[16,128]{1,0:T(8,128)(2,1)S(1)}, bf16[16,128]{1,0:T(8,128)(2,1)S(1)}, u32[]{:S(2)}, u32[]{:S(2)}) collective-permute-start(bf16[16,128]{1,0:T(8,128)(2,1)S(1)} %get-tuple-element.6), channel_id=1, source_target_pairs={{0,1},{1,2},{2,3},{3,4},{4,5},{5,6},{6,7},{7,8},{8,9},{9,10},{10,1... | collective-permute-start | bytes 12296 | tf_op jit(solution)/shard_map/ppermute | solution.py:12
  8.7 26.5 %collective-permute-start.2 = (bf16[32,3,8,128]{3,0,2,1:T(8,128)(2,1)S(1)}, bf16[32,3,8,128]{3,0,2,1:T(8,128)(2,1)S(1)}, u32[]{:S(2)}, u32[]{:S(2)}) collective-permute-start(bf16[32,3,8,128]{3,0,2,1:T(8,128)(2,1)S(1)} %bitcast_multiply_fusion.1), channel_id=1, source_target_pairs={{16,0},{32,16},{48,32},{64,48},{80,64},{96,80},{112,96},{128,112},... | collective-permute-start | bytes 589832 | tf_op jit(solution)/shard_map/ppermute | solution.py:12
  23.3 12.0 %collective-permute-start.3 = (bf16[32,3,16,128]{3,0,2,1:T(8,128)(2,1)S(1)}, bf16[32,3,16,128]{3,0,2,1:T(8,128)(2,1)S(1)}, u32[]{:S(2)}, u32[]{:S(2)}) collective-permute-start(bf16[32,3,16,128]{3,0,2,1:T(8,128)(2,1)S(1)} %bitcast_multiply_fusion), channel_id=1, source_target_pairs={{1,0},{2,1},{3,2},{4,3},{5,4},{6,5},{7,6},{8,7},{9,8},{10,9},{11,1... | collective-permute-start | bytes 1179656 | tf_op jit(solution)/shard_map/ppermute | solution.py:12

commit v14 on v12

--- a/solution.py
+++ b/solution.py
@@ -23,6 +23,30 @@
 
 def weighted(weight, values):
     return (weight.astype(jnp.float32) * values.astype(jnp.float32)).astype(jnp.bfloat16)
+
+
+def low_kernel(depth_ref, defl_ref, low_ref):
+    count, comps, rows, cols, depth = defl_ref.shape
+    lane = lax.broadcasted_iota(jnp.int32, (count, depth), 1)
+    live_mask = (lane < depth_ref[0]).astype(jnp.bfloat16)
+    for comp in range(comps):
+
+        def body(row, carry):
+            low_ref[comp, row] = defl_ref[:, comp, row, 0, :] * live_mask
+            return carry
+
+        lax.fori_loop(0, rows, body, 0, unroll=4)
+
+
+def low_layer(deflation, depths):
+    count, comps, rows, cols, depth = deflation.shape
+    return pl.pallas_call(
+        low_kernel,
+        out_shape=jax.ShapeDtypeStruct((comps, rows, count, depth), jnp.bfloat16),
+        in_specs=[pl.BlockSpec(memory_space=pltpu.SMEM), pl.BlockSpec(memory_space=pltpu.VMEM)],
+        out_specs=pl.BlockSpec(memory_space=pltpu.VMEM),
+        cost_estimate=pl.CostEstimate(flops=0, bytes_accessed=deflation.size * 2, transcendentals=0),
+    )(depths, deflation)
 
 
 def turn_kernel(depth_ref, defl_ref, live_ref, low_ref, high_ref, first_ref):
@@ -125,13 +149,14 @@
 def shards(deflation, stiffness, depths):
     cell_count = deflation.shape[2] * deflation.shape[3] * deflation.shape[4]
     normalizer = 1.0 / (24.0 * cell_count)
+    low_y, deflation = lax.optimization_barrier((low_layer(deflation, depths), deflation))
+    next_y = from_behind(low_y, "grp", -1)
     live_t, bottom_y, top_y, bottom_x = turned_field(deflation, depths)
     weight_top_x = stiffness[1, -1].reshape(-1)
     weight_top_y = stiffness[2, :, -1]
     live_t, bottom_y, bottom_x, weight_top_x, weight_top_y = lax.optimization_barrier(
         (live_t, bottom_y, bottom_x, weight_top_x, weight_top_y)
     )
-    next_y = from_behind(bottom_y, "grp", -1)
     next_x = from_behind(bottom_x, "sub", -1)
     weight_low_x = from_behind(weight_top_x, "sub", 1)
     weight_low_y = from_behind(weight_top_y, "grp", 1)

time: 56.7 us -> 58.9 us (1.039)
  Pallas kernels: 12 us -> 15.4 us
  blocking collectives: 20.5 us -> 19.2 us
    pallas_call x0 -> x1, Pallas kernels: none -> 3.38 us  [low_layer(): pl.pallas_call(low_kernel, out_shape=jax.ShapeDtypeStruct((comps, rows, c...]
    all_to_all x1, blocking collectives: 20.5 us -> 19.2 us  [shards(): gathered = lax.all_to_all(copies, 'grp', 1, 1, tiled=True)]
  transfers between devices with their start and end apart: 4 -> 4, of which waited for: 0 -> 0; matrix products, arithmetic and copies ran while one was open for 4% -> 6% of each run, Pallas kernels for 11% -> 21%
where the time goes in v14:
time: 58.9 us; the launch traced here: 58.4 us
  blocking collectives  19.2 us (33%)
  starting transfers between devices  18 us (31%)
  Pallas kernels  15.4 us (26%)
  matrix products  2.53 us (4%)
  local copies, waits for them, and re-layouts  2.39 us (4%)
  between operations  0.77 us (1%)
    all_to_all x1, blocking collectives, shards(): gathered = lax.all_to_all(copies, 'grp', 1, 1, tiled=True)  19.2 us
    ppermute x4, starting transfers between devices, from_behind(): return lax.ppermute(x, axis, pairs)  18 us
    pallas_call x1, Pallas kernels, local_terms(): pl.pallas_call(local_kernel, out_shape=jax.ShapeDtypeStruct((count, count...  6.1 us
    pallas_call x1, Pallas kernels, turned_field(): pl.pallas_call(turn_kernel, out_shape=(jax.ShapeDtypeStruct((comps, rows,...  5.9 us
    pallas_call x1, Pallas kernels, low_layer(): pl.pallas_call(low_kernel, out_shape=jax.ShapeDtypeStruct((comps, rows, c...  3.38 us
    dot_general x2, matrix products, layer_gram(): jnp.einsum('ckj,clj->kl', left_side, right_side, preferred_element_type=j...  2.04 us
  transfers between devices with their start and end apart: 4, of which 0 were waited for; matrix products, arithmetic and copies ran while one was open for 6% of the time, Pallas kernels for 21%

profile of v14, /device:TPU:10, one launch (start us, length us, event | category | flops | bytes accessed | tf_op | source)
XLA Modules:
  0.0 58.4 jit_solution(6920817166272367941)
XLA Ops:
  0.7 3.4 %shard_map.37 = bf16[3,16,32,128]{3,2,1,0:T(8,128)(2,1)} custom-call(s32[1]{0:T(128)S(6)} %copy.11.depth_ref, bf16[32,3,16,8,128]{4,3,2,1,0:T(8,128)(2,1)} %defl_ref.2), custom_call_target="tpu_custom_call" | custom-call | bytes 3145728 | tf_op jit(solution)/shard_map/pallas_call | solution.py:43
  4.0 2.3 %collective-permute-start.3 = (bf16[3,16,32,128]{3,2,1,0:T(8,128)(2,1)}, bf16[3,16,32,128]{3,2,1,0:T(8,128)(2,1)S(1)}, u32[]{:S(2)}, u32[]{:S(2)}) collective-permute-start(bf16[3,16,32,128]{3,2,1,0:T(8,128)(2,1)} %shard_map.37), channel_id=1, source_target_pairs={{1,0},{2,1},{3,2},{4,3},{5,4},{6,5},{7,6},{8,7},{9,8},{10,9},{11,1... | collective-permute-start | bytes 1179656 | tf_op jit(solution)/shard_map/ppermute | solution.py:12
  6.4 0.7 %slice_bitcast_fusion = bf16[1024]{0:T(1024)(128)(2,1)S(1)} fusion(bf16[4,16,8,128]{3,2,1,0:T(8,128)(2,1)} %coeff_ref.1), kind=kLoop, calls=%fused_computation.21 | loop fusion | bytes 4096 | tf_op jit(solution)/shard_map/reshape;squeeze | solution.py:155
  7.1 0.8 %slice.10 = bf16[1,16,1,128]{3,2,1,0:T(2,128)(2,1)S(1)} slice(bf16[4,16,8,128]{3,2,1,0:T(8,128)(2,1)} %coeff_ref.1), slice={[2:3], [0:16], [7:8], [0:128]} | slice | bytes 8192 | tf_op jit(solution)/shard_map/slice | solution.py:156
  7.8 5.9 %shard_map.38 = (bf16[3,16,32,1024]{3,2,1,0:T(8,128)(2,1)}, bf16[3,16,32,128]{3,2,1,0:T(8,128)(2,1)}, bf16[3,16,32,128]{3,2,1,0:T(8,128)(2,1)}, bf16[3,32,1024]{2,1,0:T(8,128)(2,1)}) custom-call(s32[1]{0:T(128)S(6)} %copy.11.depth_ref, bf16[32,3,16,8,128]{4,3,2,1,0:T(8,128)(2,1)} %defl_ref.2), custom_call_target="tpu_custom_call" | custom-call | bytes 7864320 | tf_op jit(solution)/shard_map/pallas_call | solution.py:112
  13.7 0.0 copy-start.2
  13.7 0.0 copy-start
  13.8 0.0 copy-start.1
  13.8 10.2 %collective-permute-start.2 = (bf16[3,32,1024]{2,1,0:T(8,128)(2,1)}, bf16[3,32,1024]{2,1,0:T(8,128)(2,1)S(1)}, u32[]{:S(2)}, u32[]{:S(2)}) collective-permute-start(bf16[3,32,1024]{2,1,0:T(8,128)(2,1)} %get-tuple-element.21), channel_id=1, source_target_pairs={{16,0},{32,16},{48,32},{64,48},{80,64},{96,80},{112,96},{128,112},... | collective-permute-start | bytes 589832 | tf_op jit(solution)/shard_map/ppermute | solution.py:12
  24.0 3.5 %collective-permute-start.1 = (bf16[16,128]{1,0:T(8,128)(2,1)S(1)}, bf16[16,128]{1,0:T(8,128)(2,1)S(1)}, u32[]{:S(2)}, u32[]{:S(2)}) collective-permute-start(bf16[16,128]{1,0:T(8,128)(2,1)S(1)} %bitcast.39), channel_id=1, source_target_pairs={{0,1},{1,2},{2,3},{3,4},{4,5},{5,6},{6,7},{7,8},{8,9},{9,10},{10,1... | collective-permute-start | bytes 12296 | tf_op jit(solution)/shard_map/ppermute | solution.py:12
  27.5 1.9 %collective-permute-start = (bf16[1024]{0:T(1024)(128)(2,1)S(1)}, bf16[1024]{0:T(1024)(128)(2,1)S(1)}, u32[]{:S(2)}, u32[]{:S(2)}) collective-permute-start(bf16[1024]{0:T(1024)(128)(2,1)S(1)} %slice_bitcast_fusion), channel_id=1, source_target_pairs={{0,16},{16,32},{32,48},{48,64},{64,80},{80,96},{96,112},{112,128},... | collective-permute-start | bytes 6152 | tf_op jit(solution)/shard_map/ppermute | solution.py:12
  29.4 6.1 %shard_map.39 = f32[32,32]{1,0:T(8,128)} custom-call(bf16[3,16,32,1024]{3,2,1,0:T(8,128)(2,1)} %get-tuple-element.20.live_ref, bf16[4,16,8,128]{3,2,1,0:T(8,128)(2,1)} %coeff_ref.1), custom_call_target="tpu_custom_call" | custom-call | flops 402653184 | bytes 3276800 | tf_op jit(solution)/shard_map/pallas_call | solution.py:128
  35.5 0.0 collective-permute-done
  35.5 0.0 collective-permute-done.1
  35.5 0.0 copy-done.2
  35.6 0.2 convolution_bitcast_fusion.1
  35.8 0.0 copy-done
  35.8 0.9 %fusion.3 = f32[32,32]{1,0:T(8,128)S(1)} fusion(f32[32,32]{1,0:T(8,128)S(1)} %convolution_bitcast_fusion.1, f32[32,32]{1,0:T(8,128)} %shard_map.39, bf16[3,32,1024]{2,1,0:T(8,128)(2,1)S(1)} %copy-done, f32[1024]{0:T(1024)S(1)} %convert_element_type.41), kind=kOutput, calls=%fused_computation.7 | convolution fusion | flops 6588416 | bytes 212992 | tf_op jit(solution)/shard_map/ckj,clj->kl/dot_general | solution.py:146
  36.7 0.0 collective-permute-done.2
  36.7 1.1 %fusion.1 = f32[32,32]{1,0:T(8,128)S(1)} fusion(bf16[3,32,1024]{2,1,0:T(8,128)(2,1)S(1)} %collective-permute-done.2, bf16[3,16,32,1024]{3,2,1,0:T(8,128)(2,1)} %get-tuple-element.20.live_ref, f32[1024]{0:T(1024)S(1)} %convert_element_type.47), kind=kOutput, calls=%fused_computation.4 | convolution fusion | flops 6587392 | bytes 401408 | tf_op jit(solution)/shard_map/ckj,clj->kl/dot_general | solution.py:146
  37.9 0.0 collective-permute-done.3
  37.9 0.0 copy-done.1
  37.9 0.2 fusion
  38.1 0.1 maximum_multiply_fusion
  38.2 0.1 mul.55
  38.3 19.2 %all_to_all.5 = f32[1,16,24,128]{3,2,0,1:T(8,128)S(1)} all-to-all(f32[1,16,24,128]{3,2,0,1:T(8,128)S(1)} %broadcast_in_dim.2), channel_id=1, replica_groups=mesh['sub'=32,'grp'=16] {'grp'}, dimensions={1} | all-to-all | bytes 393216 | tf_op jit(solution)/shard_map/all_to_all | solution.py:173
  57.6 0.8 %reshape.20 = f32[1,16,32,96]{3,2,1,0:T(8,128)} reshape(f32[1,16,24,128]{3,2,0,1:T(8,128)S(1)} %all_to_all.5) | data formatting | bytes 393216 | tf_op jit(solution)/shard_map/reshape | solution.py:174
  (6 shorter events, 0.0 us)
Async XLA Ops:
  4.0 33.8 %collective-permute-start.3 = (bf16[3,16,32,128]{3,2,1,0:T(8,128)(2,1)}, bf16[3,16,32,128]{3,2,1,0:T(8,128)(2,1)S(1)}, u32[]{:S(2)}, u32[]{:S(2)}) collective-permute-start(bf16[3,16,32,128]{3,2,1,0:T(8,128)(2,1)} %shard_map.37), channel_id=1, source_target_pairs={{1,0},{2,1},{3,2},{4,3},{5,4},{6,5},{7,6},{8,7},{9,8},{10,9},{11,1... | collective-permute-start | bytes 1179656 | tf_op jit(solution)/shard_map/ppermute | solution.py:12
  13.7 21.8 %copy-start.2 = (bf16[3,16,32,128]{3,2,1,0:T(8,128)(2,1)S(1)}, bf16[3,16,32,128]{3,2,1,0:T(8,128)(2,1)}, u32[]{:S(2)}) copy-start(bf16[3,16,32,128]{3,2,1,0:T(8,128)(2,1)} %get-tuple-element.23) | copy-start | bytes 1179652
  13.7 22.1 %copy-start = (bf16[3,32,1024]{2,1,0:T(8,128)(2,1)S(1)}, bf16[3,32,1024]{2,1,0:T(8,128)(2,1)}, u32[]{:S(2)}) copy-start(bf16[3,32,1024]{2,1,0:T(8,128)(2,1)} %get-tuple-element.21) | copy-start | bytes 589828
  13.8 24.1 %copy-start.1 = (bf16[3,16,32,128]{3,2,1,0:T(8,128)(2,1)S(1)}, bf16[3,16,32,128]{3,2,1,0:T(8,128)(2,1)}, u32[]{:S(2)}) copy-start(bf16[3,16,32,128]{3,2,1,0:T(8,128)(2,1)} %get-tuple-element.25) | copy-start | bytes 1179652
  13.8 23.0 %collective-permute-start.2 = (bf16[3,32,1024]{2,1,0:T(8,128)(2,1)}, bf16[3,32,1024]{2,1,0:T(8,128)(2,1)S(1)}, u32[]{:S(2)}, u32[]{:S(2)}) collective-permute-start(bf16[3,32,1024]{2,1,0:T(8,128)(2,1)} %get-tuple-element.21), channel_id=1, source_target_pairs={{16,0},{32,16},{48,32},{64,48},{80,64},{96,80},{112,96},{128,112},... | collective-permute-start | bytes 589832 | tf_op jit(solution)/shard_map/ppermute | solution.py:12
  24.0 11.5 %collective-permute-start.1 = (bf16[16,128]{1,0:T(8,128)(2,1)S(1)}, bf16[16,128]{1,0:T(8,128)(2,1)S(1)}, u32[]{:S(2)}, u32[]{:S(2)}) collective-permute-start(bf16[16,128]{1,0:T(8,128)(2,1)S(1)} %bitcast.39), channel_id=1, source_target_pairs={{0,1},{1,2},{2,3},{3,4},{4,5},{5,6},{6,7},{7,8},{8,9},{9,10},{10,1... | collective-permute-start | bytes 12296 | tf_op jit(solution)/shard_map/ppermute | solution.py:12
  27.5 8.0 %collective-permute-start = (bf16[1024]{0:T(1024)(128)(2,1)S(1)}, bf16[1024]{0:T(1024)(128)(2,1)S(1)}, u32[]{:S(2)}, u32[]{:S(2)}) collective-permute-start(bf16[1024]{0:T(1024)(128)(2,1)S(1)} %slice_bitcast_fusion), channel_id=1, source_target_pairs={{0,16},{16,32},{32,48},{48,64},{64,80},{80,96},{96,112},{112,128},... | collective-permute-start | bytes 6152 | tf_op jit(solution)/shard_map/ppermute | solution.py:12

commit v15 on v10

--- a/solution.py
+++ b/solution.py
@@ -134,17 +134,19 @@
     next_y = from_behind(bottom_y, "grp", -1)
     next_x = from_behind(bottom_x, "sub", -1)
     weight_low_x = from_behind(weight_top_x, "sub", 1)
-    weight_low_y = from_behind(weight_top_y, "grp", 1)
     diagonal_block = local_terms(live_t, stiffness)
     top_x = live_t[:, -1]
     coupling_x = -layer_gram(weighted(weight_top_x, top_x), next_x)
     coupling_y = -face_gram(weighted(weight_top_y[None, :, None], top_y), next_y)
     diagonal_block = diagonal_block + layer_gram(bottom_x, weighted(weight_low_x, bottom_x))
-    diagonal_block = diagonal_block + face_gram(bottom_y, weighted(weight_low_y[None, :, None], bottom_y))
-    row_block = normalizer * jnp.concatenate([diagonal_block, coupling_x, coupling_y], axis=1)
+    lower_y_next = face_gram(next_y, weighted(weight_top_y[None, :, None], next_y))
+    row_block = normalizer * jnp.concatenate([diagonal_block, coupling_x, coupling_y, lower_y_next], axis=1)
     groups = lax.axis_size("grp")
+    count = diagonal_block.shape[0]
     copies = jnp.broadcast_to(row_block[None, None], (1, groups) + row_block.shape)
-    return lax.all_to_all(copies, "grp", 1, 1, tiled=True)
+    gathered = lax.all_to_all(copies, "grp", 1, 1, tiled=True)
+    from_below = jnp.pad(gathered[:, :-1, :, 3 * count:], ((0, 0), (1, 0), (0, 0), (0, 0)))
+    return jnp.concatenate([gathered[..., :count] + from_below, gathered[..., count:3 * count]], axis=-1)
 
 
 def solution(mesh):

time: 57 us -> 53.1 us (0.932)
  starting transfers between devices: 18 us -> 14.8 us
  blocking collectives: 21 us -> 19.9 us
  other arithmetic: 0.1 us -> 0.98 us
    ppermute x4 -> x3, starting transfers between devices: 18 us -> 14.8 us  [from_behind(): return lax.ppermute(x, axis, pairs)]
    all_to_all x1, blocking collectives: 21 us -> 19.9 us  [shards(): gathered = lax.all_to_all(copies, 'grp', 1, 1, tiled=True)]
    concatenate x0 -> x1, other arithmetic: none -> 0.84 us  [shards(): jnp.concatenate([gathered[..., :count] + from_below, gathered[..., count:...]
    unnamed x8 -> x5, local copies, waits for them, and re-layouts: 0.72 us -> 0.01 us
  transfers between devices with their start and end apart: 4 -> 3, of which waited for: 0 -> 0; matrix products, arithmetic and copies ran while one was open for 4% -> 4% of each run, Pallas kernels for 11% -> 12%
where the time goes in v15:
time: 53.1 us; the launch traced here: 52.7 us
  blocking collectives  19.9 us (37%)
  starting transfers between devices  14.8 us (28%)
  Pallas kernels  12 us (23%)
  matrix products  2.53 us (5%)
  local copies, waits for them, and re-layouts  1.75 us (3%)
  other arithmetic  0.98 us (2%)
  between operations  0.77 us (1%)
    all_to_all x1, blocking collectives, shards(): gathered = lax.all_to_all(copies, 'grp', 1, 1, tiled=True)  19.9 us
    ppermute x3, starting transfers between devices, from_behind(): return lax.ppermute(x, axis, pairs)  14.8 us
    pallas_call x1, Pallas kernels, local_terms(): pl.pallas_call(local_kernel, out_shape=jax.ShapeDtypeStruct((count, count...  6.11 us
    pallas_call x1, Pallas kernels, turned_field(): pl.pallas_call(turn_kernel, out_shape=(jax.ShapeDtypeStruct((comps, rows,...  5.9 us
    dot_general x2, matrix products, layer_gram(): jnp.einsum('ckj,clj->kl', left_side, right_side, preferred_element_type=j...  2.02 us
  transfers between devices with their start and end apart: 3, of which 0 were waited for; matrix products, arithmetic and copies ran while one was open for 4% of the time, Pallas kernels for 12%

profile of v15, /device:TPU:10, one launch (start us, length us, event | category | flops | bytes accessed | tf_op | source)
XLA Modules:
  0.0 52.7 jit_solution(11612165621233928607)
XLA Ops:
  0.0 0.8 %slice.19 = bf16[1,16,1,128]{3,2,1,0:T(2,128)(2,1)S(1)} slice(bf16[4,16,8,128]{3,2,1,0:T(8,128)(2,1)} %coeff_ref.1), slice={[2:3], [0:16], [7:8], [0:128]} | slice | bytes 8192 | tf_op jit(solution)/shard_map/slice | solution.py:130
  0.8 0.7 %slice_bitcast_fusion = bf16[1024]{0:T(1024)(128)(2,1)S(1)} fusion(bf16[4,16,8,128]{3,2,1,0:T(8,128)(2,1)} %coeff_ref.1), kind=kLoop, calls=%fused_computation.22 | loop fusion | bytes 4096 | tf_op jit(solution)/shard_map/reshape;squeeze | solution.py:129
  2.1 5.9 %shard_map.37 = (bf16[3,16,32,1024]{3,2,1,0:T(8,128)(2,1)}, bf16[3,16,32,128]{3,2,1,0:T(8,128)(2,1)}, bf16[3,16,32,128]{3,2,1,0:T(8,128)(2,1)}, bf16[3,32,1024]{2,1,0:T(8,128)(2,1)}) custom-call(s32[1]{0:T(128)S(6)} %copy.12.depth_ref, bf16[32,3,16,8,128]{4,3,2,1,0:T(8,128)(2,1)} %defl_ref.1), custom_call_target="tpu_custom_call" | custom-call | bytes 7864320 | tf_op jit(solution)/shard_map/pallas_call | solution.py:88
  8.0 0.0 copy-start
  8.0 0.0 copy-start.1
  8.0 2.0 %collective-permute-start = (bf16[1024]{0:T(1024)(128)(2,1)S(1)}, bf16[1024]{0:T(1024)(128)(2,1)S(1)}, u32[]{:S(2)}, u32[]{:S(2)}) collective-permute-start(bf16[1024]{0:T(1024)(128)(2,1)S(1)} %slice_bitcast_fusion), channel_id=1, source_target_pairs={{0,16},{16,32},{32,48},{48,64},{64,80},{80,96},{96,112},{112,128},... | collective-permute-start | bytes 6152 | tf_op jit(solution)/shard_map/ppermute | solution.py:12
  10.1 10.4 %collective-permute-start.1 = (bf16[3,32,1024]{2,1,0:T(8,128)(2,1)}, bf16[3,32,1024]{2,1,0:T(8,128)(2,1)S(1)}, u32[]{:S(2)}, u32[]{:S(2)}) collective-permute-start(bf16[3,32,1024]{2,1,0:T(8,128)(2,1)} %get-tuple-element.18), channel_id=1, source_target_pairs={{16,0},{32,16},{48,32},{64,48},{80,64},{96,80},{112,96},{128,112},... | collective-permute-start | bytes 589832 | tf_op jit(solution)/shard_map/ppermute | solution.py:12
  20.4 2.4 %collective-permute-start.2 = (bf16[3,16,32,128]{3,2,1,0:T(8,128)(2,1)}, bf16[3,16,32,128]{3,2,1,0:T(8,128)(2,1)S(1)}, u32[]{:S(2)}, u32[]{:S(2)}) collective-permute-start(bf16[3,16,32,128]{3,2,1,0:T(8,128)(2,1)} %get-tuple-element.22), channel_id=1, source_target_pairs={{1,0},{2,1},{3,2},{4,3},{5,4},{6,5},{7,6},{8,7},{9,8},{10,9},{11,1... | collective-permute-start | bytes 1179656 | tf_op jit(solution)/shard_map/ppermute | solution.py:12
  22.8 6.1 %shard_map.38 = f32[32,32]{1,0:T(8,128)} custom-call(bf16[3,16,32,1024]{3,2,1,0:T(8,128)(2,1)} %get-tuple-element.17.live_ref, bf16[4,16,8,128]{3,2,1,0:T(8,128)(2,1)} %coeff_ref.1), custom_call_target="tpu_custom_call" | custom-call | flops 402653184 | bytes 3276800 | tf_op jit(solution)/shard_map/pallas_call | solution.py:104
  28.9 0.0 collective-permute-done
  28.9 0.0 copy-done
  28.9 0.9 %fusion.2 = f32[32,32]{1,0:T(8,128)S(1)} fusion(f32[32,32]{1,0:T(8,128)} %shard_map.38, bf16[3,32,1024]{2,1,0:T(8,128)(2,1)S(1)} %copy-done, f32[1024]{0:T(1024)S(1)} %convert_element_type.40), kind=kOutput, calls=%fused_computation.6 | convolution fusion | flops 6587392 | bytes 208896 | tf_op jit(solution)/shard_map/ckj,clj->kl/dot_general | solution.py:122
  29.9 0.0 collective-permute-done.1
  29.9 1.1 %fusion.1 = f32[32,32]{1,0:T(8,128)S(1)} fusion(bf16[3,32,1024]{2,1,0:T(8,128)(2,1)S(1)} %collective-permute-done.1, bf16[3,16,32,1024]{3,2,1,0:T(8,128)(2,1)} %get-tuple-element.17.live_ref, f32[1024]{0:T(1024)S(1)} %convert_element_type.43), kind=kOutput, calls=%fused_computation.4 | convolution fusion | flops 6587392 | bytes 401408 | tf_op jit(solution)/shard_map/ckj,clj->kl/dot_general | solution.py:122
  31.0 0.0 collective-permute-done.2
  31.0 0.2 convolution_bitcast_fusion
  31.3 0.0 copy-done.1
  31.3 0.3 fusion
  31.5 0.1 maximum_multiply_fusion
  31.7 19.9 %all_to_all.5 = f32[1,16,32,128]{3,2,0,1:T(8,128)S(1)} all-to-all(f32[1,16,32,128]{3,2,0,1:T(8,128)S(1)} %broadcast_in_dim.2), channel_id=1, replica_groups=mesh['sub'=32,'grp'=16] {'grp'}, dimensions={1} | all-to-all | bytes 524288 | tf_op jit(solution)/shard_map/all_to_all | solution.py:147
  51.5 0.1 slice.25
  51.7 0.1 slice.26
  51.8 0.8 %maximum_bitcast_fusion = f32[1,16,32,96]{3,2,1,0:T(8,128)} fusion(f32[1,16,32,64]{3,2,0,1:T(8,128)S(1)} %slice.26, f32[1,16,32,32]{3,2,0,1:T(8,128)S(1)} %slice_add_fusion), kind=kLoop, calls=%fused_computation.15 | loop fusion | flops 49152 | bytes 393216 | tf_op jit(solution)/shard_map/concatenate | solution.py:149
  (6 shorter events, 0.1 us)
Async XLA Ops:
  8.0 20.9 %copy-start = (bf16[3,32,1024]{2,1,0:T(8,128)(2,1)S(1)}, bf16[3,32,1024]{2,1,0:T(8,128)(2,1)}, u32[]{:S(2)}) copy-start(bf16[3,32,1024]{2,1,0:T(8,128)(2,1)} %get-tuple-element.18) | copy-start | bytes 589828
  8.0 23.2 %copy-start.1 = (bf16[3,16,32,128]{3,2,1,0:T(8,128)(2,1)S(1)}, bf16[3,16,32,128]{3,2,1,0:T(8,128)(2,1)}, u32[]{:S(2)}) copy-start(bf16[3,16,32,128]{3,2,1,0:T(8,128)(2,1)} %get-tuple-element.21) | copy-start | bytes 1179652
  8.0 20.9 %collective-permute-start = (bf16[1024]{0:T(1024)(128)(2,1)S(1)}, bf16[1024]{0:T(1024)(128)(2,1)S(1)}, u32[]{:S(2)}, u32[]{:S(2)}) collective-permute-start(bf16[1024]{0:T(1024)(128)(2,1)S(1)} %slice_bitcast_fusion), channel_id=1, source_target_pairs={{0,16},{16,32},{32,48},{48,64},{64,80},{80,96},{96,112},{112,128},... | collective-permute-start | bytes 6152 | tf_op jit(solution)/shard_map/ppermute | solution.py:12
  10.1 19.8 %collective-permute-start.1 = (bf16[3,32,1024]{2,1,0:T(8,128)(2,1)}, bf16[3,32,1024]{2,1,0:T(8,128)(2,1)S(1)}, u32[]{:S(2)}, u32[]{:S(2)}) collective-permute-start(bf16[3,32,1024]{2,1,0:T(8,128)(2,1)} %get-tuple-element.18), channel_id=1, source_target_pairs={{16,0},{32,16},{48,32},{64,48},{80,64},{96,80},{112,96},{128,112},... | collective-permute-start | bytes 589832 | tf_op jit(solution)/shard_map/ppermute | solution.py:12
  20.4 10.6 %collective-permute-start.2 = (bf16[3,16,32,128]{3,2,1,0:T(8,128)(2,1)}, bf16[3,16,32,128]{3,2,1,0:T(8,128)(2,1)S(1)}, u32[]{:S(2)}, u32[]{:S(2)}) collective-permute-start(bf16[3,16,32,128]{3,2,1,0:T(8,128)(2,1)} %get-tuple-element.22), channel_id=1, source_target_pairs={{1,0},{2,1},{3,2},{4,3},{5,4},{6,5},{7,6},{8,7},{9,8},{10,9},{11,1... | collective-permute-start | bytes 1179656 | tf_op jit(solution)/shard_map/ppermute | solution.py:12

commit v16 on v15

--- a/solution.py
+++ b/solution.py
@@ -25,7 +25,7 @@
     return (weight.astype(jnp.float32) * values.astype(jnp.float32)).astype(jnp.bfloat16)
 
 
-def turn_kernel(depth_ref, defl_ref, live_ref, low_ref, high_ref, first_ref):
+def turn_kernel(depth_ref, defl_ref, low_ref, high_ref, first_ref, last_ref):
     count, comps, rows, cols, depth = defl_ref.shape
     lane = lax.broadcasted_iota(jnp.int32, (count, cols, depth), 2)
     live_mask = (lane < depth_ref[0]).astype(jnp.bfloat16)
@@ -34,8 +34,6 @@
         for comp in range(comps):
             tiles = (defl_ref[:, comp, row] * live_mask).astype(jnp.float32)
             turned = pltpu.einshape("kyz->ykz", tiles).astype(jnp.bfloat16)
-            for col in range(cols):
-                live_ref[comp, row, :, pl.ds(col * depth, depth)] = turned[col]
             low_ref[comp, row] = turned[0]
             high_ref[comp, row] = turned[cols - 1]
 
@@ -44,16 +42,29 @@
                 for col in range(cols):
                     first_ref[comp, :, pl.ds(col * depth, depth)] = turned[col]
 
+            @pl.when(row == rows - 1)
+            def _():
+                for col in range(cols):
+                    last_ref[comp, :, pl.ds(col * depth, depth)] = turned[col]
+
         return carry
 
     lax.fori_loop(0, rows, body, 0, unroll=4)
 
 
-def local_kernel(live_ref, coeff_ref, out_ref):
-    comps, rows, count, width = live_ref.shape
-    cols, depth = coeff_ref.shape[2:]
-    lane = lax.broadcasted_iota(jnp.int32, (count, width), 1)
-    last_z = (lane & (depth - 1)) == depth - 1
+def local_kernel(depth_ref, defl_ref, coeff_ref, out_ref):
+    count, comps, rows, cols, depth = defl_ref.shape
+    width = cols * depth
+    lane = lax.broadcasted_iota(jnp.int32, (count, cols, depth), 2)
+    live_mask = (lane < depth_ref[0]).astype(jnp.bfloat16)
+    wide_lane = lax.broadcasted_iota(jnp.int32, (count, width), 1)
+    last_z = (wide_lane & (depth - 1)) == depth - 1
+    zero_slab = jnp.zeros((count, depth), jnp.float32)
+
+    def flat(row, comp):
+        tiles = (defl_ref[:, comp, row] * live_mask).astype(jnp.float32)
+        turned = pltpu.einshape("kyz->ykz", tiles)
+        return jnp.concatenate([turned[col] for col in range(cols)], axis=1).astype(jnp.bfloat16)
 
     def weight(entry, row):
         w = coeff_ref[entry, row]
@@ -65,8 +76,8 @@
         w = [weight(e, row) for e in range(4)]
         lefts, rights = [], []
         for comp in range(comps):
-            live = live_ref[comp, row]
-            next_x = jnp.where(has_next, live_ref[comp, following_row], 0)
+            live = flat(row, comp)
+            next_x = jnp.where(has_next, flat(following_row, comp), 0)
             next_y = jnp.concatenate([live[:, depth:], jnp.zeros_like(live[:, :depth])], axis=1)
             next_z = jnp.where(last_z, 0, pltpu.roll(live, width - 1, 1))
             step_x = live - next_x
@@ -88,30 +99,30 @@
     return pl.pallas_call(
         turn_kernel,
         out_shape=(
-            jax.ShapeDtypeStruct((comps, rows, count, cols * depth), jnp.bfloat16),
             jax.ShapeDtypeStruct((comps, rows, count, depth), jnp.bfloat16),
             jax.ShapeDtypeStruct((comps, rows, count, depth), jnp.bfloat16),
+            jax.ShapeDtypeStruct((comps, count, cols * depth), jnp.bfloat16),
             jax.ShapeDtypeStruct((comps, count, cols * depth), jnp.bfloat16),
         ),
         in_specs=[pl.BlockSpec(memory_space=pltpu.SMEM), pl.BlockSpec(memory_space=pltpu.VMEM)],
         out_specs=(pl.BlockSpec(memory_space=pltpu.VMEM),) * 4,
-        cost_estimate=pl.CostEstimate(flops=0, bytes_accessed=deflation.size * 5, transcendentals=0),
+        cost_estimate=pl.CostEstimate(flops=0, bytes_accessed=deflation.size * 3, transcendentals=0),
     )(depths, deflation)
 
 
-def local_terms(live_t, coefficients):
-    count = live_t.shape[2]
+def local_terms(deflation, coefficients, depths):
+    count = deflation.shape[0]
     return pl.pallas_call(
         local_kernel,
         out_shape=jax.ShapeDtypeStruct((count, count), jnp.float32),
-        in_specs=[pl.BlockSpec(memory_space=pltpu.VMEM)] * 2,
+        in_specs=[pl.BlockSpec(memory_space=pltpu.SMEM)] + [pl.BlockSpec(memory_space=pltpu.VMEM)] * 2,
         out_specs=pl.BlockSpec(memory_space=pltpu.VMEM),
         cost_estimate=pl.CostEstimate(
-            flops=2 * 4 * count * live_t.size,
-            bytes_accessed=live_t.size * 2 + coefficients.size * 2,
+            flops=2 * 4 * count * deflation.size,
+            bytes_accessed=deflation.size * 2 + coefficients.size * 2,
             transcendentals=0,
         ),
-    )(live_t, coefficients)
+    )(depths, deflation, coefficients)
 
 
 def face_gram(left_side, right_side):
@@ -125,17 +136,16 @@
 def shards(deflation, stiffness, depths):
     cell_count = deflation.shape[2] * deflation.shape[3] * deflation.shape[4]
     normalizer = 1.0 / (24.0 * cell_count)
-    live_t, bottom_y, top_y, bottom_x = turned_field(deflation, depths)
+    bottom_y, top_y, bottom_x, top_x = turned_field(deflation, depths)
     weight_top_x = stiffness[1, -1].reshape(-1)
     weight_top_y = stiffness[2, :, -1]
-    live_t, bottom_y, bottom_x, weight_top_x, weight_top_y = lax.optimization_barrier(
-        (live_t, bottom_y, bottom_x, weight_top_x, weight_top_y)
+    bottom_y, bottom_x, weight_top_x, weight_top_y = lax.optimization_barrier(
+        (bottom_y, bottom_x, weight_top_x, weight_top_y)
     )
     next_y = from_behind(bottom_y, "grp", -1)
     next_x = from_behind(bottom_x, "sub", -1)
     weight_low_x = from_behind(weight_top_x, "sub", 1)
-    diagonal_block = local_terms(live_t, stiffness)
-    top_x = live_t[:, -1]
+    diagonal_block = local_terms(deflation, stiffness, depths)
     coupling_x = -layer_gram(weighted(weight_top_x, top_x), next_x)
     coupling_y = -face_gram(weighted(weight_top_y[None, :, None], top_y), next_y)
     diagonal_block = diagonal_block + layer_gram(bottom_x, weighted(weight_low_x, bottom_x))

time: 53.1 us -> 53.2 us (level)
  Pallas kernels: 12 us -> 13 us
  matrix products: 2.53 us -> 1.59 us
    pallas_call x1, Pallas kernels: 6.11 us -> 8.1 us  [local_terms(): pl.pallas_call(local_kernel, out_shape=jax.ShapeDtypeStruct((count, count...]
    pallas_call x1, Pallas kernels: 5.9 us -> 4.94 us  [turned_field(): pl.pallas_call(turn_kernel, out_shape=(jax.ShapeDtypeStruct((comps, rows,...]
    dot_general x2, matrix products: 2.02 us -> 1.08 us  [layer_gram(): jnp.einsum('ckj,clj->kl', left_side, right_side, preferred_element_type=j...]
  transfers between devices with their start and end apart: 3 -> 3, of which waited for: 0 -> 0; matrix products, arithmetic and copies ran while one was open for 4% -> 2% of each run, Pallas kernels for 12% -> 15%
where the time goes in v16:
time: 53.2 us; the launch traced here: 52.8 us
  blocking collectives  19.9 us (37%)
  starting transfers between devices  14.8 us (28%)
  Pallas kernels  13 us (24%)
  local copies, waits for them, and re-layouts  1.75 us (3%)
  matrix products  1.59 us (3%)
  other arithmetic  0.98 us (2%)
  between operations  0.77 us (1%)
    all_to_all x1, blocking collectives, shards(): gathered = lax.all_to_all(copies, 'grp', 1, 1, tiled=True)  19.9 us
    ppermute x3, starting transfers between devices, from_behind(): return lax.ppermute(x, axis, pairs)  14.8 us
    pallas_call x1, Pallas kernels, local_terms(): pl.pallas_call(local_kernel, out_shape=jax.ShapeDtypeStruct((count, count...  8.1 us
    pallas_call x1, Pallas kernels, turned_field(): pl.pallas_call(turn_kernel, out_shape=(jax.ShapeDtypeStruct((comps, rows,...  4.94 us
    dot_general x2, matrix products, layer_gram(): jnp.einsum('ckj,clj->kl', left_side, right_side, preferred_element_type=j...  1.08 us
  transfers between devices with their start and end apart: 3, of which 0 were waited for; matrix products, arithmetic and copies ran while one was open for 2% of the time, Pallas kernels for 15%

profile of v16, /device:TPU:10, one launch (start us, length us, event | category | flops | bytes accessed | tf_op | source)
XLA Modules:
  0.0 52.8 jit_solution(3299422886564484498)
XLA Ops:
  0.0 0.8 %slice.16 = bf16[1,16,1,128]{3,2,1,0:T(2,128)(2,1)S(1)} slice(bf16[4,16,8,128]{3,2,1,0:T(8,128)(2,1)} %coeff_ref.1), slice={[2:3], [0:16], [7:8], [0:128]} | slice | bytes 8192 | tf_op jit(solution)/shard_map/slice | solution.py:141
  0.8 0.7 %slice_bitcast_fusion = bf16[1024]{0:T(1024)(128)(2,1)S(1)} fusion(bf16[4,16,8,128]{3,2,1,0:T(8,128)(2,1)} %coeff_ref.1), kind=kLoop, calls=%fused_computation.19 | loop fusion | bytes 4096 | tf_op jit(solution)/shard_map/reshape;squeeze | solution.py:140
  2.1 4.9 %shard_map.38 = (bf16[3,16,32,128]{3,2,1,0:T(8,128)(2,1)}, bf16[3,16,32,128]{3,2,1,0:T(8,128)(2,1)}, bf16[3,32,1024]{2,1,0:T(8,128)(2,1)}, bf16[3,32,1024]{2,1,0:T(8,128)(2,1)}) custom-call(s32[1]{0:T(128)S(6)} %copy.12.depth_ref, bf16[32,3,16,8,128]{4,3,2,1,0:T(8,128)(2,1)} %defl_ref.3), custom_call_target="tpu_custom_call" | custom-call | bytes 4718592 | tf_op jit(solution)/shard_map/pallas_call | solution.py:99
  7.1 0.0 copy-start
  7.1 0.0 copy-start.2
  7.1 0.0 copy-start.1
  7.1 10.5 %collective-permute-start.1 = (bf16[3,32,1024]{2,1,0:T(8,128)(2,1)}, bf16[3,32,1024]{2,1,0:T(8,128)(2,1)S(1)}, u32[]{:S(2)}, u32[]{:S(2)}) collective-permute-start(bf16[3,32,1024]{2,1,0:T(8,128)(2,1)} %get-tuple-element.15), channel_id=1, source_target_pairs={{16,0},{32,16},{48,32},{64,48},{80,64},{96,80},{112,96},{128,112},... | collective-permute-start | bytes 589832 | tf_op jit(solution)/shard_map/ppermute | solution.py:12
  17.6 2.4 %collective-permute-start.2 = (bf16[3,16,32,128]{3,2,1,0:T(8,128)(2,1)}, bf16[3,16,32,128]{3,2,1,0:T(8,128)(2,1)S(1)}, u32[]{:S(2)}, u32[]{:S(2)}) collective-permute-start(bf16[3,16,32,128]{3,2,1,0:T(8,128)(2,1)} %get-tuple-element.20), channel_id=1, source_target_pairs={{1,0},{2,1},{3,2},{4,3},{5,4},{6,5},{7,6},{8,7},{9,8},{10,9},{11,1... | collective-permute-start | bytes 1179656 | tf_op jit(solution)/shard_map/ppermute | solution.py:12
  19.9 1.9 %collective-permute-start = (bf16[1024]{0:T(1024)(128)(2,1)S(1)}, bf16[1024]{0:T(1024)(128)(2,1)S(1)}, u32[]{:S(2)}, u32[]{:S(2)}) collective-permute-start(bf16[1024]{0:T(1024)(128)(2,1)S(1)} %slice_bitcast_fusion), channel_id=1, source_target_pairs={{0,16},{16,32},{32,48},{48,64},{64,80},{80,96},{96,112},{112,128},... | collective-permute-start | bytes 6152 | tf_op jit(solution)/shard_map/ppermute | solution.py:12
  21.9 8.1 %shard_map.37 = f32[32,32]{1,0:T(8,128)} custom-call(s32[1]{0:T(128)S(6)} %copy.12.depth_ref, bf16[32,3,16,8,128]{4,3,2,1,0:T(8,128)(2,1)} %defl_ref.3, bf16[4,16,8,128]{3,2,1,0:T(8,128)(2,1)} %coeff_ref.1), custom_call_target="tpu_custom_call" | custom-call | flops 402653184 | bytes 3276800 | tf_op jit(solution)/shard_map/pallas_call | solution.py:115
  30.0 0.0 collective-permute-done
  30.0 0.0 copy-done
  30.0 0.9 %fusion.2 = f32[32,32]{1,0:T(8,128)S(1)} fusion(f32[32,32]{1,0:T(8,128)} %shard_map.37, bf16[3,32,1024]{2,1,0:T(8,128)(2,1)S(1)} %copy-done, f32[1024]{0:T(1024)S(1)} %convert_element_type.37), kind=kOutput, calls=%fused_computation.6 | convolution fusion | flops 6587392 | bytes 208896 | tf_op jit(solution)/shard_map/ckj,clj->kl/dot_general | solution.py:133
  30.9 0.0 collective-permute-done.1
  30.9 0.0 copy-done.2
  30.9 0.2 fusion.1
  31.1 0.0 collective-permute-done.2
  31.1 0.2 convolution_bitcast_fusion
  31.4 0.0 copy-done.1
  31.4 0.3 fusion
  31.6 0.1 maximum_multiply_fusion
  31.8 19.9 %all_to_all.5 = f32[1,16,32,128]{3,2,0,1:T(8,128)S(1)} all-to-all(f32[1,16,32,128]{3,2,0,1:T(8,128)S(1)} %broadcast_in_dim.2), channel_id=1, replica_groups=mesh['sub'=32,'grp'=16] {'grp'}, dimensions={1} | all-to-all | bytes 524288 | tf_op jit(solution)/shard_map/all_to_all | solution.py:157
  51.6 0.1 slice.21
  51.8 0.1 slice.22
  52.0 0.8 %maximum_bitcast_fusion = f32[1,16,32,96]{3,2,1,0:T(8,128)} fusion(f32[1,16,32,64]{3,2,0,1:T(8,128)S(1)} %slice.22, f32[1,16,32,32]{3,2,0,1:T(8,128)S(1)} %slice_add_fusion), kind=kLoop, calls=%fused_computation.14 | loop fusion | flops 49152 | bytes 393216 | tf_op jit(solution)/shard_map/concatenate | solution.py:159
  (6 shorter events, 0.1 us)
Async XLA Ops:
  7.1 22.9 %copy-start = (bf16[3,32,1024]{2,1,0:T(8,128)(2,1)S(1)}, bf16[3,32,1024]{2,1,0:T(8,128)(2,1)}, u32[]{:S(2)}) copy-start(bf16[3,32,1024]{2,1,0:T(8,128)(2,1)} %get-tuple-element.15) | copy-start | bytes 589828
  7.1 23.8 %copy-start.2 = (bf16[3,32,1024]{2,1,0:T(8,128)(2,1)S(1)}, bf16[3,32,1024]{2,1,0:T(8,128)(2,1)}, u32[]{:S(2)}) copy-start(bf16[3,32,1024]{2,1,0:T(8,128)(2,1)} %get-tuple-element.17) | copy-start | bytes 589828
  7.1 24.3 %copy-start.1 = (bf16[3,16,32,128]{3,2,1,0:T(8,128)(2,1)S(1)}, bf16[3,16,32,128]{3,2,1,0:T(8,128)(2,1)}, u32[]{:S(2)}) copy-start(bf16[3,16,32,128]{3,2,1,0:T(8,128)(2,1)} %get-tuple-element.19) | copy-start | bytes 1179652
  7.1 23.8 %collective-permute-start.1 = (bf16[3,32,1024]{2,1,0:T(8,128)(2,1)}, bf16[3,32,1024]{2,1,0:T(8,128)(2,1)S(1)}, u32[]{:S(2)}, u32[]{:S(2)}) collective-permute-start(bf16[3,32,1024]{2,1,0:T(8,128)(2,1)} %get-tuple-element.15), channel_id=1, source_target_pairs={{16,0},{32,16},{48,32},{64,48},{80,64},{96,80},{112,96},{128,112},... | collective-permute-start | bytes 589832 | tf_op jit(solution)/shard_map/ppermute | solution.py:12
  17.6 13.6 %collective-permute-start.2 = (bf16[3,16,32,128]{3,2,1,0:T(8,128)(2,1)}, bf16[3,16,32,128]{3,2,1,0:T(8,128)(2,1)S(1)}, u32[]{:S(2)}, u32[]{:S(2)}) collective-permute-start(bf16[3,16,32,128]{3,2,1,0:T(8,128)(2,1)} %get-tuple-element.20), channel_id=1, source_target_pairs={{1,0},{2,1},{3,2},{4,3},{5,4},{6,5},{7,6},{8,7},{9,8},{10,9},{11,1... | collective-permute-start | bytes 1179656 | tf_op jit(solution)/shard_map/ppermute | solution.py:12
  19.9 10.0 %collective-permute-start = (bf16[1024]{0:T(1024)(128)(2,1)S(1)}, bf16[1024]{0:T(1024)(128)(2,1)S(1)}, u32[]{:S(2)}, u32[]{:S(2)}) collective-permute-start(bf16[1024]{0:T(1024)(128)(2,1)S(1)} %slice_bitcast_fusion), channel_id=1, source_target_pairs={{0,16},{16,32},{32,48},{48,64},{64,80},{80,96},{96,112},{112,128},... | collective-permute-start | bytes 6152 | tf_op jit(solution)/shard_map/ppermute | solution.py:12

commit v17 on v16

--- a/solution.py
+++ b/solution.py
@@ -139,9 +139,7 @@
     bottom_y, top_y, bottom_x, top_x = turned_field(deflation, depths)
     weight_top_x = stiffness[1, -1].reshape(-1)
     weight_top_y = stiffness[2, :, -1]
-    bottom_y, bottom_x, weight_top_x, weight_top_y = lax.optimization_barrier(
-        (bottom_y, bottom_x, weight_top_x, weight_top_y)
-    )
+    bottom_y, bottom_x, weight_top_y = lax.optimization_barrier((bottom_y, bottom_x, weight_top_y))
     next_y = from_behind(bottom_y, "grp", -1)
     next_x = from_behind(bottom_x, "sub", -1)
     weight_low_x = from_behind(weight_top_x, "sub", 1)

time: 53.2 us -> 53.2 us (level)
  other arithmetic: 0.98 us -> 1.66 us
  local copies, waits for them, and re-layouts: 1.75 us -> 1.07 us
    another operation x1 -> x0, local copies, waits for them, and re-layouts: 0.69 us -> none  [shards(): weight_top_x = stiffness[1, -1].reshape(-1)]
    another operation x0 -> x1, other arithmetic: none -> 0.68 us  [shards(): weight_top_x = stiffness[1, -1].reshape(-1)]
  transfers between devices with their start and end apart: 3 -> 3, of which waited for: 0 -> 0; matrix products, arithmetic and copies ran while one was open for 2% -> 4% of each run, Pallas kernels for 15% -> 25%
where the time goes in v17:
time: 53.2 us; the launch traced here: 52.8 us
  blocking collectives  19.9 us (37%)
  starting transfers between devices  14.8 us (28%)
  Pallas kernels  13 us (24%)
  other arithmetic  1.66 us (3%)
  matrix products  1.6 us (3%)
  local copies, waits for them, and re-layouts  1.07 us (2%)
  between operations  0.76 us (1%)
    all_to_all x1, blocking collectives, shards(): gathered = lax.all_to_all(copies, 'grp', 1, 1, tiled=True)  19.9 us
    ppermute x3, starting transfers between devices, from_behind(): return lax.ppermute(x, axis, pairs)  14.8 us
    pallas_call x1, Pallas kernels, local_terms(): pl.pallas_call(local_kernel, out_shape=jax.ShapeDtypeStruct((count, count...  8.11 us
    pallas_call x1, Pallas kernels, turned_field(): pl.pallas_call(turn_kernel, out_shape=(jax.ShapeDtypeStruct((comps, rows,...  4.94 us
    dot_general x2, matrix products, layer_gram(): jnp.einsum('ckj,clj->kl', left_side, right_side, preferred_element_type=j...  1.08 us
  transfers between devices with their start and end apart: 3, of which 0 were waited for; matrix products, arithmetic and copies ran while one was open for 4% of the time, Pallas kernels for 25%

profile of v17, /device:TPU:10, one launch (start us, length us, event | category | flops | bytes accessed | tf_op | source)
XLA Modules:
  0.0 52.8 jit_solution(14312111028170993440)
XLA Ops:
  0.0 0.7 %slice_bitcast_fusion = (bf16[1024]{0:T(1024)(128)(2,1)S(1)}, f32[1024]{0:T(1024)S(1)}) fusion(bf16[4,16,8,128]{3,2,1,0:T(8,128)(2,1)} %coeff_ref.1), kind=kLoop, calls=%fused_computation.19 | loop fusion | flops 1024 | bytes 8192 | tf_op jit(solution)/shard_map/reshape;squeeze | solution.py:140
  0.7 1.9 %collective-permute-start = (bf16[1024]{0:T(1024)(128)(2,1)S(1)}, bf16[1024]{0:T(1024)(128)(2,1)S(1)}, u32[]{:S(2)}, u32[]{:S(2)}) collective-permute-start(bf16[1024]{0:T(1024)(128)(2,1)S(1)} %get-tuple-element.19), channel_id=1, source_target_pairs={{0,16},{16,32},{32,48},{48,64},{64,80},{80,96},{96,112},{112,128},... | collective-permute-start | bytes 6152 | tf_op jit(solution)/shard_map/ppermute | solution.py:12
  2.6 0.8 %slice.15 = bf16[1,16,1,128]{3,2,1,0:T(2,128)(2,1)S(1)} slice(bf16[4,16,8,128]{3,2,1,0:T(8,128)(2,1)} %coeff_ref.1), slice={[2:3], [0:16], [7:8], [0:128]} | slice | bytes 8192 | tf_op jit(solution)/shard_map/slice | solution.py:141
  4.0 4.9 %shard_map.38 = (bf16[3,16,32,128]{3,2,1,0:T(8,128)(2,1)}, bf16[3,16,32,128]{3,2,1,0:T(8,128)(2,1)}, bf16[3,32,1024]{2,1,0:T(8,128)(2,1)}, bf16[3,32,1024]{2,1,0:T(8,128)(2,1)}) custom-call(s32[1]{0:T(128)S(6)} %copy.12.depth_ref, bf16[32,3,16,8,128]{4,3,2,1,0:T(8,128)(2,1)} %defl_ref.3), custom_call_target="tpu_custom_call" | custom-call | bytes 4718592 | tf_op jit(solution)/shard_map/pallas_call | solution.py:99
  9.0 0.0 copy-start
  9.0 0.0 copy-start.2
  9.0 0.0 copy-start.1
  9.0 10.5 %collective-permute-start.1 = (bf16[3,32,1024]{2,1,0:T(8,128)(2,1)}, bf16[3,32,1024]{2,1,0:T(8,128)(2,1)S(1)}, u32[]{:S(2)}, u32[]{:S(2)}) collective-permute-start(bf16[3,32,1024]{2,1,0:T(8,128)(2,1)} %get-tuple-element.14), channel_id=1, source_target_pairs={{16,0},{32,16},{48,32},{64,48},{80,64},{96,80},{112,96},{128,112},... | collective-permute-start | bytes 589832 | tf_op jit(solution)/shard_map/ppermute | solution.py:12
  19.5 2.4 %collective-permute-start.2 = (bf16[3,16,32,128]{3,2,1,0:T(8,128)(2,1)}, bf16[3,16,32,128]{3,2,1,0:T(8,128)(2,1)S(1)}, u32[]{:S(2)}, u32[]{:S(2)}) collective-permute-start(bf16[3,16,32,128]{3,2,1,0:T(8,128)(2,1)} %get-tuple-element.18), channel_id=1, source_target_pairs={{1,0},{2,1},{3,2},{4,3},{5,4},{6,5},{7,6},{8,7},{9,8},{10,9},{11,1... | collective-permute-start | bytes 1179656 | tf_op jit(solution)/shard_map/ppermute | solution.py:12
  21.8 8.1 %shard_map.37 = f32[32,32]{1,0:T(8,128)} custom-call(s32[1]{0:T(128)S(6)} %copy.12.depth_ref, bf16[32,3,16,8,128]{4,3,2,1,0:T(8,128)(2,1)} %defl_ref.3, bf16[4,16,8,128]{3,2,1,0:T(8,128)(2,1)} %coeff_ref.1), custom_call_target="tpu_custom_call" | custom-call | flops 402653184 | bytes 3276800 | tf_op jit(solution)/shard_map/pallas_call | solution.py:115
  30.0 0.0 collective-permute-done
  30.0 0.0 copy-done
  30.0 0.9 %fusion.2 = f32[32,32]{1,0:T(8,128)S(1)} fusion(f32[32,32]{1,0:T(8,128)} %shard_map.37, bf16[3,32,1024]{2,1,0:T(8,128)(2,1)S(1)} %copy-done, f32[1024]{0:T(1024)S(1)} %convert_element_type.41), kind=kOutput, calls=%fused_computation.6 | convolution fusion | flops 6587392 | bytes 208896 | tf_op jit(solution)/shard_map/ckj,clj->kl/dot_general | solution.py:133
  30.9 0.0 collective-permute-done.1
  30.9 0.0 copy-done.2
  30.9 0.2 fusion.1
  31.1 0.0 collective-permute-done.2
  31.1 0.2 convolution_bitcast_fusion
  31.4 0.0 copy-done.1
  31.4 0.3 fusion
  31.6 0.1 maximum_multiply_fusion
  31.8 19.9 %all_to_all.5 = f32[1,16,32,128]{3,2,0,1:T(8,128)S(1)} all-to-all(f32[1,16,32,128]{3,2,0,1:T(8,128)S(1)} %broadcast_in_dim.2), channel_id=1, replica_groups=mesh['sub'=32,'grp'=16] {'grp'}, dimensions={1} | all-to-all | bytes 524288 | tf_op jit(solution)/shard_map/all_to_all | solution.py:155
  51.6 0.1 slice.21
  51.7 0.1 slice.22
  51.9 0.8 %maximum_bitcast_fusion = f32[1,16,32,96]{3,2,1,0:T(8,128)} fusion(f32[1,16,32,64]{3,2,0,1:T(8,128)S(1)} %slice.22, f32[1,16,32,32]{3,2,0,1:T(8,128)S(1)} %slice_add_fusion), kind=kLoop, calls=%fused_computation.14 | loop fusion | flops 49152 | bytes 393216 | tf_op jit(solution)/shard_map/concatenate | solution.py:157
  (5 shorter events, 0.1 us)
Async XLA Ops:
  0.7 29.3 %collective-permute-start = (bf16[1024]{0:T(1024)(128)(2,1)S(1)}, bf16[1024]{0:T(1024)(128)(2,1)S(1)}, u32[]{:S(2)}, u32[]{:S(2)}) collective-permute-start(bf16[1024]{0:T(1024)(128)(2,1)S(1)} %get-tuple-element.19), channel_id=1, source_target_pairs={{0,16},{16,32},{32,48},{48,64},{64,80},{80,96},{96,112},{112,128},... | collective-permute-start | bytes 6152 | tf_op jit(solution)/shard_map/ppermute | solution.py:12
  9.0 21.0 %copy-start = (bf16[3,32,1024]{2,1,0:T(8,128)(2,1)S(1)}, bf16[3,32,1024]{2,1,0:T(8,128)(2,1)}, u32[]{:S(2)}) copy-start(bf16[3,32,1024]{2,1,0:T(8,128)(2,1)} %get-tuple-element.14) | copy-start | bytes 589828
  9.0 21.9 %copy-start.2 = (bf16[3,32,1024]{2,1,0:T(8,128)(2,1)S(1)}, bf16[3,32,1024]{2,1,0:T(8,128)(2,1)}, u32[]{:S(2)}) copy-start(bf16[3,32,1024]{2,1,0:T(8,128)(2,1)} %get-tuple-element.15) | copy-start | bytes 589828
  9.0 22.4 %copy-start.1 = (bf16[3,16,32,128]{3,2,1,0:T(8,128)(2,1)S(1)}, bf16[3,16,32,128]{3,2,1,0:T(8,128)(2,1)}, u32[]{:S(2)}) copy-start(bf16[3,16,32,128]{3,2,1,0:T(8,128)(2,1)} %get-tuple-element.17) | copy-start | bytes 1179652
  9.0 21.9 %collective-permute-start.1 = (bf16[3,32,1024]{2,1,0:T(8,128)(2,1)}, bf16[3,32,1024]{2,1,0:T(8,128)(2,1)S(1)}, u32[]{:S(2)}, u32[]{:S(2)}) collective-permute-start(bf16[3,32,1024]{2,1,0:T(8,128)(2,1)} %get-tuple-element.14), channel_id=1, source_target_pairs={{16,0},{32,16},{48,32},{64,48},{80,64},{96,80},{112,96},{128,112},... | collective-permute-start | bytes 589832 | tf_op jit(solution)/shard_map/ppermute | solution.py:12
  19.5 11.6 %collective-permute-start.2 = (bf16[3,16,32,128]{3,2,1,0:T(8,128)(2,1)}, bf16[3,16,32,128]{3,2,1,0:T(8,128)(2,1)S(1)}, u32[]{:S(2)}, u32[]{:S(2)}) collective-permute-start(bf16[3,16,32,128]{3,2,1,0:T(8,128)(2,1)} %get-tuple-element.18), channel_id=1, source_target_pairs={{1,0},{2,1},{3,2},{4,3},{5,4},{6,5},{7,6},{8,7},{9,8},{10,9},{11,1... | collective-permute-start | bytes 1179656 | tf_op jit(solution)/shard_map/ppermute | solution.py:12

commit v18 on v15

--- a/solution.py
+++ b/solution.py
@@ -46,7 +46,7 @@
 
         return carry
 
-    lax.fori_loop(0, rows, body, 0, unroll=4)
+    lax.fori_loop(0, rows, body, 0, unroll=rows)
 
 
 def local_kernel(live_ref, coeff_ref, out_ref):
@@ -80,7 +80,7 @@
             left, right, (((1,), (1,)), ((), ())), preferred_element_type=jnp.float32
         )
 
-    out_ref[...] = lax.fori_loop(0, rows, body, jnp.zeros((count, count), jnp.float32), unroll=8)
+    out_ref[...] = lax.fori_loop(0, rows, body, jnp.zeros((count, count), jnp.float32), unroll=rows)
 
 
 def turned_field(deflation, depths):

time: 53.1 us -> 52.7 us (level)
  transfers between devices with their start and end apart: 3 -> 3, of which waited for: 0 -> 0; matrix products, arithmetic and copies ran while one was open for 4% -> 4% of each run, Pallas kernels for 12% -> 11%
where the time goes in v18:
time: 52.7 us; the launch traced here: 52.3 us
  blocking collectives  19.9 us (38%)
  starting transfers between devices  14.8 us (28%)
  Pallas kernels  11.6 us (22%)
  matrix products  2.53 us (5%)
  local copies, waits for them, and re-layouts  1.75 us (3%)
  other arithmetic  0.98 us (2%)
  between operations  0.76 us (1%)
    all_to_all x1, blocking collectives, shards(): gathered = lax.all_to_all(copies, 'grp', 1, 1, tiled=True)  19.9 us
    ppermute x3, starting transfers between devices, from_behind(): return lax.ppermute(x, axis, pairs)  14.8 us
    pallas_call x1, Pallas kernels, local_terms(): pl.pallas_call(local_kernel, out_shape=jax.ShapeDtypeStruct((count, count...  5.95 us
    pallas_call x1, Pallas kernels, turned_field(): pl.pallas_call(turn_kernel, out_shape=(jax.ShapeDtypeStruct((comps, rows,...  5.63 us
    dot_general x2, matrix products, layer_gram(): jnp.einsum('ckj,clj->kl', left_side, right_side, preferred_element_type=j...  2.02 us
  transfers between devices with their start and end apart: 3, of which 0 were waited for; matrix products, arithmetic and copies ran while one was open for 4% of the time, Pallas kernels for 11%

profile of v18, /device:TPU:10, one launch (start us, length us, event | category | flops | bytes accessed | tf_op | source)
XLA Modules:
  0.0 52.3 jit_solution(2995006271603854508)
XLA Ops:
  0.0 0.8 %slice.19 = bf16[1,16,1,128]{3,2,1,0:T(2,128)(2,1)S(1)} slice(bf16[4,16,8,128]{3,2,1,0:T(8,128)(2,1)} %coeff_ref.1), slice={[2:3], [0:16], [7:8], [0:128]} | slice | bytes 8192 | tf_op jit(solution)/shard_map/slice | solution.py:130
  0.8 0.7 %slice_bitcast_fusion = bf16[1024]{0:T(1024)(128)(2,1)S(1)} fusion(bf16[4,16,8,128]{3,2,1,0:T(8,128)(2,1)} %coeff_ref.1), kind=kLoop, calls=%fused_computation.22 | loop fusion | bytes 4096 | tf_op jit(solution)/shard_map/reshape;squeeze | solution.py:129
  2.1 5.6 %shard_map.37 = (bf16[3,16,32,1024]{3,2,1,0:T(8,128)(2,1)}, bf16[3,16,32,128]{3,2,1,0:T(8,128)(2,1)}, bf16[3,16,32,128]{3,2,1,0:T(8,128)(2,1)}, bf16[3,32,1024]{2,1,0:T(8,128)(2,1)}) custom-call(s32[1]{0:T(128)S(6)} %copy.12.depth_ref, bf16[32,3,16,8,128]{4,3,2,1,0:T(8,128)(2,1)} %defl_ref.1), custom_call_target="tpu_custom_call" | custom-call | bytes 7864320 | tf_op jit(solution)/shard_map/pallas_call | solution.py:88
  7.8 0.0 copy-start
  7.8 0.0 copy-start.1
  7.8 2.0 %collective-permute-start = (bf16[1024]{0:T(1024)(128)(2,1)S(1)}, bf16[1024]{0:T(1024)(128)(2,1)S(1)}, u32[]{:S(2)}, u32[]{:S(2)}) collective-permute-start(bf16[1024]{0:T(1024)(128)(2,1)S(1)} %slice_bitcast_fusion), channel_id=1, source_target_pairs={{0,16},{16,32},{32,48},{48,64},{64,80},{80,96},{96,112},{112,128},... | collective-permute-start | bytes 6152 | tf_op jit(solution)/shard_map/ppermute | solution.py:12
  9.8 10.4 %collective-permute-start.1 = (bf16[3,32,1024]{2,1,0:T(8,128)(2,1)}, bf16[3,32,1024]{2,1,0:T(8,128)(2,1)S(1)}, u32[]{:S(2)}, u32[]{:S(2)}) collective-permute-start(bf16[3,32,1024]{2,1,0:T(8,128)(2,1)} %get-tuple-element.18), channel_id=1, source_target_pairs={{16,0},{32,16},{48,32},{64,48},{80,64},{96,80},{112,96},{128,112},... | collective-permute-start | bytes 589832 | tf_op jit(solution)/shard_map/ppermute | solution.py:12
  20.2 2.4 %collective-permute-start.2 = (bf16[3,16,32,128]{3,2,1,0:T(8,128)(2,1)}, bf16[3,16,32,128]{3,2,1,0:T(8,128)(2,1)S(1)}, u32[]{:S(2)}, u32[]{:S(2)}) collective-permute-start(bf16[3,16,32,128]{3,2,1,0:T(8,128)(2,1)} %get-tuple-element.22), channel_id=1, source_target_pairs={{1,0},{2,1},{3,2},{4,3},{5,4},{6,5},{7,6},{8,7},{9,8},{10,9},{11,1... | collective-permute-start | bytes 1179656 | tf_op jit(solution)/shard_map/ppermute | solution.py:12
  22.5 6.0 %shard_map.38 = f32[32,32]{1,0:T(8,128)} custom-call(bf16[3,16,32,1024]{3,2,1,0:T(8,128)(2,1)} %get-tuple-element.17.live_ref, bf16[4,16,8,128]{3,2,1,0:T(8,128)(2,1)} %coeff_ref.1), custom_call_target="tpu_custom_call" | custom-call | flops 402653184 | bytes 3276800 | tf_op jit(solution)/shard_map/pallas_call | solution.py:104
  28.5 0.0 collective-permute-done
  28.5 0.0 copy-done
  28.5 0.9 %fusion.2 = f32[32,32]{1,0:T(8,128)S(1)} fusion(f32[32,32]{1,0:T(8,128)} %shard_map.38, bf16[3,32,1024]{2,1,0:T(8,128)(2,1)S(1)} %copy-done, f32[1024]{0:T(1024)S(1)} %convert_element_type.40), kind=kOutput, calls=%fused_computation.6 | convolution fusion | flops 6587392 | bytes 208896 | tf_op jit(solution)/shard_map/ckj,clj->kl/dot_general | solution.py:122
  29.4 0.0 collective-permute-done.1
  29.4 1.1 %fusion.1 = f32[32,32]{1,0:T(8,128)S(1)} fusion(bf16[3,32,1024]{2,1,0:T(8,128)(2,1)S(1)} %collective-permute-done.1, bf16[3,16,32,1024]{3,2,1,0:T(8,128)(2,1)} %get-tuple-element.17.live_ref, f32[1024]{0:T(1024)S(1)} %convert_element_type.43), kind=kOutput, calls=%fused_computation.4 | convolution fusion | flops 6587392 | bytes 401408 | tf_op jit(solution)/shard_map/ckj,clj->kl/dot_general | solution.py:122
  30.6 0.0 collective-permute-done.2
  30.6 0.2 convolution_bitcast_fusion
  30.8 0.0 copy-done.1
  30.8 0.3 fusion
  31.1 0.1 maximum_multiply_fusion
  31.2 19.9 %all_to_all.5 = f32[1,16,32,128]{3,2,0,1:T(8,128)S(1)} all-to-all(f32[1,16,32,128]{3,2,0,1:T(8,128)S(1)} %broadcast_in_dim.2), channel_id=1, replica_groups=mesh['sub'=32,'grp'=16] {'grp'}, dimensions={1} | all-to-all | bytes 524288 | tf_op jit(solution)/shard_map/all_to_all | solution.py:147
  51.1 0.1 slice.25
  51.2 0.1 slice.26
  51.4 0.8 %maximum_bitcast_fusion = f32[1,16,32,96]{3,2,1,0:T(8,128)} fusion(f32[1,16,32,64]{3,2,0,1:T(8,128)S(1)} %slice.26, f32[1,16,32,32]{3,2,0,1:T(8,128)S(1)} %slice_add_fusion), kind=kLoop, calls=%fused_computation.15 | loop fusion | flops 49152 | bytes 393216 | tf_op jit(solution)/shard_map/concatenate | solution.py:149
  (6 shorter events, 0.1 us)
Async XLA Ops:
  7.8 20.8 %copy-start = (bf16[3,32,1024]{2,1,0:T(8,128)(2,1)S(1)}, bf16[3,32,1024]{2,1,0:T(8,128)(2,1)}, u32[]{:S(2)}) copy-start(bf16[3,32,1024]{2,1,0:T(8,128)(2,1)} %get-tuple-element.18) | copy-start | bytes 589828
  7.8 23.1 %copy-start.1 = (bf16[3,16,32,128]{3,2,1,0:T(8,128)(2,1)S(1)}, bf16[3,16,32,128]{3,2,1,0:T(8,128)(2,1)}, u32[]{:S(2)}) copy-start(bf16[3,16,32,128]{3,2,1,0:T(8,128)(2,1)} %get-tuple-element.21) | copy-start | bytes 1179652
  7.8 20.7 %collective-permute-start = (bf16[1024]{0:T(1024)(128)(2,1)S(1)}, bf16[1024]{0:T(1024)(128)(2,1)S(1)}, u32[]{:S(2)}, u32[]{:S(2)}) collective-permute-start(bf16[1024]{0:T(1024)(128)(2,1)S(1)} %slice_bitcast_fusion), channel_id=1, source_target_pairs={{0,16},{16,32},{32,48},{48,64},{64,80},{80,96},{96,112},{112,128},... | collective-permute-start | bytes 6152 | tf_op jit(solution)/shard_map/ppermute | solution.py:12
  9.8 19.6 %collective-permute-start.1 = (bf16[3,32,1024]{2,1,0:T(8,128)(2,1)}, bf16[3,32,1024]{2,1,0:T(8,128)(2,1)S(1)}, u32[]{:S(2)}, u32[]{:S(2)}) collective-permute-start(bf16[3,32,1024]{2,1,0:T(8,128)(2,1)} %get-tuple-element.18), channel_id=1, source_target_pairs={{16,0},{32,16},{48,32},{64,48},{80,64},{96,80},{112,96},{128,112},... | collective-permute-start | bytes 589832 | tf_op jit(solution)/shard_map/ppermute | solution.py:12
  20.2 10.4 %collective-permute-start.2 = (bf16[3,16,32,128]{3,2,1,0:T(8,128)(2,1)}, bf16[3,16,32,128]{3,2,1,0:T(8,128)(2,1)S(1)}, u32[]{:S(2)}, u32[]{:S(2)}) collective-permute-start(bf16[3,16,32,128]{3,2,1,0:T(8,128)(2,1)} %get-tuple-element.22), channel_id=1, source_target_pairs={{1,0},{2,1},{3,2},{4,3},{5,4},{6,5},{7,6},{8,7},{9,8},{10,9},{11,1... | collective-permute-start | bytes 1179656 | tf_op jit(solution)/shard_map/ppermute | solution.py:12

commit v19 on v18

--- a/solution.py
+++ b/solution.py
@@ -32,8 +32,7 @@
 
     def body(row, carry):
         for comp in range(comps):
-            tiles = (defl_ref[:, comp, row] * live_mask).astype(jnp.float32)
-            turned = pltpu.einshape("kyz->ykz", tiles).astype(jnp.bfloat16)
+            turned = pltpu.einshape("kyz->ykz", defl_ref[:, comp, row] * live_mask)
             for col in range(cols):
                 live_ref[comp, row, :, pl.ds(col * depth, depth)] = turned[col]
             low_ref[comp, row] = turned[0]

time: 52.7 us -> 52.1 us (0.989)
  Pallas kernels: 11.6 us -> 11 us
    pallas_call x1, Pallas kernels: 5.63 us -> 5.09 us  [turned_field(): pl.pallas_call(turn_kernel, out_shape=(jax.ShapeDtypeStruct((comps, rows,...]
  transfers between devices with their start and end apart: 3 -> 3, of which waited for: 0 -> 0; matrix products, arithmetic and copies ran while one was open for 4% -> 4% of each run, Pallas kernels for 11% -> 12%
where the time goes in v19:
time: 52.1 us; the launch traced here: 51.7 us
  blocking collectives  19.9 us (38%)
  starting transfers between devices  14.8 us (28%)
  Pallas kernels  11 us (21%)
  matrix products  2.53 us (5%)
  local copies, waits for them, and re-layouts  1.75 us (3%)
  other arithmetic  0.98 us (2%)
  between operations  0.76 us (1%)
    all_to_all x1, blocking collectives, shards(): gathered = lax.all_to_all(copies, 'grp', 1, 1, tiled=True)  19.9 us
    ppermute x3, starting transfers between devices, from_behind(): return lax.ppermute(x, axis, pairs)  14.8 us
    pallas_call x1, Pallas kernels, local_terms(): pl.pallas_call(local_kernel, out_shape=jax.ShapeDtypeStruct((count, count...  5.95 us
    pallas_call x1, Pallas kernels, turned_field(): pl.pallas_call(turn_kernel, out_shape=(jax.ShapeDtypeStruct((comps, rows,...  5.09 us
    dot_general x2, matrix products, layer_gram(): jnp.einsum('ckj,clj->kl', left_side, right_side, preferred_element_type=j...  2.02 us
  transfers between devices with their start and end apart: 3, of which 0 were waited for; matrix products, arithmetic and copies ran while one was open for 4% of the time, Pallas kernels for 12%

profile of v19, /device:TPU:10, one launch (start us, length us, event | category | flops | bytes accessed | tf_op | source)
XLA Modules:
  0.0 51.7 jit_solution(3457947503912178290)
XLA Ops:
  0.0 0.8 %slice.19 = bf16[1,16,1,128]{3,2,1,0:T(2,128)(2,1)S(1)} slice(bf16[4,16,8,128]{3,2,1,0:T(8,128)(2,1)} %coeff_ref.1), slice={[2:3], [0:16], [7:8], [0:128]} | slice | bytes 8192 | tf_op jit(solution)/shard_map/slice | solution.py:129
  0.8 0.7 %slice_bitcast_fusion = bf16[1024]{0:T(1024)(128)(2,1)S(1)} fusion(bf16[4,16,8,128]{3,2,1,0:T(8,128)(2,1)} %coeff_ref.1), kind=kLoop, calls=%fused_computation.22 | loop fusion | bytes 4096 | tf_op jit(solution)/shard_map/reshape;squeeze | solution.py:128
  2.1 5.1 %shard_map.37 = (bf16[3,16,32,1024]{3,2,1,0:T(8,128)(2,1)}, bf16[3,16,32,128]{3,2,1,0:T(8,128)(2,1)}, bf16[3,16,32,128]{3,2,1,0:T(8,128)(2,1)}, bf16[3,32,1024]{2,1,0:T(8,128)(2,1)}) custom-call(s32[1]{0:T(128)S(6)} %copy.12.depth_ref, bf16[32,3,16,8,128]{4,3,2,1,0:T(8,128)(2,1)} %defl_ref.1), custom_call_target="tpu_custom_call" | custom-call | bytes 7864320 | tf_op jit(solution)/shard_map/pallas_call | solution.py:87
  7.2 0.0 copy-start
  7.2 0.0 copy-start.1
  7.2 2.0 %collective-permute-start = (bf16[1024]{0:T(1024)(128)(2,1)S(1)}, bf16[1024]{0:T(1024)(128)(2,1)S(1)}, u32[]{:S(2)}, u32[]{:S(2)}) collective-permute-start(bf16[1024]{0:T(1024)(128)(2,1)S(1)} %slice_bitcast_fusion), channel_id=1, source_target_pairs={{0,16},{16,32},{32,48},{48,64},{64,80},{80,96},{96,112},{112,128},... | collective-permute-start | bytes 6152 | tf_op jit(solution)/shard_map/ppermute | solution.py:12
  9.3 10.4 %collective-permute-start.1 = (bf16[3,32,1024]{2,1,0:T(8,128)(2,1)}, bf16[3,32,1024]{2,1,0:T(8,128)(2,1)S(1)}, u32[]{:S(2)}, u32[]{:S(2)}) collective-permute-start(bf16[3,32,1024]{2,1,0:T(8,128)(2,1)} %get-tuple-element.18), channel_id=1, source_target_pairs={{16,0},{32,16},{48,32},{64,48},{80,64},{96,80},{112,96},{128,112},... | collective-permute-start | bytes 589832 | tf_op jit(solution)/shard_map/ppermute | solution.py:12
  19.6 2.4 %collective-permute-start.2 = (bf16[3,16,32,128]{3,2,1,0:T(8,128)(2,1)}, bf16[3,16,32,128]{3,2,1,0:T(8,128)(2,1)S(1)}, u32[]{:S(2)}, u32[]{:S(2)}) collective-permute-start(bf16[3,16,32,128]{3,2,1,0:T(8,128)(2,1)} %get-tuple-element.22), channel_id=1, source_target_pairs={{1,0},{2,1},{3,2},{4,3},{5,4},{6,5},{7,6},{8,7},{9,8},{10,9},{11,1... | collective-permute-start | bytes 1179656 | tf_op jit(solution)/shard_map/ppermute | solution.py:12
  22.0 6.0 %shard_map.38 = f32[32,32]{1,0:T(8,128)} custom-call(bf16[3,16,32,1024]{3,2,1,0:T(8,128)(2,1)} %get-tuple-element.17.live_ref, bf16[4,16,8,128]{3,2,1,0:T(8,128)(2,1)} %coeff_ref.1), custom_call_target="tpu_custom_call" | custom-call | flops 402653184 | bytes 3276800 | tf_op jit(solution)/shard_map/pallas_call | solution.py:103
  28.0 0.0 collective-permute-done
  28.0 0.0 copy-done
  28.0 0.9 %fusion.2 = f32[32,32]{1,0:T(8,128)S(1)} fusion(f32[32,32]{1,0:T(8,128)} %shard_map.38, bf16[3,32,1024]{2,1,0:T(8,128)(2,1)S(1)} %copy-done, f32[1024]{0:T(1024)S(1)} %convert_element_type.40), kind=kOutput, calls=%fused_computation.6 | convolution fusion | flops 6587392 | bytes 208896 | tf_op jit(solution)/shard_map/ckj,clj->kl/dot_general | solution.py:121
  28.9 0.0 collective-permute-done.1
  28.9 1.1 %fusion.1 = f32[32,32]{1,0:T(8,128)S(1)} fusion(bf16[3,32,1024]{2,1,0:T(8,128)(2,1)S(1)} %collective-permute-done.1, bf16[3,16,32,1024]{3,2,1,0:T(8,128)(2,1)} %get-tuple-element.17.live_ref, f32[1024]{0:T(1024)S(1)} %convert_element_type.43), kind=kOutput, calls=%fused_computation.4 | convolution fusion | flops 6587392 | bytes 401408 | tf_op jit(solution)/shard_map/ckj,clj->kl/dot_general | solution.py:121
  30.0 0.0 collective-permute-done.2
  30.0 0.2 convolution_bitcast_fusion
  30.3 0.0 copy-done.1
  30.3 0.3 fusion
  30.6 0.1 maximum_multiply_fusion
  30.7 19.9 %all_to_all.5 = f32[1,16,32,128]{3,2,0,1:T(8,128)S(1)} all-to-all(f32[1,16,32,128]{3,2,0,1:T(8,128)S(1)} %broadcast_in_dim.2), channel_id=1, replica_groups=mesh['sub'=32,'grp'=16] {'grp'}, dimensions={1} | all-to-all | bytes 524288 | tf_op jit(solution)/shard_map/all_to_all | solution.py:146
  50.6 0.1 slice.25
  50.7 0.1 slice.26
  50.9 0.8 %maximum_bitcast_fusion = f32[1,16,32,96]{3,2,1,0:T(8,128)} fusion(f32[1,16,32,64]{3,2,0,1:T(8,128)S(1)} %slice.26, f32[1,16,32,32]{3,2,0,1:T(8,128)S(1)} %slice_add_fusion), kind=kLoop, calls=%fused_computation.15 | loop fusion | flops 49152 | bytes 393216 | tf_op jit(solution)/shard_map/concatenate | solution.py:148
  (6 shorter events, 0.1 us)
Async XLA Ops:
  7.2 20.8 %copy-start = (bf16[3,32,1024]{2,1,0:T(8,128)(2,1)S(1)}, bf16[3,32,1024]{2,1,0:T(8,128)(2,1)}, u32[]{:S(2)}) copy-start(bf16[3,32,1024]{2,1,0:T(8,128)(2,1)} %get-tuple-element.18) | copy-start | bytes 589828
  7.2 23.1 %copy-start.1 = (bf16[3,16,32,128]{3,2,1,0:T(8,128)(2,1)S(1)}, bf16[3,16,32,128]{3,2,1,0:T(8,128)(2,1)}, u32[]{:S(2)}) copy-start(bf16[3,16,32,128]{3,2,1,0:T(8,128)(2,1)} %get-tuple-element.21) | copy-start | bytes 1179652
  7.2 20.7 %collective-permute-start = (bf16[1024]{0:T(1024)(128)(2,1)S(1)}, bf16[1024]{0:T(1024)(128)(2,1)S(1)}, u32[]{:S(2)}, u32[]{:S(2)}) collective-permute-start(bf16[1024]{0:T(1024)(128)(2,1)S(1)} %slice_bitcast_fusion), channel_id=1, source_target_pairs={{0,16},{16,32},{32,48},{48,64},{64,80},{80,96},{96,112},{112,128},... | collective-permute-start | bytes 6152 | tf_op jit(solution)/shard_map/ppermute | solution.py:12
  9.3 19.6 %collective-permute-start.1 = (bf16[3,32,1024]{2,1,0:T(8,128)(2,1)}, bf16[3,32,1024]{2,1,0:T(8,128)(2,1)S(1)}, u32[]{:S(2)}, u32[]{:S(2)}) collective-permute-start(bf16[3,32,1024]{2,1,0:T(8,128)(2,1)} %get-tuple-element.18), channel_id=1, source_target_pairs={{16,0},{32,16},{48,32},{64,48},{80,64},{96,80},{112,96},{128,112},... | collective-permute-start | bytes 589832 | tf_op jit(solution)/shard_map/ppermute | solution.py:12
  19.6 10.4 %collective-permute-start.2 = (bf16[3,16,32,128]{3,2,1,0:T(8,128)(2,1)}, bf16[3,16,32,128]{3,2,1,0:T(8,128)(2,1)S(1)}, u32[]{:S(2)}, u32[]{:S(2)}) collective-permute-start(bf16[3,16,32,128]{3,2,1,0:T(8,128)(2,1)} %get-tuple-element.22), channel_id=1, source_target_pairs={{1,0},{2,1},{3,2},{4,3},{5,4},{6,5},{7,6},{8,7},{9,8},{10,9},{11,1... | collective-permute-start | bytes 1179656 | tf_op jit(solution)/shard_map/ppermute | solution.py:12
